TPU v7x, 32 devices: a whole 2x2x4 slice. The times are simulated.
32 devices in a mesh: groups: 2 (over y), ctx: 4 (over x, core), tp: 4 (over z).
Axes of the slice: x: 2, y: 2, z: 4, core: 2. Of those that a mesh axis runs over, the one named last changes fastest.
Arguments:
- question_hidden: bfloat16 [256, 8192], P(('groups', 'ctx')), parts along dimension 0, may hold values from -1800 to 1800
- recomp_hidden: bfloat16 [512, 8192], P(('groups', 'ctx')), parts along dimension 0, may hold values from -1800 to 1800
- norm_gain: bfloat16 [8192], replicated, may hold values from 0.099609375 to 1.8984375
- w_query: bfloat16 [8192, 8192], P('ctx', 'tp'), may hold values from -0.0625 to 0.0625
- w_keyval: bfloat16 [8192, 2, 1024], P('ctx', None, 'tp'), may hold values from -0.25 to 0.25
- pool_codes: bfloat16 [384, 2, 64, 1024], P(('groups', 'ctx'), None, None, 'tp'), parts along dimension 0, may hold values from -127 to 127
- pool_scales: bfloat16 [384, 2, 8], P(('groups', 'ctx'), None, 'tp'), parts along dimension 0, may hold values from 0.025 to 2
- block_owner: int32 [256, 1], P('groups'), parts along dimension 0, may hold values from 0 to 3; in each aligned block of 32 rows (0 to 31, 32 to 63, ...) at most 16 rows name the same one
- block_slot: int32 [256], P('groups'), parts along dimension 0, may hold values from 0 to 47
- recomp_pos: int32 [512], P('groups'), parts along dimension 0, may hold values from 0 to 8191, as said below
Outputs:
- attended: bfloat16 [256, 8192], P(('groups', 'ctx'), 'tp'), parts along dimension 0
- kv_cache: bfloat16 [2, 16384, 1024], P(None, ('groups', 'ctx'), 'tp'), parts along dimension 1
There are 2 independent parts, one for each index of `groups`. A program takes and returns all parts, laid end to end along the dimension named above; an argument that names none is the same for every part. Nothing has to cross between parts.
Inputs may be any that keep to these rules, and one draw needn't show every extreme that they name: Among the 32 context blocks of each index of ctx (rows of block_owner in aligned blocks), at most 16 name the same pool shard. `recomp_pos`: 256 distinct positions in no particular order; the first and the last context position are always listed.
All inputs are finite; a program needn't handle non-finite values.
Results may differ from a plain program's by a relative error of at most 0.018.
The roundings to bfloat16 on the way count: a program that leaves them out, or rounds other values in their place, can miss the bound.
Values may be sent and summed in bfloat16 or wider, within the bound.
No kernel may reach another device: no remote copies, remote signals or barrier semaphores. Data moves between devices by JAX's collectives and lax.ppermute only.
A program may use at most 128 MiB of HBM per device.

v0:
```python
import jax
import jax.numpy as jnp
from jax import lax
from jax.sharding import PartitionSpec as P

HD = 128


norm_eps = 1e-05
neg_large = -1e30


def rms_rows(hidden, norm_gain):
    floats = hidden.astype(jnp.float32)
    factor = lax.rsqrt(jnp.mean(floats * floats, axis=-1, keepdims=True) + norm_eps)
    return (floats * factor * norm_gain.astype(jnp.float32)).astype(jnp.bfloat16)


def attend_block(running, queries, key_rows, val_rows, visible, score_scale):
    row_max, row_total, weighted = running
    scores = (
        jnp.einsum("thgd,nhd->htgn", queries, key_rows, preferred_element_type=jnp.float32)
        * score_scale
    )
    shown = visible[None, :, None, :]
    masked = jnp.where(shown, scores, neg_large)
    new_max = jnp.maximum(row_max, jnp.max(masked, axis=-1))
    weights = jnp.where(shown, jnp.exp(masked - new_max[..., None]), 0.0)
    row_total = jnp.sum(weights, axis=-1)
    weighted = jnp.einsum(
        "htgn,nhd->htgd", weights.astype(jnp.bfloat16), val_rows, preferred_element_type=jnp.float32
    )
    return (new_max, row_total, weighted)


def fold_keys(running, queries, token_index, key_rows, val_rows, key_rank, score_scale):
    visible = key_rank[None, :] <= token_index[:, None]
    return attend_block(running, queries, key_rows, val_rows, visible, score_scale)


def empty_state(kv_heads, token_count, group_size):
    return (
        jnp.full((kv_heads, token_count, group_size), neg_large, jnp.float32),
        jnp.zeros((kv_heads, token_count, group_size), jnp.float32),
        jnp.zeros((kv_heads, token_count, group_size, HD), jnp.float32),
    )


def body(
    question_hidden,
    recomp_hidden,
    norm_gain,
    w_query,
    w_keyval,
    pool_codes,
    pool_scales,
    block_owner,
    block_slot,
    recomp_pos,
):
    shards = lax.axis_size("ctx")
    own_index = lax.axis_index("ctx")
    q_rows = question_hidden.shape[0]
    r_rows = recomp_hidden.shape[0]
    row_count = q_rows + r_rows
    kv_width = w_keyval.shape[2]
    kv_heads = kv_width // HD
    q_width = w_query.shape[1]
    group_size = q_width // kv_width
    score_scale = HD ** (-0.5)
    normed = jnp.concatenate(
        [rms_rows(question_hidden, norm_gain), rms_rows(recomp_hidden, norm_gain)], axis=0
    )
    pieces = lax.all_to_all(normed, "ctx", split_axis=1, concat_axis=0, tiled=True)
    arranged = pieces.reshape(shards, row_count, pieces.shape[1])
    question_part = arranged[:, :q_rows, :].reshape(shards * q_rows, pieces.shape[1])
    block_rows = question_part
    query = lax.psum_scatter(
        jnp.dot(block_rows, w_query, preferred_element_type=jnp.float32),
        "ctx",
        scatter_dimension=0,
        tiled=True,
    ).astype(jnp.bfloat16)
    kv_weight = w_keyval.reshape(w_keyval.shape[0], 2 * kv_width)
    block_rows = pieces
    projected = (
        lax.psum_scatter(
            jnp.dot(block_rows, kv_weight, preferred_element_type=jnp.float32),
            "ctx",
            scatter_dimension=0,
            tiled=True,
        )
        .astype(jnp.bfloat16)
        .reshape(row_count, 2, kv_width)
    )
    question_kv = projected[:q_rows]
    recomp_kv = projected[q_rows:]
    owners = block_owner[:, 0].reshape(shards, -1)
    per_dev = owners.shape[1]
    slot_table = block_slot.reshape(shards, per_dev)
    capacity = max(2, 2 * per_dev // shards)
    positions = jnp.arange(per_dev)
    earlier_mask = positions[None, :] < positions[:, None]
    same_owner = owners[:, :, None] == owners[:, None, :]
    order_rank = jnp.sum((same_owner & earlier_mask[None]).astype(jnp.int32), axis=2)
    slot_ids = jnp.arange(capacity)
    chosen = (owners == own_index)[:, :, None] & (order_rank[:, :, None] == slot_ids[None, None, :])
    send_slot = jnp.sum(jnp.where(chosen, slot_table[:, :, None], 0), axis=1).reshape(-1)
    send_codes = jnp.take(pool_codes, send_slot, axis=0).reshape(
        (shards, capacity) + pool_codes.shape[1:]
    )
    send_scales = jnp.take(pool_scales, send_slot, axis=0).reshape(
        (shards, capacity) + pool_scales.shape[1:]
    )
    got_codes, got_scales = (
        lax.all_to_all(send_codes, "ctx", split_axis=0, concat_axis=0, tiled=True),
        lax.all_to_all(send_scales, "ctx", split_axis=0, concat_axis=0, tiled=True),
    )
    own_owner = lax.dynamic_index_in_dim(owners, own_index, 0, keepdims=False)
    own_rank = lax.dynamic_index_in_dim(order_rank, own_index, 0, keepdims=False)
    flat_index = own_owner * capacity + own_rank
    block_codes = jnp.take(
        got_codes.reshape((shards * capacity,) + pool_codes.shape[1:]), flat_index, axis=0
    )
    block_scales = jnp.take(
        got_scales.reshape((shards * capacity,) + pool_scales.shape[1:]), flat_index, axis=0
    )
    block_len = block_codes.shape[2]
    dequant = (
        block_codes.astype(jnp.float32).reshape(per_dev, 2, block_len, kv_heads, HD)
        * block_scales.astype(jnp.float32)[:, :, None, :, None]
    )
    ctx_dev = per_dev * block_len
    cached = jnp.transpose(
        dequant.astype(jnp.bfloat16).reshape(per_dev, 2, block_len, kv_width), (1, 0, 2, 3)
    ).reshape(2, ctx_dev, kv_width)
    all_recomp = lax.all_gather(recomp_kv, "ctx", axis=0, tiled=True)
    local_pos = recomp_pos - own_index * ctx_dev
    target = jnp.where((local_pos >= 0) & (local_pos < ctx_dev), local_pos, ctx_dev)
    kv_cache = cached.at[:, target, :].set(jnp.transpose(all_recomp, (1, 0, 2)), mode="drop")
    key_local = jnp.concatenate([kv_cache[0], question_kv[:, 0]], axis=0)
    val_local = jnp.concatenate([kv_cache[1], question_kv[:, 1]], axis=0)
    key_span = ctx_dev + q_rows
    every_query = lax.all_gather(query, "ctx", axis=0, tiled=True)
    total_tokens = every_query.shape[0]
    per_step = q_rows
    while (
        per_step * 2 <= total_tokens
        and total_tokens % (per_step * 2) == 0
        and (per_step * group_size < 512)
    ):
        per_step = per_step * 2
    block_count = total_tokens // per_step
    query_blocks = every_query.reshape(block_count, per_step, kv_heads, group_size, HD)
    key_offset = jnp.arange(key_span)
    local_rank = jnp.where(key_offset < ctx_dev, -1, own_index * q_rows + key_offset - ctx_dev)
    key_three = key_local.reshape(key_span, kv_heads, HD)
    val_three = val_local.reshape(key_span, kv_heads, HD)

    def one_block(packed):
        block_queries, first_token = packed
        token_index = first_token + jnp.arange(per_step)
        return fold_keys(
            empty_state(kv_heads, per_step, group_size),
            block_queries,
            token_index,
            key_three,
            val_three,
            local_rank,
            score_scale,
        )

    part_max, part_total, part_sums = lax.map(
        one_block, (query_blocks, jnp.arange(block_count) * per_step)
    )

    def by_token(value, trailing):
        return jnp.moveaxis(value, 1, 2).reshape(shards, q_rows, trailing)

    sent = (
        by_token(part_sums, q_width),
        by_token(part_max, kv_heads * group_size),
        by_token(part_total, kv_heads * group_size),
    )
    got_sums, got_max, got_total = (
        lax.all_to_all(sent[0], "ctx", split_axis=0, concat_axis=0, tiled=True),
        lax.all_to_all(sent[1], "ctx", split_axis=0, concat_axis=0, tiled=True),
        lax.all_to_all(sent[2], "ctx", split_axis=0, concat_axis=0, tiled=True),
    )
    best_max = jnp.max(got_max, axis=0)
    factor = jnp.exp(got_max - best_max[None])
    row_total = jnp.sum(got_total * factor, axis=0)
    weighted = jnp.sum(
        got_sums.reshape(shards, q_rows, kv_heads * group_size, HD) * factor[..., None], axis=0
    )
    attended = (weighted / row_total[..., None]).reshape(q_rows, q_width).astype(jnp.bfloat16)
    return (attended, kv_cache)


def solution(mesh):
    placed = (
        P(("groups", "ctx"), None),
        P(("groups", "ctx"), None),
        P(),
        P("ctx", "tp"),
        P("ctx", None, "tp"),
        P(("groups", "ctx"), None, None, "tp"),
        P(("groups", "ctx"), None, "tp"),
        P("groups", None),
        P("groups"),
        P("groups"),
    )
    return jax.shard_map(
        body,
        mesh=mesh,
        in_specs=placed,
        out_specs=(P(("groups", "ctx"), "tp"), P(None, ("groups", "ctx"), "tp")),
        check_vma=False,
    )
```

profile of v0, /device:TPU:0, one launch (start us, length us, event | category | flops | bytes accessed | tf_op | source)
XLA Modules:
  0.0 228.8 jit_solution(15619929386132747075)
XLA Ops:
  12.7 4.2 %all-to-all-start.2 = ((bf16[4,16,2,2]{1,3,2,0:T(2,128)(2,1)}), bf16[4,16,2,2]{1,3,2,0:T(2,128)(2,1)S(1)}, u32[]{:S(2)}, u32[]{:S(2)}) async-start(bf16[4,16,2,2]{1,3,2,0:T(2,128)(2,1)} %broadcast_select_fusion.2), calls=%async_computation.3 | async-start | bytes 8192 | tf_op jit(solution)/shard_map/all_to_all | solution.py:117
  22.5 4.4 %all-to-all-start = ((bf16[96,4,2048]{2,0,1:T(8,128)(2,1)}), bf16[96,4,2048]{2,0,1:T(8,128)(2,1)}, u32[]{:S(2)}, u32[]{:S(2)}) async-start(bf16[96,4,2048]{2,0,1:T(8,128)(2,1)} %bitcast.108), calls=%async_computation | async-start | bytes 3145728 | tf_op jit(solution)/shard_map/all_to_all | solution.py:74
  29.7 4.6 %broadcast_select_fusion = bf16[4,16,2,64,256]{4,3,2,1,0:T(8,128)(2,1)} fusion(bf16[4,16,2,64,256]{4,3,2,1,0:T(8,128)(2,1)} %bitcast.105, pred[4,16]{1,0:T(4,128)(4,1)S(1)} %compare_and_fusion), kind=kLoop, calls=%fused_computation.32 | loop fusion | flops 2097152 | bytes 8388672 | tf_op jit(solution)/shard_map/jit(_take)/select_n | solution.py:109
  34.2 12.8 %all-to-all-done = bf16[96,4,2048]{2,0,1:T(8,128)(2,1)} async-done(((bf16[96,4,2048]{2,0,1:T(8,128)(2,1)}), bf16[96,4,2048]{2,0,1:T(8,128)(2,1)}, u32[]{:S(2)}, u32[]{:S(2)}) %all-to-all-start) | async-done | bytes 1572896 | tf_op jit(solution)/shard_map/all_to_all | solution.py:74
  47.0 4.8 %all-to-all-start.1 = ((bf16[4,16,2,64,256]{4,3,2,1,0:T(8,128)(2,1)}), bf16[4,16,2,64,256]{4,3,2,1,0:T(8,128)(2,1)}, u32[]{:S(2)}, u32[]{:S(2)}) async-start(bf16[4,16,2,64,256]{4,3,2,1,0:T(8,128)(2,1)} %broadcast_select_fusion), calls=%async_computation.2 | async-start | bytes 8388608 | tf_op jit(solution)/shard_map/all_to_all | solution.py:116
  52.4 3.3 %fusion.35 = f32[384,512]{1,0:T(8,128)} fusion(bf16[384,2048]{1,0:T(8,128)(2,1)} %bitcast.13, bf16[2048,512]{1,0:T(8,128)(2,1)S(1)} %bitcast.115), kind=kOutput, calls=%fused_computation.83 | convolution fusion | flops 805306368 | bytes 4456448 | tf_op jit(solution)/shard_map/dot_general | solution.py:88
  59.1 5.7 %fusion.34 = f32[128,2048]{1,0:T(8,128)} fusion(bf16[128,2048]{1,0:T(8,128)(2,1)S(1)} %bitcast.112, bf16[2048,2048]{1,0:T(8,128)(2,1)} %param.15), kind=kOutput, calls=%fused_computation.82 | convolution fusion | flops 1073741824 | bytes 9961472 | tf_op jit(solution)/shard_map/dot_general | solution.py:79
  64.9 20.7 %reduce-scatter.5.cloned.1.call-done = f32[96,512]{1,0:T(8,128)} async-done(((f32[384,512]{1,0:T(8,128)}), f32[96,512]{1,0:T(8,128)}) %reduce-scatter.5.cloned.1.call-update) | async-done | bytes 196624 | tf_op jit(solution)/shard_map/reduce_scatter | solution.py:87
  86.9 19.5 %all_gather.7 = bf16[256,2,256]{2,1,0:T(2,128)(2,1)S(1)} all-gather(bf16[64,2,256]{2,1,0:T(2,128)(2,1)S(1)} %slice.29), channel_id=1, replica_groups=mesh['groups'=2,'ctx'=4,'tp'=4] {'ctx'}, dimensions={0}, use_global_device_ids=true | all-gather | bytes 327680 | tf_op jit(solution)/shard_map/all_gather | solution.py:137
  110.5 12.8 %copy.83 = bf16[2,2048,256]{2,0,1:T(2,128)(2,1)S(1)} copy(bf16[2,2048,256]{2,1,0:T(8,128)(2,1)S(1)} %bitcast.106) | data formatting | bytes 4194304 | tf_op jit(solution)/shard_map/reshape | solution.py:136
  123.4 7.5 %scatter_fusion = bf16[2,2048,256]{2,0,1:T(2,128)(2,1)S(1)} fusion(bf16[2,2048,256]{2,0,1:T(2,128)(2,1)S(1)} %copy.83, s32[256]{0:T(256)S(1)} %copy-done.10, bf16[256,2,256]{2,1,0:T(2,128)(2,1)S(1)} %all_gather.7), kind=kCustom, calls=%fused_computation.4 | custom fusion | bytes 787456 | tf_op jit(solution)/shard_map/scatter | solution.py:140
  130.8 4.2 %fusion.32 = (bf16[1,2048,256]{2,0,1:T(2,128)(2,1)}, bf16[1,2048,256]{2,0,1:T(2,128)(2,1)}) fusion(bf16[2,2048,256]{2,0,1:T(2,128)(2,1)S(1)} %scatter_fusion), kind=kLoop, calls=%fused_computation.77 | loop fusion | bytes 4194304 | tf_op jit(solution)/shard_map/slice | solution.py:142
  135.0 4.6 %copy.84 = bf16[1,2048,256]{1,2,0:T(8,128)(2,1)S(1)} copy(bf16[1,2048,256]{2,0,1:T(2,128)(2,1)} %get-tuple-element.157) | data formatting | bytes 2097152 | tf_op jit(solution)/shard_map/slice | solution.py:141
  142.3 5.9 %copy.87 = bf16[1,2048,256]{1,2,0:T(8,128)(2,1)} copy(bf16[1,2048,256]{2,0,1:T(2,128)(2,1)} %get-tuple-element.156) | data formatting | bytes 2097152 | tf_op jit(solution)/shard_map/slice | solution.py:142
  153.8 7.5 %all_gather.6 = bf16[128,2048]{1,0:T(8,128)(2,1)S(1)} all-gather(bf16[32,2048]{1,0:T(8,128)(2,1)S(1)} %convert_element_type.57), channel_id=1, replica_groups=mesh['groups'=2,'ctx'=4,'tp'=4] {'ctx'}, dimensions={0}, use_global_device_ids=true | all-gather | bytes 655360 | tf_op jit(solution)/shard_map/all_gather | solution.py:144
  162.2 23.5 %while.15 = (s32[]{:T(128)}, f32[2,2,64,8]{3,2,1,0:T(8,128)S(1)}, f32[2,2,64,8]{3,2,1,0:T(8,128)S(1)}, f32[2,2,64,8,128]{4,3,2,1,0:T(8,128)}, s32[2]{0:T(128)S(1...) while((s32[]{:T(128)}, f32[2,2,64,8]{3,2,1,0:T(8,128)S(1)}, ...), condition=%wide.region_10.11_spmd.clone, body=%wide.region_7.10_spmd.clone.sunk | while | flops 1118349568 | bytes 42421216 | solution.py:173
  163.6 3.4 %fusion.47 = (f32[2,64,8]{2,1,0:T(8,128)S(1)}, f32[2,64,8,2080]{3,2,1,0:T(8,128)S(1)}) fusion(pred[64,2080]{1,0:T(8,128)(4,1)S(1)} %broadcast_compare_fusion.3, bf16[2080,2,128]{2,0,1:T(8,128)(2,1)S(1)} %get-tuple-element.249, bf16[2,64,2,8,128]{4,3,2,1,0:T(8,128)(2,1)} %get-tuple-element.248, s32[]{:T(128)S(6)} %copy.137), kind=kOutput, calls=%fused_computation.8.clone.1 | convolution fusion | flops 551648256 | bytes 9984004 | tf_op jit(solution)/shard_map/while/body/eval_jaxpr/thgd,nhd->htgn/dot_general | solution.py:22
  167.1 3.2 %fusion.48 = f32[2,64,8]{2,1,0:T(8,128)S(1)} fusion(f32[2,64,8,2080]{3,2,1,0:T(8,128)S(1)} %get-tuple-element.219, f32[2,64,8]{2,1,0:T(8,128)S(1)} %broadcast_maximum_fusion.2, pred[64,2080]{1,0:T(8,128)(4,1)S(1)} %broadcast_compare_fusion.3), kind=kLoop, calls=%fused_computation.10.clone.1 | loop fusion | flops 10648576 | bytes 8660992 | tf_op jit(solution)/shard_map/while/body/eval_jaxpr/reduce_sum | solution.py:29
  175.3 3.4 %fusion.47 = (f32[2,64,8]{2,1,0:T(8,128)S(1)}, f32[2,64,8,2080]{3,2,1,0:T(8,128)S(1)}) fusion(pred[64,2080]{1,0:T(8,128)(4,1)S(1)} %broadcast_compare_fusion.3, bf16[2080,2,128]{2,0,1:T(8,128)(2,1)S(1)} %get-tuple-element.249, bf16[2,64,2,8,128]{4,3,2,1,0:T(8,128)(2,1)} %get-tuple-element.248, s32[]{:T(128)S(6)} %copy.137), kind=kOutput, calls=%fused_computation.8.clone.1 | convolution fusion | flops 551648256 | bytes 9984004 | tf_op jit(solution)/shard_map/while/body/eval_jaxpr/thgd,nhd->htgn/dot_general | solution.py:22
  178.8 3.2 %fusion.48 = f32[2,64,8]{2,1,0:T(8,128)S(1)} fusion(f32[2,64,8,2080]{3,2,1,0:T(8,128)S(1)} %get-tuple-element.219, f32[2,64,8]{2,1,0:T(8,128)S(1)} %broadcast_maximum_fusion.2, pred[64,2080]{1,0:T(8,128)(4,1)S(1)} %broadcast_compare_fusion.3), kind=kLoop, calls=%fused_computation.10.clone.1 | loop fusion | flops 10648576 | bytes 8660992 | tf_op jit(solution)/shard_map/while/body/eval_jaxpr/reduce_sum | solution.py:29
  186.6 3.2 %all-to-all-start.4 = ((f32[4,1,512]{2,1,0:T(1,128)}), f32[4,1,512]{2,1,0:T(1,128)S(1)}, u32[]{:S(2)}, u32[]{:S(2)}) async-start(f32[4,1,512]{2,1,0:T(1,128)} %reshape.295), calls=%async_computation.6 | async-start | bytes 16384 | tf_op jit(solution)/shard_map/all_to_all | solution.py:187
  193.6 3.2 %all-to-all-start.5 = ((f32[4,1,512]{2,1,0:T(1,128)}), f32[4,1,512]{2,1,0:T(1,128)S(1)}, u32[]{:S(2)}, u32[]{:S(2)}) async-start(f32[4,1,512]{2,1,0:T(1,128)} %reshape.297), calls=%async_computation.7 | async-start | bytes 16384 | tf_op jit(solution)/shard_map/all_to_all | solution.py:188
  200.7 4.2 %all-to-all-start.3 = ((f32[4,32,2048]{2,1,0:T(8,128)}), f32[4,32,2048]{2,1,0:T(8,128)}, u32[]{:S(2)}, u32[]{:S(2)}) async-start(f32[4,32,2048]{2,1,0:T(8,128)} %reshape.240), calls=%async_computation.5 | async-start | bytes 2097152 | tf_op jit(solution)/shard_map/all_to_all | solution.py:186
  212.4 7.0 %all-to-all-done.3 = f32[4,32,2048]{2,1,0:T(8,128)} async-done(((f32[4,32,2048]{2,1,0:T(8,128)}), f32[4,32,2048]{2,1,0:T(8,128)}, u32[]{:S(2)}, u32[]{:S(2)}) %all-to-all-start.3) | async-done | bytes 1048608 | tf_op jit(solution)/shard_map/all_to_all | solution.py:186
  (138 shorter events, 60.8 us)
Async XLA Ops:
  7.2 19.7 %copy-start = (bf16[48,2,64,256]{3,2,1,0:T(8,128)(2,1)S(1)}, bf16[48,2,64,256]{3,2,1,0:T(8,128)(2,1)}, u32[]{:S(2)}) copy-start(bf16[48,2,64,256]{3,2,1,0:T(8,128)(2,1)} %param.17) | copy-start | bytes 9437188
  12.7 9.8 %all-to-all-start.2 = ((bf16[4,16,2,2]{1,3,2,0:T(2,128)(2,1)}), bf16[4,16,2,2]{1,3,2,0:T(2,128)(2,1)S(1)}, u32[]{:S(2)}, u32[]{:S(2)}) async-start(bf16[4,16,2,2]{1,3,2,0:T(2,128)(2,1)} %broadcast_select_fusion.2), calls=%async_computation.3 | async-start | bytes 8192 | tf_op jit(solution)/shard_map/all_to_all | solution.py:117
  16.9 3.7 %copy-start.2 = (bf16[64,8192]{1,0:T(8,128)(2,1)S(1)}, bf16[64,8192]{1,0:T(8,128)(2,1)}, u32[]{:S(2)}) copy-start(bf16[64,8192]{1,0:T(8,128)(2,1)} %param.13) | copy-start | bytes 3145732
  16.9 4.0 %copy-start.4 = (bf16[32,8192]{1,0:T(8,128)(2,1)S(1)}, bf16[32,8192]{1,0:T(8,128)(2,1)}, u32[]{:S(2)}) copy-start(bf16[32,8192]{1,0:T(8,128)(2,1)} %param.12) | copy-start | bytes 1572868
  22.5 24.5 %all-to-all-start = ((bf16[96,4,2048]{2,0,1:T(8,128)(2,1)}), bf16[96,4,2048]{2,0,1:T(8,128)(2,1)}, u32[]{:S(2)}, u32[]{:S(2)}) async-start(bf16[96,4,2048]{2,0,1:T(8,128)(2,1)} %bitcast.108), calls=%async_computation | async-start | bytes 3145728 | tf_op jit(solution)/shard_map/all_to_all | solution.py:74
  34.2 17.7 %copy-start.3 = (bf16[2048,2,256]{2,1,0:T(2,128)(2,1)S(1)}, bf16[2048,2,256]{2,1,0:T(2,128)(2,1)}, u32[]{:S(2)}) copy-start(bf16[2048,2,256]{2,1,0:T(2,128)(2,1)} %param.16) | copy-start | bytes 6291460
  47.0 59.4 %all-to-all-start.1 = ((bf16[4,16,2,64,256]{4,3,2,1,0:T(8,128)(2,1)}), bf16[4,16,2,64,256]{4,3,2,1,0:T(8,128)(2,1)}, u32[]{:S(2)}, u32[]{:S(2)}) async-start(bf16[4,16,2,64,256]{4,3,2,1,0:T(8,128)(2,1)} %broadcast_select_fusion), calls=%async_computation.2 | async-start | bytes 8388608 | tf_op jit(solution)/shard_map/all_to_all | solution.py:116
  51.8 33.7 %reduce-scatter.5.cloned.1.call-start = ((), (), s32[]{:S(2)}) async-start(), calls=%async_computation.9 | async-start | bytes 983040 | tf_op jit(solution)/shard_map/reduce_scatter | solution.py:87
  52.3 4.0 %copy-start.11 = (s32[256]{0:T(256)S(1)}, s32[256]{0:T(256)}, u32[]{:S(2)}) copy-start(s32[256]{0:T(256)} %param.21) | copy-start | bytes 3076
  55.6 97.2 %reduce-scatter.3.cloned.1.call-start = ((), (), s32[]{:S(2)}) async-start(), calls=%async_computation.8 | async-start | bytes 1310720 | tf_op jit(solution)/shard_map/reduce_scatter | solution.py:78
  110.5 12.8 %copy-start.10 = (s32[256]{0:T(256)S(1)}, s32[256]{0:T(256)}, u32[]{:S(2)}) copy-start(s32[256]{0:T(256)} %compare_select_fusion.1) | copy-start | bytes 3076
  150.5 11.7 %copy-start.8 = (f32[2,2,64,8]{3,2,1,0:T(8,128)S(1)}, f32[2,2,64,8]{3,2,1,0:T(8,128)}, u32[]{:S(2)}) copy-start(f32[2,2,64,8]{3,2,1,0:T(8,128)} %custom-call.8) | copy-start | bytes 24580
  150.5 11.7 %copy-start.9 = (f32[2,2,64,8]{3,2,1,0:T(8,128)S(1)}, f32[2,2,64,8]{3,2,1,0:T(8,128)}, u32[]{:S(2)}) copy-start(f32[2,2,64,8]{3,2,1,0:T(8,128)} %custom-call.9) | copy-start | bytes 24580
  150.5 11.7 %copy-start.12 = (s32[2]{0:T(128)S(1)}, s32[2]{0:T(128)}, u32[]{:S(2)}) copy-start(s32[2]{0:T(128)} %iota_multiply_fusion) | copy-start | bytes 28
  167.1 3.3 %copy-start.5 = (bf16[2080,2,128]{2,0,1:T(8,128)(2,1)S(1)}, bf16[2080,2,128]{2,0,1:T(8,128)(2,1)}, u32[]{:S(2)}) copy-start(bf16[2080,2,128]{2,0,1:T(8,128)(2,1)} %get-tuple-element.250) | copy-start | bytes 3194884 | tf_op jit(solution)/shard_map/while
  167.1 3.3 %copy-start.6 = (f32[2,2,64,8,128]{4,3,2,1,0:T(8,128)S(1)}, f32[2,2,64,8,128]{4,3,2,1,0:T(8,128)}, u32[]{:S(2)}) copy-start(f32[2,2,64,8,128]{4,3,2,1,0:T(8,128)} %get-tuple-element.236) | copy-start | bytes 3145732 | tf_op jit(solution)/shard_map/while
  172.9 1.0 copy-start.7
  178.8 3.3 %copy-start.5 = (bf16[2080,2,128]{2,0,1:T(8,128)(2,1)S(1)}, bf16[2080,2,128]{2,0,1:T(8,128)(2,1)}, u32[]{:S(2)}) copy-start(bf16[2080,2,128]{2,0,1:T(8,128)(2,1)} %get-tuple-element.250) | copy-start | bytes 3194884 | tf_op jit(solution)/shard_map/while
  178.8 3.3 %copy-start.6 = (f32[2,2,64,8,128]{4,3,2,1,0:T(8,128)S(1)}, f32[2,2,64,8,128]{4,3,2,1,0:T(8,128)}, u32[]{:S(2)}) copy-start(f32[2,2,64,8,128]{4,3,2,1,0:T(8,128)} %get-tuple-element.236) | copy-start | bytes 3145732 | tf_op jit(solution)/shard_map/while
  184.7 1.0 copy-start.7
  186.6 7.0 %all-to-all-start.4 = ((f32[4,1,512]{2,1,0:T(1,128)}), f32[4,1,512]{2,1,0:T(1,128)S(1)}, u32[]{:S(2)}, u32[]{:S(2)}) async-start(f32[4,1,512]{2,1,0:T(1,128)} %reshape.295), calls=%async_computation.6 | async-start | bytes 16384 | tf_op jit(solution)/shard_map/all_to_all | solution.py:187
  193.6 7.0 %all-to-all-start.5 = ((f32[4,1,512]{2,1,0:T(1,128)}), f32[4,1,512]{2,1,0:T(1,128)S(1)}, u32[]{:S(2)}, u32[]{:S(2)}) async-start(f32[4,1,512]{2,1,0:T(1,128)} %reshape.297), calls=%async_computation.7 | async-start | bytes 16384 | tf_op jit(solution)/shard_map/all_to_all | solution.py:188
  200.7 18.7 %all-to-all-start.3 = ((f32[4,32,2048]{2,1,0:T(8,128)}), f32[4,32,2048]{2,1,0:T(8,128)}, u32[]{:S(2)}, u32[]{:S(2)}) async-start(f32[4,32,2048]{2,1,0:T(8,128)} %reshape.240), calls=%async_computation.5 | async-start | bytes 2097152 | tf_op jit(solution)/shard_map/all_to_all | solution.py:186
  208.6 13.3 %copy-start.1 = (bf16[48,2,64,256]{3,2,1,0:T(8,128)(2,1)S(1)}, bf16[48,2,64,256]{3,2,1,0:T(8,128)(2,1)}, u32[]{:S(2)}) copy-start(bf16[48,2,64,256]{3,2,1,0:T(8,128)(2,1)} %param.17) | copy-start | bytes 9437188
Sparse Core Ops, SparseCore 0:
  55.8 29.7 reduce-scatter.4
  88.1 24.7 reduce-scatter.2
where the time goes:
time: 230 us; the launch traced here: 229 us
  local copies, waits for them, and re-layouts  66.5 us (29%)
  waiting for transfers between devices  44.6 us (19%)
  other arithmetic  30.7 us (13%)
  blocking collectives  27 us (12%)
  starting transfers between devices  24.3 us (11%)
  matrix products  21 us (9%)
  between operations  14.5 us (6%)
    reduce_scatter x1, waiting for transfers between devices, body(): lax.psum_scatter(jnp.dot(block_rows, kv_weight, preferred_element_type=jn...  20.7 us
    all_gather x1, blocking collectives, body(): all_recomp = lax.all_gather(recomp_kv, 'ctx', axis=0, tiled=True)  19.5 us
    reshape x1, local copies, waits for them, and re-layouts, body(): cached = jnp.transpose(dequant.astype(jnp.bfloat16).reshape(per_dev, 2, b...  12.8 us
    all_to_all x1, waiting for transfers between devices, body(): lax.all_to_all(normed, 'ctx', split_axis=1, concat_axis=0, tiled=True)  12.8 us
    slice x3, local copies, waits for them, and re-layouts, body(): val_local = jnp.concatenate([kv_cache[1], question_kv[:, 1]], axis=0)  10.1 us
    unnamed x31, local copies, waits for them, and re-layouts  9.79 us
    all_gather x1, blocking collectives, body(): every_query = lax.all_gather(query, 'ctx', axis=0, tiled=True)  7.49 us
    scatter x1, local copies, waits for them, and re-layouts, body(): cached.at[:, target, :]  7.48 us
  transfers between devices with their start and end apart: 8, of which 5 were waited for; matrix products, arithmetic and copies ran while one was open for 37% of the time, Pallas kernels for 0%

commit v1 on v0

v1 whole, which is shorter than its diff:
```python
import functools

import jax
import jax.numpy as jnp
from jax import lax
from jax.experimental import pallas as pl
from jax.sharding import PartitionSpec as P

HD = 128


norm_eps = 1e-05
neg_large = -1e30


def rms_rows(hidden, norm_gain):
    floats = hidden.astype(jnp.float32)
    factor = lax.rsqrt(jnp.mean(floats * floats, axis=-1, keepdims=True) + norm_eps)
    return (floats * factor * norm_gain.astype(jnp.float32)).astype(jnp.bfloat16)


def attn_kernel(rank_ref, q_ref, k_ref, v_ref, o_ref, m_ref, l_ref, *, score_scale):
    tq = q_ref.shape[0]
    first = pl.program_id(0) * tq
    scores = (
        lax.dot_general(
            q_ref[...], k_ref[...], (((1,), (1,)), ((), ())), preferred_element_type=jnp.float32
        )
        * score_scale
    )
    token = first + lax.broadcasted_iota(jnp.int32, scores.shape, 0)
    shown = rank_ref[...] <= token
    masked = jnp.where(shown, scores, neg_large)
    row_max = jnp.max(masked, axis=1, keepdims=True)
    weights = jnp.where(shown, jnp.exp(masked - row_max), 0.0)
    m_ref[...] = row_max
    l_ref[...] = jnp.sum(weights, axis=1, keepdims=True)
    o_ref[...] = jnp.dot(
        weights.astype(jnp.bfloat16), v_ref[...], preferred_element_type=jnp.float32
    )


def attend(queries, keys, vals, key_rank, group_size, score_scale):
    tokens, q_width = queries.shape
    key_count = keys.shape[0]
    heads = q_width // HD
    tq = min(tokens, 128)
    grid = (tokens // tq, heads)
    return pl.pallas_call(
        functools.partial(attn_kernel, score_scale=score_scale),
        grid=grid,
        in_specs=[
            pl.BlockSpec((1, key_count), lambda i, n: (0, 0)),
            pl.BlockSpec((tq, HD), lambda i, n: (i, n)),
            pl.BlockSpec((key_count, HD), lambda i, n: (0, n // group_size)),
            pl.BlockSpec((key_count, HD), lambda i, n: (0, n // group_size)),
        ],
        out_specs=[
            pl.BlockSpec((tq, HD), lambda i, n: (i, n)),
            pl.BlockSpec((None, tq, 1), lambda i, n: (n, i, 0)),
            pl.BlockSpec((None, tq, 1), lambda i, n: (n, i, 0)),
        ],
        out_shape=[
            jax.ShapeDtypeStruct((tokens, q_width), jnp.float32),
            jax.ShapeDtypeStruct((heads, tokens, 1), jnp.float32),
            jax.ShapeDtypeStruct((heads, tokens, 1), jnp.float32),
        ],
    )(key_rank, queries, keys, vals)


def body(
    question_hidden,
    recomp_hidden,
    norm_gain,
    w_query,
    w_keyval,
    pool_codes,
    pool_scales,
    block_owner,
    block_slot,
    recomp_pos,
):
    shards = lax.axis_size("ctx")
    own_index = lax.axis_index("ctx")
    q_rows = question_hidden.shape[0]
    r_rows = recomp_hidden.shape[0]
    row_count = q_rows + r_rows
    kv_width = w_keyval.shape[2]
    kv_heads = kv_width // HD
    q_width = w_query.shape[1]
    group_size = q_width // kv_width
    score_scale = HD ** (-0.5)

    owners = block_owner[:, 0].reshape(shards, -1)
    per_dev = owners.shape[1]
    slot_table = block_slot.reshape(shards, per_dev)
    capacity = max(2, 2 * per_dev // shards)
    positions = jnp.arange(per_dev)
    earlier_mask = positions[None, :] < positions[:, None]
    same_owner = owners[:, :, None] == owners[:, None, :]
    order_rank = jnp.sum((same_owner & earlier_mask[None]).astype(jnp.int32), axis=2)
    slot_ids = jnp.arange(capacity)
    chosen = (owners == own_index)[:, :, None] & (order_rank[:, :, None] == slot_ids[None, None, :])
    send_slot = jnp.sum(jnp.where(chosen, slot_table[:, :, None], 0), axis=1).reshape(-1)
    send_codes = jnp.take(pool_codes, send_slot, axis=0).reshape(
        (shards, capacity) + pool_codes.shape[1:]
    )
    send_scales = jnp.take(pool_scales, send_slot, axis=0).reshape(
        (shards, capacity) + pool_scales.shape[1:]
    )
    got_codes, got_scales = (
        lax.all_to_all(send_codes, "ctx", split_axis=0, concat_axis=0, tiled=True),
        lax.all_to_all(send_scales, "ctx", split_axis=0, concat_axis=0, tiled=True),
    )

    normed = jnp.concatenate(
        [rms_rows(question_hidden, norm_gain), rms_rows(recomp_hidden, norm_gain)], axis=0
    )
    pieces = lax.all_to_all(normed, "ctx", split_axis=1, concat_axis=0, tiled=True)
    width_part = pieces.shape[1]
    arranged = pieces.reshape(shards, row_count, width_part)
    question_part = arranged[:, :q_rows, :].reshape(shards * q_rows, width_part)
    kv_weight = w_keyval.reshape(w_keyval.shape[0], 2 * kv_width)
    query_part = jnp.dot(question_part, w_query, preferred_element_type=jnp.float32)
    kv_part = jnp.dot(pieces, kv_weight, preferred_element_type=jnp.float32)
    query_sum, kv_sum = lax.psum((query_part, kv_part), "ctx")
    every_query = query_sum.astype(jnp.bfloat16)
    every_kv = kv_sum.astype(jnp.bfloat16).reshape(shards, row_count, 2, kv_width)
    question_kv = lax.dynamic_index_in_dim(every_kv, own_index, 0, keepdims=False)[:q_rows]
    recomp_kv = every_kv[:, q_rows:].reshape(shards * r_rows, 2, kv_width)

    own_owner = lax.dynamic_index_in_dim(owners, own_index, 0, keepdims=False)
    own_rank = lax.dynamic_index_in_dim(order_rank, own_index, 0, keepdims=False)
    flat_index = own_owner * capacity + own_rank
    block_codes = jnp.take(
        got_codes.reshape((shards * capacity,) + pool_codes.shape[1:]), flat_index, axis=0
    )
    block_scales = jnp.take(
        got_scales.reshape((shards * capacity,) + pool_scales.shape[1:]), flat_index, axis=0
    )
    block_len = block_codes.shape[2]
    dequant = (
        block_codes.astype(jnp.float32).reshape(per_dev, 2, block_len, kv_heads, HD)
        * block_scales.astype(jnp.float32)[:, :, None, :, None]
    )
    ctx_dev = per_dev * block_len
    cached = jnp.transpose(
        dequant.astype(jnp.bfloat16).reshape(per_dev, 2, block_len, kv_width), (1, 0, 2, 3)
    ).reshape(2, ctx_dev, kv_width)

    local_pos = recomp_pos - own_index * ctx_dev
    match = local_pos[None, :] == jnp.arange(ctx_dev)[:, None]
    hit = jnp.any(match, axis=1)
    one_hot = match.astype(jnp.bfloat16)
    placed = jnp.einsum(
        "pi,ick->cpk", one_hot, recomp_kv, preferred_element_type=jnp.float32
    ).astype(jnp.bfloat16)
    kv_cache = jnp.where(hit[None, :, None], placed, cached)

    key_local = jnp.concatenate([kv_cache[0], question_kv[:, 0]], axis=0)
    val_local = jnp.concatenate([kv_cache[1], question_kv[:, 1]], axis=0)
    key_span = ctx_dev + q_rows
    key_offset = jnp.arange(key_span)
    key_rank = jnp.where(
        key_offset < ctx_dev, -1, own_index * q_rows + key_offset - ctx_dev
    ).astype(jnp.int32)[None, :]

    part_sums, part_max, part_total = attend(
        every_query, key_local, val_local, key_rank, group_size, score_scale
    )
    heads = q_width // HD

    def by_token(value):
        return jnp.transpose(value[:, :, 0]).reshape(shards, q_rows, heads)

    sent = (
        part_sums.reshape(shards, q_rows, q_width),
        by_token(part_max),
        by_token(part_total),
    )
    got_sums, got_max, got_total = (
        lax.all_to_all(sent[0], "ctx", split_axis=0, concat_axis=0, tiled=True),
        lax.all_to_all(sent[1], "ctx", split_axis=0, concat_axis=0, tiled=True),
        lax.all_to_all(sent[2], "ctx", split_axis=0, concat_axis=0, tiled=True),
    )
    best_max = jnp.max(got_max, axis=0)
    factor = jnp.exp(got_max - best_max[None])
    row_total = jnp.sum(got_total * factor, axis=0)
    weighted = jnp.sum(
        got_sums.reshape(shards, q_rows, heads, HD) * factor[..., None], axis=0
    )
    attended = (weighted / row_total[..., None]).reshape(q_rows, q_width).astype(jnp.bfloat16)
    return (attended, kv_cache)


def solution(mesh):
    placed = (
        P(("groups", "ctx"), None),
        P(("groups", "ctx"), None),
        P(),
        P("ctx", "tp"),
        P("ctx", None, "tp"),
        P(("groups", "ctx"), None, None, "tp"),
        P(("groups", "ctx"), None, "tp"),
        P("groups", None),
        P("groups"),
        P("groups"),
    )
    return jax.shard_map(
        body,
        mesh=mesh,
        in_specs=placed,
        out_specs=(P(("groups", "ctx"), "tp"), P(None, ("groups", "ctx"), "tp")),
        check_vma=False,
    )
```

time: 230 us -> 194 us (0.84)
  blocking collectives: 27 us -> 68.3 us
  local copies, waits for them, and re-layouts: 66.5 us -> 27.1 us
  waiting for transfers between devices: 44.6 us -> 23.3 us
  Pallas kernels: 0 us -> 18.2 us
  between operations: 14.5 us -> 1.05 us
  matrix products: 21 us -> 10.5 us
  other arithmetic: 30.7 us -> 24 us
  starting transfers between devices: 24.3 us -> 21 us
    psum x0 -> x1, blocking collectives: none -> 62.1 us  [body(): query_sum, kv_sum = lax.psum((query_part, kv_part), 'ctx')]
    all_gather x2 -> x0, blocking collectives: 27 us -> none  [the longest x1 19.5 us: body(): all_recomp = lax.all_gather(recomp_kv, 'ctx', axis=0, tiled=True)]
    reduce_scatter x2 -> x0, waiting for transfers between devices: 20.7 us -> none  [the longest x1 20.7 us: body(): lax.psum_scatter(jnp.dot(block_rows, kv_weight, preferred_element_type=jn...]
    pallas_call x0 -> x1, Pallas kernels: none -> 18.2 us  [attend(): pl.pallas_call(functools.partial(attn_kernel, score_scale=score_scale), g...]
    slice x9 -> x4, local copies, waits for them, and re-layouts: 15.7 us -> 1.79 us  [the longest x1 1.08 us: body(): question_part = arranged[:, :q_rows, :].reshape(shards * q_rows, width_part)]
    reshape x6 -> x5, local copies, waits for them, and re-layouts: 14.2 us -> 1.26 us  [the longest x1 1.09 us: body(): kv_sum.astype(jnp.bfloat16).reshape(shards, row_count, 2, kv_width)]
    dot_general x6 -> x3, matrix products: 21 us -> 10.5 us  [the longest x1 5.64 us: body(): jnp.dot(question_part, w_query, preferred_element_type=jnp.float32)]
    scatter x1 -> x0, local copies, waits for them, and re-layouts: 7.48 us -> none  [body(): cached.at[:, target, :]]
  transfers between devices with their start and end apart: 8 -> 5, of which waited for: 5 -> 3; matrix products, arithmetic and copies ran while one was open for 37% -> 20% of each run, Pallas kernels for 0% -> 0%
where the time goes in v1:
time: 194 us; the launch traced here: 193 us
  blocking collectives  68.3 us (35%)
  local copies, waits for them, and re-layouts  27.1 us (14%)
  other arithmetic  24 us (12%)
  waiting for transfers between devices  23.3 us (12%)
  starting transfers between devices  21 us (11%)
  Pallas kernels  18.2 us (9%)
  matrix products  10.5 us (5%)
    psum x1, blocking collectives, body(): query_sum, kv_sum = lax.psum((query_part, kv_part), 'ctx')  62.1 us
    pallas_call x1, Pallas kernels, attend(): pl.pallas_call(functools.partial(attn_kernel, score_scale=score_scale), g...  18.2 us
    all_to_all x1, waiting for transfers between devices, body(): lax.all_to_all(normed, 'ctx', split_axis=1, concat_axis=0, tiled=True)  12.7 us
    all_to_all x1, waiting for transfers between devices, body(): lax.all_to_all(sent[0], 'ctx', split_axis=0, concat_axis=0, tiled=True)  8.53 us
    unnamed x32, local copies, waits for them, and re-layouts  6.81 us
    all_to_all x1, blocking collectives, body(): lax.all_to_all(sent[2], 'ctx', split_axis=0, concat_axis=0, tiled=True)  6.14 us
    dot_general x1, matrix products, body(): jnp.dot(question_part, w_query, preferred_element_type=jnp.float32)  5.64 us
    all_to_all x1, starting transfers between devices, body(): lax.all_to_all(send_codes, 'ctx', split_axis=0, concat_axis=0, tiled=True)  4.84 us
  transfers between devices with their start and end apart: 5, of which 3 were waited for; matrix products, arithmetic and copies ran while one was open for 20% of the time, Pallas kernels for 0%

profile of v1, /device:TPU:0, one launch (start us, length us, event | category | flops | bytes accessed | tf_op | source)
XLA Modules:
  0.0 193.3 jit_solution(16668839388811474687)
XLA Ops:
  1.2 1.6 reduce.6
  6.3 4.2 %all-to-all-start.2 = ((bf16[4,16,2,2]{1,3,2,0:T(2,128)(2,1)}), bf16[4,16,2,2]{1,3,2,0:T(2,128)(2,1)S(1)}, u32[]{:S(2)}, u32[]{:S(2)}) async-start(bf16[4,16,2,2]{1,3,2,0:T(2,128)(2,1)} %broadcast_select_fusion.2), calls=%async_computation.2 | async-start | bytes 8192 | tf_op jit(solution)/shard_map/all_to_all | solution.py:113
  11.3 1.5 fusion.3
  16.1 4.4 %all-to-all-start = ((bf16[96,4,2048]{2,0,1:T(8,128)(2,1)}), bf16[96,4,2048]{2,0,1:T(8,128)(2,1)}, u32[]{:S(2)}, u32[]{:S(2)}) async-start(bf16[96,4,2048]{2,0,1:T(8,128)(2,1)} %bitcast.78), calls=%async_computation | async-start | bytes 3145728 | tf_op jit(solution)/shard_map/all_to_all | solution.py:119
  20.5 2.8 %gather_fusion = bf16[64,2,64,256]{3,2,1,0:T(8,128)(2,1)} fusion(bf16[48,2,64,256]{3,2,1,0:T(8,128)(2,1)S(1)} %copy-done, s32[1024]{0:T(1024)S(1)} %pad_clamp_fusion.1), kind=kCustom, calls=%fused_computation | custom fusion | bytes 8388864 | tf_op jit(solution)/shard_map/jit(_take)/gather | solution.py:105
  23.3 4.6 %broadcast_select_fusion = bf16[4,16,2,64,256]{4,3,2,1,0:T(8,128)(2,1)} fusion(bf16[4,16,2,64,256]{4,3,2,1,0:T(8,128)(2,1)} %bitcast.77, pred[4,16]{1,0:T(4,128)(4,1)S(1)} %compare_and_fusion), kind=kLoop, calls=%fused_computation.6 | loop fusion | flops 2097152 | bytes 8388672 | tf_op jit(solution)/shard_map/jit(_take)/select_n | solution.py:105
  27.9 12.7 %all-to-all-done = bf16[96,4,2048]{2,0,1:T(8,128)(2,1)} async-done(((bf16[96,4,2048]{2,0,1:T(8,128)(2,1)}), bf16[96,4,2048]{2,0,1:T(8,128)(2,1)}, u32[]{:S(2)}, u32[]{:S(2)}) %all-to-all-start) | async-done | bytes 1572896 | tf_op jit(solution)/shard_map/all_to_all | solution.py:119
  40.6 4.8 %all-to-all-start.1 = ((bf16[4,16,2,64,256]{4,3,2,1,0:T(8,128)(2,1)}), bf16[4,16,2,64,256]{4,3,2,1,0:T(8,128)(2,1)}, u32[]{:S(2)}, u32[]{:S(2)}) async-start(bf16[4,16,2,64,256]{4,3,2,1,0:T(8,128)(2,1)} %broadcast_select_fusion), calls=%async_computation.1 | async-start | bytes 8388608 | tf_op jit(solution)/shard_map/all_to_all | solution.py:112
  45.4 3.4 %copy.68 = bf16[256,8,2,256]{3,1,2,0:T(8,128)(2,1)} copy(bf16[256,8,2,256]{3,2,1,0:T(2,128)(2,1)} %bitcast.81) | data formatting | bytes 4194304
  52.0 3.9 %fusion.23 = f32[384,512]{1,0:T(8,128)} fusion(bf16[384,2048]{1,0:T(8,128)(2,1)} %bitcast.2, bf16[2048,512]{1,0:T(8,128)(2,1)} %bitcast.82), kind=kOutput, calls=%fused_computation.71 | convolution fusion | flops 805306368 | bytes 4456448 | tf_op jit(solution)/shard_map/dot_general | solution.py:125
  57.0 5.6 %fusion.22 = f32[128,2048]{1,0:T(8,128)} fusion(bf16[128,2048]{1,0:T(8,128)(2,1)S(1)} %bitcast.80, bf16[2048,2048]{1,0:T(8,128)(2,1)} %param.13), kind=kOutput, calls=%fused_computation.70 | convolution fusion | flops 1073741824 | bytes 9961472 | tf_op jit(solution)/shard_map/dot_general | solution.py:124
  62.7 62.1 %all-reduce.2 = (bf16[128,2048]{1,0:T(8,128)(2,1)}, bf16[384,512]{1,0:T(8,128)(2,1)}) all-reduce(f32[128,2048]{1,0:T(8,128)} %fusion.22, f32[384,512]{1,0:T(8,128)} %fusion.23), channel_id=1, replica_groups=mesh['groups'=2,'ctx'=4,'tp'=4] {'ctx'}, use_global_device_ids=true, to_apply=%region_2.3 | all-reduce | flops 458752 | bytes 2752512 | tf_op jit(solution)/shard_map/psum | solution.py:126
  126.7 4.3 %gather_fusion.1 = bf16[32,2,64,256]{3,2,1,0:T(8,128)(2,1)} fusion(bf16[64,2,64,256]{3,2,1,0:T(8,128)(2,1)} %bitcast.9, s32[1024]{0:T(1024)} %copy-done.6), kind=kCustom, calls=%fused_computation.1 | custom fusion | bytes 4194432 | tf_op jit(solution)/shard_map/jit(_take)/gather | solution.py:135
  131.0 2.6 %fusion = bf16[2,32,64,256]{3,2,0,1:T(8,128)(2,1)S(1)} fusion(f32[2,32,256]{2,0,1:T(2,128)} %bitcast.87, bf16[32,2,64,256]{3,2,1,0:T(8,128)(2,1)} %gather_fusion.1, pred[32]{0:T(512)(128)(4,1)} %copy-done.7), kind=kLoop, calls=%fused_computation.5 | loop fusion | flops 4194304 | bytes 4259872 | tf_op jit(solution)/shard_map/convert_element_type | solution.py:148
  138.3 18.2 %shard_map.113 = (f32[128,2048]{1,0:T(8,128)}, f32[16,128,1]{2,1,0:T(8,128)}, f32[16,128,1]{2,1,0:T(8,128)}) custom-call(s32[1,2080]{1,0:T(1,128)} %compare_select_fusion.rank_ref, bf16[128,2048]{1,0:T(8,128)(2,1)} %get-tuple-element.8.q_ref, bf16[2080,256]{1,0:T(8,128)(2,1)} %get-tuple-element.18.k_ref, bf16[2080,256]{1,0:T(8,128)(2,1)} %get-tuple-element.19.v_ref), custom_call_target="tpu_custom_call" | custom-call | tf_op jit(solution)/shard_map/pallas_call | solution.py:49
  156.5 1.6 reduce.2
  158.8 3.2 %all-to-all-start.4 = ((f32[4,1,512]{2,1,0:T(1,128)}), f32[4,1,512]{2,1,0:T(1,128)S(1)}, u32[]{:S(2)}, u32[]{:S(2)}) async-start(f32[4,1,512]{2,1,0:T(1,128)} %reshape.258), calls=%async_computation.4 | async-start | bytes 16384 | tf_op jit(solution)/shard_map/all_to_all | solution.py:183
  162.1 1.6 reduce.3
  163.8 2.0 %all-to-all-done.4 = f32[4,1,512]{2,1,0:T(1,128)S(1)} async-done(((f32[4,1,512]{2,1,0:T(1,128)}), f32[4,1,512]{2,1,0:T(1,128)S(1)}, u32[]{:S(2)}, u32[]{:S(2)}) %all-to-all-start.4) | async-done | bytes 8224 | tf_op jit(solution)/shard_map/all_to_all | solution.py:183
  165.9 6.1 %all_to_all.44 = f32[4,1,512]{2,1,0:T(1,128)S(1)} all-to-all(f32[4,1,512]{2,1,0:T(1,128)S(1)} %reshape.260), channel_id=1, replica_groups=mesh['groups'=2,'ctx'=4,'tp'=4] {'ctx'}, dimensions={0} | all-to-all | bytes 16384 | tf_op jit(solution)/shard_map/all_to_all | solution.py:184
  172.0 4.2 %all-to-all-start.3 = ((f32[4,32,2048]{2,1,0:T(8,128)}), f32[4,32,2048]{2,1,0:T(8,128)}, u32[]{:S(2)}, u32[]{:S(2)}) async-start(f32[4,32,2048]{2,1,0:T(8,128)} %bitcast.85), calls=%async_computation.3 | async-start | bytes 2097152 | tf_op jit(solution)/shard_map/all_to_all | solution.py:182
  179.7 2.4 %mul.111 = f32[4,32,2048]{2,1,0:T(8,128)} reshape(f32[4,32,16,128]{3,2,1,0:T(8,128)} %mul.110) | data formatting | bytes 2097152 | tf_op jit(solution)/shard_map/mul | solution.py:190
  182.2 8.5 %all-to-all-done.3 = f32[4,32,2048]{2,1,0:T(8,128)} async-done(((f32[4,32,2048]{2,1,0:T(8,128)}), f32[4,32,2048]{2,1,0:T(8,128)}, u32[]{:S(2)}, u32[]{:S(2)}) %all-to-all-start.3) | async-done | bytes 1048608 | tf_op jit(solution)/shard_map/all_to_all | solution.py:182
  190.7 1.7 multiply_reduce_fusion
  (89 shorter events, 24.1 us)
Async XLA Ops:
  0.6 19.8 %copy-start = (bf16[48,2,64,256]{3,2,1,0:T(8,128)(2,1)S(1)}, bf16[48,2,64,256]{3,2,1,0:T(8,128)(2,1)}, u32[]{:S(2)}) copy-start(bf16[48,2,64,256]{3,2,1,0:T(8,128)(2,1)} %param.15) | copy-start | bytes 9437188
  6.3 9.8 %all-to-all-start.2 = ((bf16[4,16,2,2]{1,3,2,0:T(2,128)(2,1)}), bf16[4,16,2,2]{1,3,2,0:T(2,128)(2,1)S(1)}, u32[]{:S(2)}, u32[]{:S(2)}) async-start(bf16[4,16,2,2]{1,3,2,0:T(2,128)(2,1)} %broadcast_select_fusion.2), calls=%async_computation.2 | async-start | bytes 8192 | tf_op jit(solution)/shard_map/all_to_all | solution.py:113
  10.5 3.7 %copy-start.1 = (bf16[64,8192]{1,0:T(8,128)(2,1)S(1)}, bf16[64,8192]{1,0:T(8,128)(2,1)}, u32[]{:S(2)}) copy-start(bf16[64,8192]{1,0:T(8,128)(2,1)} %param.11) | copy-start | bytes 3145732
  10.5 4.0 %copy-start.3 = (bf16[32,8192]{1,0:T(8,128)(2,1)S(1)}, bf16[32,8192]{1,0:T(8,128)(2,1)}, u32[]{:S(2)}) copy-start(bf16[32,8192]{1,0:T(8,128)(2,1)} %param.10) | copy-start | bytes 1572868
  16.1 24.5 %all-to-all-start = ((bf16[96,4,2048]{2,0,1:T(8,128)(2,1)}), bf16[96,4,2048]{2,0,1:T(8,128)(2,1)}, u32[]{:S(2)}, u32[]{:S(2)}) async-start(bf16[96,4,2048]{2,0,1:T(8,128)(2,1)} %bitcast.78), calls=%async_computation | async-start | bytes 3145728 | tf_op jit(solution)/shard_map/all_to_all | solution.py:119
  20.5 2.8 %copy-start.8 = (s32[256]{0:T(256)S(1)}, s32[256]{0:T(256)}, u32[]{:S(2)}) copy-start(s32[256]{0:T(256)} %param.19) | copy-start | bytes 3076
  23.3 27.8 %copy-start.7 = (pred[32]{0:T(512)(128)(4,1)}, pred[32]{0:T(512)(128)(4,1)S(1)}, u32[]{:S(2)}) copy-start(pred[32]{0:T(512)(128)(4,1)S(1)} %get-tuple-element.12) | copy-start | bytes 100
  23.3 25.5 %copy-start.9 = (s32[256]{0:T(256)}, s32[256]{0:T(256)S(1)}, u32[]{:S(2)}) copy-start(s32[256]{0:T(256)S(1)} %broadcast_subtract_fusion) | copy-start | bytes 3076
  40.6 86.1 %all-to-all-start.1 = ((bf16[4,16,2,64,256]{4,3,2,1,0:T(8,128)(2,1)}), bf16[4,16,2,64,256]{4,3,2,1,0:T(8,128)(2,1)}, u32[]{:S(2)}, u32[]{:S(2)}) async-start(bf16[4,16,2,64,256]{4,3,2,1,0:T(8,128)(2,1)} %broadcast_select_fusion), calls=%async_computation.1 | async-start | bytes 8388608 | tf_op jit(solution)/shard_map/all_to_all | solution.py:112
  48.8 2.2 %copy-start.6 = (s32[1024]{0:T(1024)}, s32[1024]{0:T(1024)S(1)}, u32[]{:S(2)}) copy-start(s32[1024]{0:T(1024)S(1)} %pad_clamp_fusion) | copy-start | bytes 12292
  125.9 5.1 %copy-start.4 = (bf16[4,96,2,256]{3,2,1,0:T(2,128)(2,1)}, bf16[4,96,2,256]{3,2,1,0:T(2,128)(2,1)S(1)}, u32[]{:S(2)}) copy-start(bf16[4,96,2,256]{3,2,1,0:T(2,128)(2,1)S(1)} %reshape.205) | copy-start | bytes 1179652
  133.6 1.0 slice-start
  133.6 0.9 copy-start.10
  133.6 0.9 copy-start.11
  135.4 1.3 copy-start.2
  135.5 1.3 copy-start.5
  158.8 7.0 %all-to-all-start.4 = ((f32[4,1,512]{2,1,0:T(1,128)}), f32[4,1,512]{2,1,0:T(1,128)S(1)}, u32[]{:S(2)}, u32[]{:S(2)}) async-start(f32[4,1,512]{2,1,0:T(1,128)} %reshape.258), calls=%async_computation.4 | async-start | bytes 16384 | tf_op jit(solution)/shard_map/all_to_all | solution.py:183
  172.0 18.7 %all-to-all-start.3 = ((f32[4,32,2048]{2,1,0:T(8,128)}), f32[4,32,2048]{2,1,0:T(8,128)}, u32[]{:S(2)}, u32[]{:S(2)}) async-start(f32[4,32,2048]{2,1,0:T(8,128)} %bitcast.85), calls=%async_computation.3 | async-start | bytes 2097152 | tf_op jit(solution)/shard_map/all_to_all | solution.py:182

commit v2 on v1

v2 whole, which is shorter than its diff:
```python
import functools

import jax
import jax.numpy as jnp
from jax import lax
from jax.experimental import pallas as pl
from jax.sharding import PartitionSpec as P

HD = 128


norm_eps = 1e-05
neg_large = -1e30


def rms_rows(hidden, norm_gain):
    floats = hidden.astype(jnp.float32)
    factor = lax.rsqrt(jnp.mean(floats * floats, axis=-1, keepdims=True) + norm_eps)
    return (floats * factor * norm_gain.astype(jnp.float32)).astype(jnp.bfloat16)


def attn_kernel(rank_ref, q_ref, k_ref, v_ref, o_ref, m_ref, l_ref, *, score_scale, ctx_keys):
    tq = q_ref.shape[0]
    first = pl.program_id(0) * tq
    dims = (((1,), (1,)), ((), ()))
    queries = q_ref[...]
    ctx_scores = (
        lax.dot_general(queries, k_ref[:ctx_keys, :], dims, preferred_element_type=jnp.float32)
        * score_scale
    )
    own_scores = (
        lax.dot_general(queries, k_ref[ctx_keys:, :], dims, preferred_element_type=jnp.float32)
        * score_scale
    )
    token = first + lax.broadcasted_iota(jnp.int32, own_scores.shape, 0)
    shown = rank_ref[...] <= token
    own_masked = jnp.where(shown, own_scores, neg_large)
    row_max = jnp.maximum(
        jnp.max(ctx_scores, axis=1, keepdims=True), jnp.max(own_masked, axis=1, keepdims=True)
    )
    ctx_weights = jnp.exp(ctx_scores - row_max)
    own_weights = jnp.where(shown, jnp.exp(own_masked - row_max), 0.0)
    m_ref[...] = row_max
    l_ref[...] = jnp.sum(ctx_weights, axis=1, keepdims=True) + jnp.sum(
        own_weights, axis=1, keepdims=True
    )
    o_ref[...] = jnp.dot(
        ctx_weights.astype(jnp.bfloat16), v_ref[:ctx_keys, :], preferred_element_type=jnp.float32
    ) + jnp.dot(
        own_weights.astype(jnp.bfloat16), v_ref[ctx_keys:, :], preferred_element_type=jnp.float32
    )


def attend(queries, keys, vals, key_rank, ctx_keys, group_size, score_scale):
    tokens, q_width = queries.shape
    key_count = keys.shape[0]
    heads = q_width // HD
    tq = min(tokens, 128)
    grid = (tokens // tq, heads)
    return pl.pallas_call(
        functools.partial(attn_kernel, score_scale=score_scale, ctx_keys=ctx_keys),
        grid=grid,
        in_specs=[
            pl.BlockSpec((1, key_count - ctx_keys), lambda i, n: (0, 0)),
            pl.BlockSpec((tq, HD), lambda i, n: (i, n)),
            pl.BlockSpec((key_count, HD), lambda i, n: (0, n // group_size)),
            pl.BlockSpec((key_count, HD), lambda i, n: (0, n // group_size)),
        ],
        out_specs=[
            pl.BlockSpec((tq, HD), lambda i, n: (i, n)),
            pl.BlockSpec((None, tq, 1), lambda i, n: (n, i, 0)),
            pl.BlockSpec((None, tq, 1), lambda i, n: (n, i, 0)),
        ],
        out_shape=[
            jax.ShapeDtypeStruct((tokens, q_width), jnp.float32),
            jax.ShapeDtypeStruct((heads, tokens, 1), jnp.float32),
            jax.ShapeDtypeStruct((heads, tokens, 1), jnp.float32),
        ],
    )(key_rank, queries, keys, vals)


def body(
    question_hidden,
    recomp_hidden,
    norm_gain,
    w_query,
    w_keyval,
    pool_codes,
    pool_scales,
    block_owner,
    block_slot,
    recomp_pos,
):
    shards = lax.axis_size("ctx")
    own_index = lax.axis_index("ctx")
    q_rows = question_hidden.shape[0]
    r_rows = recomp_hidden.shape[0]
    row_count = q_rows + r_rows
    kv_width = w_keyval.shape[2]
    kv_heads = kv_width // HD
    q_width = w_query.shape[1]
    heads = q_width // HD
    group_size = q_width // kv_width
    score_scale = HD ** (-0.5)

    owners = block_owner[:, 0].reshape(shards, -1)
    per_dev = owners.shape[1]
    slot_table = block_slot.reshape(shards, per_dev)
    capacity = max(2, 2 * per_dev // shards)
    positions = jnp.arange(per_dev)
    earlier_mask = positions[None, :] < positions[:, None]
    same_owner = owners[:, :, None] == owners[:, None, :]
    order_rank = jnp.sum((same_owner & earlier_mask[None]).astype(jnp.int32), axis=2)
    slot_ids = jnp.arange(capacity)
    chosen = (owners == own_index)[:, :, None] & (order_rank[:, :, None] == slot_ids[None, None, :])
    send_slot = jnp.sum(jnp.where(chosen, slot_table[:, :, None], 0), axis=1).reshape(-1)
    block_len = pool_codes.shape[2]
    send_codes = jnp.take(pool_codes, send_slot, axis=0)
    send_scales = jnp.take(pool_scales, send_slot, axis=0)
    send_blocks = (
        send_codes.astype(jnp.float32).reshape(shards * capacity, 2, block_len, kv_heads, HD)
        * send_scales.astype(jnp.float32)[:, :, None, :, None]
    ).astype(jnp.bfloat16).reshape((shards, capacity, 2, block_len, kv_width))
    got_blocks = lax.all_to_all(send_blocks, "ctx", split_axis=0, concat_axis=0, tiled=True)

    normed = jnp.concatenate(
        [rms_rows(question_hidden, norm_gain), rms_rows(recomp_hidden, norm_gain)], axis=0
    )
    pieces = lax.all_to_all(normed, "ctx", split_axis=1, concat_axis=0, tiled=True)
    width_part = pieces.shape[1]
    arranged = pieces.reshape(shards, row_count, width_part)
    question_part = arranged[:, :q_rows, :].reshape(shards * q_rows, width_part)
    kv_weight = w_keyval.reshape(w_keyval.shape[0], 2 * kv_width)
    query_part = jnp.dot(question_part, w_query, preferred_element_type=jnp.float32)
    kv_part = jnp.dot(pieces, kv_weight, preferred_element_type=jnp.float32)

    q_size = q_rows * q_width
    partials = jnp.concatenate(
        [query_part.reshape(shards, q_size), kv_part.reshape(shards, row_count * 2 * kv_width)],
        axis=1,
    )
    summed = jnp.sum(
        lax.all_to_all(partials, "ctx", split_axis=0, concat_axis=0, tiled=True), axis=0
    ).astype(jnp.bfloat16)
    gathered = lax.all_gather(summed, "ctx", axis=0, tiled=False)
    every_query = gathered[:, :q_size].reshape(shards * q_rows, q_width)
    every_kv = gathered[:, q_size:].reshape(shards, row_count, 2, kv_width)
    question_kv = summed[q_size:].reshape(row_count, 2, kv_width)[:q_rows]
    recomp_kv = every_kv[:, q_rows:].reshape(shards * r_rows, 2, kv_width)

    own_owner = lax.dynamic_index_in_dim(owners, own_index, 0, keepdims=False)
    own_rank = lax.dynamic_index_in_dim(order_rank, own_index, 0, keepdims=False)
    flat_index = own_owner * capacity + own_rank
    block_rows = jnp.take(
        got_blocks.reshape((shards * capacity, 2, block_len, kv_width)), flat_index, axis=0
    )
    ctx_dev = per_dev * block_len
    cached = jnp.transpose(block_rows, (1, 0, 2, 3)).reshape(2, ctx_dev, kv_width)

    local_pos = recomp_pos - own_index * ctx_dev
    match = local_pos[None, :] == jnp.arange(ctx_dev)[:, None]
    hit = jnp.any(match, axis=1)
    one_hot = match.astype(jnp.bfloat16)
    placed = jnp.einsum(
        "pi,ick->cpk", one_hot, recomp_kv, preferred_element_type=jnp.float32
    ).astype(jnp.bfloat16)
    kv_cache = jnp.where(hit[None, :, None], placed, cached)

    key_local = jnp.concatenate([kv_cache[0], question_kv[:, 0]], axis=0)
    val_local = jnp.concatenate([kv_cache[1], question_kv[:, 1]], axis=0)
    key_rank = (own_index * q_rows + jnp.arange(q_rows)).astype(jnp.int32)[None, :]

    part_sums, part_max, part_total = attend(
        every_query, key_local, val_local, key_rank, ctx_dev, group_size, score_scale
    )

    def by_token(value):
        return jnp.transpose(value[:, :, 0]).reshape(shards, q_rows, heads)

    sent = jnp.concatenate(
        [part_sums.reshape(shards, q_rows, q_width), by_token(part_max), by_token(part_total)],
        axis=2,
    )
    got = lax.all_to_all(sent, "ctx", split_axis=0, concat_axis=0, tiled=True)
    got_sums = got[:, :, :q_width]
    got_max = got[:, :, q_width : q_width + heads]
    got_total = got[:, :, q_width + heads :]
    best_max = jnp.max(got_max, axis=0)
    factor = jnp.exp(got_max - best_max[None])
    row_total = jnp.sum(got_total * factor, axis=0)
    weighted = jnp.sum(
        got_sums.reshape(shards, q_rows, heads, HD) * factor[..., None], axis=0
    )
    attended = (weighted / row_total[..., None]).reshape(q_rows, q_width).astype(jnp.bfloat16)
    return (attended, kv_cache)


def solution(mesh):
    placed = (
        P(("groups", "ctx"), None),
        P(("groups", "ctx"), None),
        P(),
        P("ctx", "tp"),
        P("ctx", None, "tp"),
        P(("groups", "ctx"), None, None, "tp"),
        P(("groups", "ctx"), None, "tp"),
        P("groups", None),
        P("groups"),
        P("groups"),
    )
    return jax.shard_map(
        body,
        mesh=mesh,
        in_specs=placed,
        out_specs=(P(("groups", "ctx"), "tp"), P(None, ("groups", "ctx"), "tp")),
        check_vma=False,
    )
```

time: 194 us -> 195 us (level)
  starting transfers between devices: 21 us -> 13.9 us
  waiting for transfers between devices: 23.3 us -> 28.2 us
  local copies, waits for them, and re-layouts: 27.1 us -> 31.6 us
  Pallas kernels: 18.2 us -> 16.2 us
    psum x1 -> x0, blocking collectives: 62.1 us -> none  [body(): query_sum, kv_sum = lax.psum((query_part, kv_part), 'ctx')]
    all_gather x0 -> x1, blocking collectives: none -> 49.4 us  [body(): gathered = lax.all_gather(summed, 'ctx', axis=0, tiled=False)]
    all_to_all x1, blocking collectives: 6.14 us -> 17.5 us  [body(): got = lax.all_to_all(sent, 'ctx', split_axis=0, concat_axis=0, tiled=True)]
    all_to_all x4 -> x2, starting transfers between devices: 16.6 us -> 9.48 us  [the longest x1 5.02 us: body(): lax.all_to_all(send_blocks, 'ctx', split_axis=0, concat_axis=0, tiled=True)]
    reshape x1 -> x4, local copies, waits for them, and re-layouts: 1.09 us -> 7.16 us  [the longest x1 2.93 us: body(): query_part.reshape(shards, q_size)]
    select_n x5 -> x3, other arithmetic: 5.77 us -> 0.27 us  [the longest x2 0.27 us: body(): jnp.take(got_blocks.reshape((shards * capacity, 2, block_len, kv_width)),...]
    convert_element_type x2, other arithmetic: 2.66 us -> 6.25 us  [the longest x1 6.12 us: body(): send_blocks = (send_codes.astype(jnp.float32).reshape(shards * capacity,...]
    reduce_sum x0 -> x1, other arithmetic: none -> 3.21 us  [body(): jnp.sum(lax.all_to_all(partials, 'ctx', split_axis=0, concat_axis=0, tile...]
  transfers between devices with their start and end apart: 5 -> 3, of which waited for: 3 -> 2; matrix products, arithmetic and copies ran while one was open for 20% -> 11% of each run, Pallas kernels for 0% -> 0%
where the time goes in v2:
time: 195 us; the launch traced here: 194 us
  blocking collectives  67 us (34%)
  local copies, waits for them, and re-layouts  31.6 us (16%)
  waiting for transfers between devices  28.2 us (14%)
  other arithmetic  25.9 us (13%)
  Pallas kernels  16.2 us (8%)
  starting transfers between devices  13.9 us (7%)
  matrix products  10.5 us (5%)
    all_gather x1, blocking collectives, body(): gathered = lax.all_gather(summed, 'ctx', axis=0, tiled=False)  49.4 us
    all_to_all x1, blocking collectives, body(): got = lax.all_to_all(sent, 'ctx', split_axis=0, concat_axis=0, tiled=True)  17.5 us
    pallas_call x1, Pallas kernels, attend(): pl.pallas_call(functools.partial(attn_kernel, score_scale=score_scale, ct...  16.2 us
    all_to_all x1, waiting for transfers between devices, body(): lax.all_to_all(normed, 'ctx', split_axis=1, concat_axis=0, tiled=True)  15.4 us
    all_to_all x1, waiting for transfers between devices, body(): lax.all_to_all(partials, 'ctx', split_axis=0, concat_axis=0, tiled=True)  12.8 us
    unnamed x27, local copies, waits for them, and re-layouts  6.19 us
    convert_element_type x1, other arithmetic, body(): send_blocks = (send_codes.astype(jnp.float32).reshape(shards * capacity,...  6.12 us
    dot_general x1, matrix products, body(): jnp.dot(question_part, w_query, preferred_element_type=jnp.float32)  5.65 us
  transfers between devices with their start and end apart: 3, of which 2 were waited for; matrix products, arithmetic and copies ran while one was open for 11% of the time, Pallas kernels for 0%

profile of v2, /device:TPU:0, one launch (start us, length us, event | category | flops | bytes accessed | tf_op | source)
XLA Modules:
  0.0 194.3 jit_solution(1243157139741643156)
XLA Ops:
  1.5 1.7 fusion.2
  6.4 4.5 %all-to-all-start = ((bf16[96,4,2048]{2,0,1:T(8,128)(2,1)}), bf16[96,4,2048]{2,0,1:T(8,128)(2,1)}, u32[]{:S(2)}, u32[]{:S(2)}) async-start(bf16[96,4,2048]{2,0,1:T(8,128)(2,1)} %bitcast.57), calls=%async_computation | async-start | bytes 3145728 | tf_op jit(solution)/shard_map/all_to_all | solution.py:129
  12.9 3.4 %copy.66 = bf16[256,8,2,256]{3,1,2,0:T(8,128)(2,1)} copy(bf16[256,8,2,256]{3,2,1,0:T(2,128)(2,1)} %bitcast.60) | data formatting | bytes 4194304
  16.3 15.4 %all-to-all-done = bf16[96,4,2048]{2,0,1:T(8,128)(2,1)} async-done(((bf16[96,4,2048]{2,0,1:T(8,128)(2,1)}), bf16[96,4,2048]{2,0,1:T(8,128)(2,1)}, u32[]{:S(2)}, u32[]{:S(2)}) %all-to-all-start) | async-done | bytes 1572896 | tf_op jit(solution)/shard_map/all_to_all | solution.py:129
  31.7 3.9 %fusion.22 = f32[384,512]{1,0:T(8,128)} fusion(bf16[384,2048]{1,0:T(8,128)(2,1)} %bitcast.2, bf16[2048,512]{1,0:T(8,128)(2,1)} %bitcast.61), kind=kOutput, calls=%fused_computation.67 | convolution fusion | flops 805306368 | bytes 4456448 | tf_op jit(solution)/shard_map/dot_general | solution.py:135
  35.6 2.6 %reshape.212 = f32[4,49152]{1,0:T(4,128)} reshape(f32[384,512]{1,0:T(8,128)} %fusion.22) | data formatting | bytes 1572864 | tf_op jit(solution)/shard_map/reshape | solution.py:139
  39.2 5.6 %fusion.21 = f32[128,2048]{1,0:T(8,128)} fusion(bf16[128,2048]{1,0:T(8,128)(2,1)S(1)} %bitcast.59, bf16[2048,2048]{1,0:T(8,128)(2,1)} %param.13), kind=kOutput, calls=%fused_computation.66 | convolution fusion | flops 1073741824 | bytes 9961472 | tf_op jit(solution)/shard_map/dot_general | solution.py:134
  44.9 2.9 %reshape.210 = f32[4,65536]{1,0:T(4,128)} reshape(f32[128,2048]{1,0:T(8,128)} %fusion.21) | data formatting | bytes 2097152 | tf_op jit(solution)/shard_map/reshape | solution.py:139
  47.8 1.9 pad_maximum_fusion
  49.7 2.5 %all_to_all.30 = f32[4,1,114688]{2,1,0:T(1,128)} reshape(f32[4,114688]{1,0:T(4,128)S(1)} %pad_maximum_fusion) | data formatting | bytes 3670016 | tf_op jit(solution)/shard_map/all_to_all | solution.py:143
  52.2 4.5 %all-to-all-start.1 = ((f32[4,1,114688]{2,1,0:T(1,128)}), f32[4,1,114688]{2,1,0:T(1,128)}, u32[]{:S(2)}, u32[]{:S(2)}) async-start(f32[4,1,114688]{2,1,0:T(1,128)} %all_to_all.30), calls=%async_computation.1 | async-start | bytes 3670016 | tf_op jit(solution)/shard_map/all_to_all | solution.py:143
  57.8 2.8 %gather_fusion = bf16[64,2,64,256]{3,2,1,0:T(8,128)(2,1)} fusion(bf16[48,2,64,256]{3,2,1,0:T(8,128)(2,1)S(1)} %copy-done, s32[1024]{0:T(1024)S(1)} %pad_clamp_fusion.1), kind=kCustom, calls=%fused_computation | custom fusion | bytes 8388864 | tf_op jit(solution)/shard_map/jit(_take)/gather | solution.py:118
  60.6 6.1 %multiply_convert_fusion = bf16[4,16,2,64,256]{4,3,2,1,0:T(8,128)(2,1)} fusion(f32[4,16,2,256]{3,2,1,0:T(2,128)S(1)} %mul.103, bf16[4,16,2,64,256]{4,3,2,1,0:T(8,128)(2,1)} %bitcast.56, pred[4,16]{1,0:T(4,128)(4,1)S(1)} %compare_and_fusion.1), kind=kLoop, calls=%fused_computation.3 | loop fusion | flops 8388608 | bytes 8519744 | tf_op jit(solution)/shard_map/convert_element_type | solution.py:123
  66.8 12.8 %all-to-all-done.1 = f32[4,1,114688]{2,1,0:T(1,128)} async-done(((f32[4,1,114688]{2,1,0:T(1,128)}), f32[4,1,114688]{2,1,0:T(1,128)}, u32[]{:S(2)}, u32[]{:S(2)}) %all-to-all-start.1) | async-done | bytes 1835040 | tf_op jit(solution)/shard_map/all_to_all | solution.py:143
  79.6 5.0 %all-to-all-start.2 = ((bf16[4,16,2,64,256]{4,3,2,1,0:T(8,128)(2,1)}), bf16[4,16,2,64,256]{4,3,2,1,0:T(8,128)(2,1)}, u32[]{:S(2)}, u32[]{:S(2)}) async-start(bf16[4,16,2,64,256]{4,3,2,1,0:T(8,128)(2,1)} %multiply_convert_fusion), calls=%async_computation.2 | async-start | bytes 8388608 | tf_op jit(solution)/shard_map/all_to_all | solution.py:124
  85.5 3.2 %reduce_sum.65 = bf16[114688]{0:T(1024)(128)(2,1)S(1)} reduce(f32[4,1,114688]{2,1,0:T(1,128)} %all-to-all-done.1, f32[]{:T(128)} %constant.43.clone.1), dimensions={0,1}, to_apply=%region_2.3 | reduce | flops 344064 | bytes 2064388 | tf_op jit(solution)/shard_map/reduce_sum | solution.py:142
  88.9 49.4 %all-gather = bf16[458752]{0:T(1024)(128)(2,1)S(1)} all-gather(bf16[114688]{0:T(1024)(128)(2,1)S(1)} %reduce_sum.65), channel_id=2, replica_groups=mesh['groups'=2,'ctx'=4,'tp'=4] {'ctx'}, dimensions={0}, use_global_device_ids=true | all-gather | bytes 1146880 | tf_op jit(solution)/shard_map/all_gather | solution.py:145
  140.8 2.9 %gather_fusion.2 = bf16[32,2,64,256]{3,2,1,0:T(8,128)(2,1)S(1)} fusion(bf16[64,2,64,256]{3,2,1,0:T(8,128)(2,1)} %bitcast.9, s32[1024]{0:T(1024)S(1)} %pad_clamp_fusion), kind=kCustom, calls=%fused_computation.2 | custom fusion | bytes 4194432 | tf_op jit(solution)/shard_map/jit(_take)/gather | solution.py:154
  149.3 16.2 %shard_map.113 = (f32[128,2048]{1,0:T(8,128)}, f32[16,128,1]{2,1,0:T(8,128)}, f32[16,128,1]{2,1,0:T(8,128)}) custom-call(s32[1,32]{1,0:T(1,128)} %iota_add_fusion.rank_ref, bf16[128,2048]{1,0:T(8,128)(2,1)} %reshape.213.q_ref, bf16[2080,256]{1,0:T(8,128)(2,1)} %pad_maximum_fusion.2.k_ref, bf16[2080,256]{1,0:T(8,128)(2,1)} %pad_maximum_fusion.3.v_ref), custom_call_target="tpu_custom_call" | custom-call | tf_op jit(solution)/shard_map/pallas_call | solution.py:60
  165.5 1.7 reduce.3
  167.2 1.6 reduce.4
  169.2 17.5 %all_to_all.38 = f32[4,32,2080]{2,1,0:T(8,128)S(1)} all-to-all(f32[4,32,2080]{2,1,0:T(8,128)S(1)} %concatenate.19), channel_id=1, replica_groups=mesh['groups'=2,'ctx'=4,'tp'=4] {'ctx'}, dimensions={0} | all-to-all | bytes 2129920 | tf_op jit(solution)/shard_map/all_to_all | solution.py:184
  189.1 2.5 %mul.107 = f32[4,32,2048]{2,1,0:T(8,128)} reshape(f32[4,32,16,128]{3,2,1,0:T(8,128)} %mul.106) | data formatting | bytes 2097152 | tf_op jit(solution)/shard_map/mul | solution.py:192
  191.7 1.7 fusion.11
  (83 shorter events, 21.1 us)
Async XLA Ops:
  0.6 57.2 %copy-start = (bf16[48,2,64,256]{3,2,1,0:T(8,128)(2,1)S(1)}, bf16[48,2,64,256]{3,2,1,0:T(8,128)(2,1)}, u32[]{:S(2)}) copy-start(bf16[48,2,64,256]{3,2,1,0:T(8,128)(2,1)} %param.15) | copy-start | bytes 9437188
  0.6 3.8 %copy-start.3 = (bf16[64,8192]{1,0:T(8,128)(2,1)S(1)}, bf16[64,8192]{1,0:T(8,128)(2,1)}, u32[]{:S(2)}) copy-start(bf16[64,8192]{1,0:T(8,128)(2,1)} %param.11) | copy-start | bytes 3145732
  0.7 4.2 %copy-start.5 = (bf16[32,8192]{1,0:T(8,128)(2,1)S(1)}, bf16[32,8192]{1,0:T(8,128)(2,1)}, u32[]{:S(2)}) copy-start(bf16[32,8192]{1,0:T(8,128)(2,1)} %param.10) | copy-start | bytes 1572868
  6.4 5.0 %copy-start.11 = (s32[128,1]{0,1:T(1,128)S(1)}, s32[128,1]{0,1:T(1,128)}, u32[]{:S(2)}) copy-start(s32[128,1]{0,1:T(1,128)} %param.17) | copy-start | bytes 1540
  6.4 5.7 %copy-start.10 = (s32[128]{0:T(128)S(1)}, s32[128]{0:T(128)}, u32[]{:S(2)}) copy-start(s32[128]{0:T(128)} %param.18) | copy-start | bytes 1540
  6.4 6.4 %copy-start.8 = (bf16[48,2,2]{0,2,1:T(2,128)(2,1)S(1)}, bf16[48,2,2]{0,2,1:T(2,128)(2,1)}, u32[]{:S(2)}) copy-start(bf16[48,2,2]{0,2,1:T(2,128)(2,1)} %param.16) | copy-start | bytes 1156
  6.4 25.3 %all-to-all-start = ((bf16[96,4,2048]{2,0,1:T(8,128)(2,1)}), bf16[96,4,2048]{2,0,1:T(8,128)(2,1)}, u32[]{:S(2)}, u32[]{:S(2)}) async-start(bf16[96,4,2048]{2,0,1:T(8,128)(2,1)} %bitcast.57), calls=%async_computation | async-start | bytes 3145728 | tf_op jit(solution)/shard_map/all_to_all | solution.py:129
  52.2 27.4 %all-to-all-start.1 = ((f32[4,1,114688]{2,1,0:T(1,128)}), f32[4,1,114688]{2,1,0:T(1,128)}, u32[]{:S(2)}, u32[]{:S(2)}) async-start(f32[4,1,114688]{2,1,0:T(1,128)} %all_to_all.30), calls=%async_computation.1 | async-start | bytes 3670016 | tf_op jit(solution)/shard_map/all_to_all | solution.py:143
  66.7 18.4 %copy-start.9 = (s32[256]{0:T(256)S(1)}, s32[256]{0:T(256)}, u32[]{:S(2)}) copy-start(s32[256]{0:T(256)} %param.19) | copy-start | bytes 3076
  79.6 61.2 %all-to-all-start.2 = ((bf16[4,16,2,64,256]{4,3,2,1,0:T(8,128)(2,1)}), bf16[4,16,2,64,256]{4,3,2,1,0:T(8,128)(2,1)}, u32[]{:S(2)}, u32[]{:S(2)}) async-start(bf16[4,16,2,64,256]{4,3,2,1,0:T(8,128)(2,1)} %multiply_convert_fusion), calls=%async_computation.2 | async-start | bytes 8388608 | tf_op jit(solution)/shard_map/all_to_all | solution.py:124
  139.4 4.2 %copy-start.6 = (bf16[4,96,2,256]{3,2,1,0:T(2,128)(2,1)}, bf16[4,96,2,256]{3,2,1,0:T(2,128)(2,1)S(1)}, u32[]{:S(2)}) copy-start(bf16[4,96,2,256]{3,2,1,0:T(2,128)(2,1)S(1)} %reshape.214) | copy-start | bytes 1179652
  143.9 1.0 slice-start
  145.8 1.3 copy-start.4
  165.5 3.4 %copy-start.7 = (f32[128,2048]{1,0:T(8,128)S(1)}, f32[128,2048]{1,0:T(8,128)}, u32[]{:S(2)}) copy-start(f32[128,2048]{1,0:T(8,128)} %get-tuple-element.5) | copy-start | bytes 3145732
  186.7 1.0 copy-start.2
  189.1 5.1 %copy-start.1 = (bf16[48,2,64,256]{3,2,1,0:T(8,128)(2,1)S(1)}, bf16[48,2,64,256]{3,2,1,0:T(8,128)(2,1)}, u32[]{:S(2)}) copy-start(bf16[48,2,64,256]{3,2,1,0:T(8,128)(2,1)} %param.15) | copy-start | bytes 9437188

commit v3 on v2

--- a/solution.py
+++ b/solution.py
@@ -79,6 +79,73 @@
     )(key_rank, queries, keys, vals)
 
 
+def shift_pairs(shards, step):
+    chips = shards // 2
+    return [(i, ((i // 2 + step) % chips) * 2 + i % 2) for i in range(shards)]
+
+
+def core_pairs(shards):
+    return [(i, i ^ 1) for i in range(shards)]
+
+
+def pick_core(pair, core):
+    return jnp.take(pair, jnp.arange(2) ^ core, axis=1)
+
+
+def hier_reduce_gather(partials, shards, own_index):
+    chips = shards // 2
+    core = own_index % 2
+    chip = own_index // 2
+    by_core = partials.reshape(chips, 2, -1)
+    mine = lax.dynamic_index_in_dim(by_core, core, 1, keepdims=False)
+    other = lax.dynamic_index_in_dim(by_core, 1 - core, 1, keepdims=False)
+    chip_sum = mine + lax.ppermute(other, "ctx", core_pairs(shards))
+    total = lax.dynamic_index_in_dim(chip_sum, chip, 0, keepdims=False)
+    for step in range(1, chips):
+        send = lax.dynamic_index_in_dim(chip_sum, (chip + step) % chips, 0, keepdims=False)
+        total = total + lax.ppermute(send, "ctx", shift_pairs(shards, step))
+    rounded = total.astype(jnp.bfloat16)
+    got = [rounded] + [
+        lax.ppermute(rounded, "ctx", shift_pairs(shards, step)) for step in range(1, chips)
+    ]
+    by_shift = jnp.stack(got)
+    by_chip = jnp.take(by_shift, (chip - jnp.arange(chips)) % chips, axis=0)
+    pair = jnp.stack([by_chip, lax.ppermute(by_chip, "ctx", core_pairs(shards))], axis=1)
+    return pick_core(pair, core).reshape(shards, -1)
+
+
+def merge(parts, sums_width):
+    sums = [p[..., :sums_width] for p in parts]
+    maxes = [p[..., sums_width:sums_width + (p.shape[-1] - sums_width) // 2] for p in parts]
+    totals = [p[..., sums_width + (p.shape[-1] - sums_width) // 2:] for p in parts]
+    best = maxes[0]
+    for m in maxes[1:]:
+        best = jnp.maximum(best, m)
+    factors = [jnp.exp(m - best) for m in maxes]
+    heads = best.shape[-1]
+    lead = sums[0].shape[:-1]
+    out_sum = sum(
+        s.reshape(lead + (heads, HD)) * f[..., None] for s, f in zip(sums, factors)
+    ).reshape(lead + (sums_width,))
+    out_total = sum(t * f for t, f in zip(totals, factors))
+    return jnp.concatenate([out_sum, best, out_total], axis=-1)
+
+
+def hier_combine(sent, shards, own_index, sums_width):
+    chips = shards // 2
+    core = own_index % 2
+    chip = own_index // 2
+    by_core = sent.reshape((chips, 2) + sent.shape[1:])
+    mine = lax.dynamic_index_in_dim(by_core, core, 1, keepdims=False)
+    other = lax.dynamic_index_in_dim(by_core, 1 - core, 1, keepdims=False)
+    chip_merged = merge([mine, lax.ppermute(other, "ctx", core_pairs(shards))], sums_width)
+    parts = [lax.dynamic_index_in_dim(chip_merged, chip, 0, keepdims=False)]
+    for step in range(1, chips):
+        send = lax.dynamic_index_in_dim(chip_merged, (chip + step) % chips, 0, keepdims=False)
+        parts.append(lax.ppermute(send, "ctx", shift_pairs(shards, step)))
+    return merge(parts, sums_width)
+
+
 def body(
     question_hidden,
     recomp_hidden,
@@ -139,10 +206,8 @@
         [query_part.reshape(shards, q_size), kv_part.reshape(shards, row_count * 2 * kv_width)],
         axis=1,
     )
-    summed = jnp.sum(
-        lax.all_to_all(partials, "ctx", split_axis=0, concat_axis=0, tiled=True), axis=0
-    ).astype(jnp.bfloat16)
-    gathered = lax.all_gather(summed, "ctx", axis=0, tiled=False)
+    gathered = hier_reduce_gather(partials, shards, own_index)
+    summed = lax.dynamic_index_in_dim(gathered, own_index, 0, keepdims=False)
     every_query = gathered[:, :q_size].reshape(shards * q_rows, q_width)
     every_kv = gathered[:, q_size:].reshape(shards, row_count, 2, kv_width)
     question_kv = summed[q_size:].reshape(row_count, 2, kv_width)[:q_rows]
@@ -181,16 +246,9 @@
         [part_sums.reshape(shards, q_rows, q_width), by_token(part_max), by_token(part_total)],
         axis=2,
     )
-    got = lax.all_to_all(sent, "ctx", split_axis=0, concat_axis=0, tiled=True)
-    got_sums = got[:, :, :q_width]
-    got_max = got[:, :, q_width : q_width + heads]
-    got_total = got[:, :, q_width + heads :]
-    best_max = jnp.max(got_max, axis=0)
-    factor = jnp.exp(got_max - best_max[None])
-    row_total = jnp.sum(got_total * factor, axis=0)
-    weighted = jnp.sum(
-        got_sums.reshape(shards, q_rows, heads, HD) * factor[..., None], axis=0
-    )
+    got = hier_combine(sent, shards, own_index, q_width)
+    weighted = got[:, :q_width].reshape(q_rows, heads, HD)
+    row_total = got[:, q_width + heads :]
     attended = (weighted / row_total[..., None]).reshape(q_rows, q_width).astype(jnp.bfloat16)
     return (attended, kv_cache)
 

time: 195 us -> 185 us (0.949)
  blocking collectives: 67 us -> 0 us
  waiting for transfers between devices: 28.2 us -> 80.5 us
  local copies, waits for them, and re-layouts: 31.6 us -> 39.2 us
    ppermute x0 -> x6, waiting for transfers between devices: none -> 69.1 us  [the longest x1 53.9 us: hier_reduce_gather(): total = total + lax.ppermute(send, 'ctx', shift_pairs(shards, step))]
    all_gather x1 -> x0, blocking collectives: 49.4 us -> none  [body(): gathered = lax.all_gather(summed, 'ctx', axis=0, tiled=False)]
    all_to_all x1 -> x0, blocking collectives: 17.5 us -> none  [body(): got = lax.all_to_all(sent, 'ctx', split_axis=0, concat_axis=0, tiled=True)]
    all_to_all x1 -> x0, waiting for transfers between devices: 12.8 us -> none  [body(): lax.all_to_all(partials, 'ctx', split_axis=0, concat_axis=0, tiled=True)]
    reshape x4 -> x0, local copies, waits for them, and re-layouts: 5.69 us -> none  [the longest x1 2.93 us: body(): query_part.reshape(shards, q_size)]
    reduce_sum x3 -> x0, other arithmetic: 4.98 us -> none  [the longest x1 3.21 us: body(): jnp.sum(lax.all_to_all(partials, 'ctx', split_axis=0, concat_axis=0, tile...]
    concatenate x0 -> x4, local copies, waits for them, and re-layouts: none -> 4.91 us  [the longest x3 2.84 us: body(): jnp.concatenate([query_part.reshape(shards, q_size), kv_part.reshape(shar...]
    gather x0 -> x4, local copies, waits for them, and re-layouts: none -> 4.83 us  [the longest x3 3.69 us: pick_core(): return jnp.take(pair, jnp.arange(2) ^ core, axis=1)]
  transfers between devices with their start and end apart: 3 -> 8, of which waited for: 2 -> 5; matrix products, arithmetic and copies ran while one was open for 11% -> 14% of each run, Pallas kernels for 0% -> 0%
where the time goes in v3:
time: 185 us; the launch traced here: 184 us
  waiting for transfers between devices  80.5 us (44%)
  local copies, waits for them, and re-layouts  39.2 us (21%)
  other arithmetic  24.5 us (13%)
  Pallas kernels  16.2 us (9%)
  starting transfers between devices  13.5 us (7%)
  matrix products  8.85 us (5%)
    ppermute x1, waiting for transfers between devices, hier_reduce_gather(): total = total + lax.ppermute(send, 'ctx', shift_pairs(shards, step))  53.9 us
    pallas_call x1, Pallas kernels, attend(): pl.pallas_call(functools.partial(attn_kernel, score_scale=score_scale, ct...  16.2 us
    all_to_all x1, waiting for transfers between devices, body(): lax.all_to_all(normed, 'ctx', split_axis=1, concat_axis=0, tiled=True)  11.4 us
    ppermute x1, waiting for transfers between devices, hier_combine(): parts.append(lax.ppermute(send, 'ctx', shift_pairs(shards, step)))  8.1 us
    unnamed x34, local copies, waits for them, and re-layouts  7.55 us
    ppermute x1, waiting for transfers between devices, hier_reduce_gather(): lax.ppermute(rounded, 'ctx', shift_pairs(shards, step))  5.5 us
    all_to_all x1, starting transfers between devices, body(): lax.all_to_all(send_blocks, 'ctx', split_axis=0, concat_axis=0, tiled=True)  5.15 us
    dot_general x1, matrix products, body(): jnp.dot(question_part, w_query, preferred_element_type=jnp.float32)  4.64 us
  transfers between devices with their start and end apart: 8, of which 5 were waited for; matrix products, arithmetic and copies ran while one was open for 14% of the time, Pallas kernels for 0%

profile of v3, /device:TPU:0, one launch (start us, length us, event | category | flops | bytes accessed | tf_op | source)
XLA Modules:
  0.0 184.0 jit_solution(4806589940569655584)
XLA Ops:
  2.1 1.5 fusion.2
  7.3 4.5 %all-to-all-start = ((bf16[96,4,2048]{2,0,1:T(8,128)(2,1)}), bf16[96,4,2048]{2,0,1:T(8,128)(2,1)}, u32[]{:S(2)}, u32[]{:S(2)}) async-start(bf16[96,4,2048]{2,0,1:T(8,128)(2,1)} %bitcast.97), calls=%async_computation | async-start | bytes 3145728 | tf_op jit(solution)/shard_map/all_to_all | solution.py:196
  15.1 3.4 %copy.71 = bf16[256,8,2,256]{3,1,2,0:T(8,128)(2,1)} copy(bf16[256,8,2,256]{3,2,1,0:T(2,128)(2,1)} %bitcast.101) | data formatting | bytes 4194304
  18.4 2.7 %gather_fusion.2 = bf16[64,2,64,256]{3,2,1,0:T(8,128)(2,1)} fusion(bf16[48,2,64,256]{3,2,1,0:T(8,128)(2,1)S(1)} %copy-done, s32[1024]{0:T(1024)S(1)} %pad_clamp_fusion.1), kind=kCustom, calls=%fused_computation.2 | custom fusion | bytes 8388864 | tf_op jit(solution)/shard_map/jit(_take)/gather | solution.py:185
  21.2 11.4 %all-to-all-done = bf16[96,4,2048]{2,0,1:T(8,128)(2,1)} async-done(((bf16[96,4,2048]{2,0,1:T(8,128)(2,1)}), bf16[96,4,2048]{2,0,1:T(8,128)(2,1)}, u32[]{:S(2)}, u32[]{:S(2)}) %all-to-all-start) | async-done | bytes 1572896 | tf_op jit(solution)/shard_map/all_to_all | solution.py:196
  33.7 4.6 %fusion.33 = f32[128,2048]{1,0:T(8,128)S(1)} fusion(bf16[128,2048]{1,0:T(8,128)(2,1)S(1)} %bitcast.100, bf16[2048,2048]{1,0:T(8,128)(2,1)} %param.13), kind=kOutput, calls=%fused_computation.119 | convolution fusion | flops 1073741824 | bytes 9961472 | tf_op jit(solution)/shard_map/dot_general | solution.py:201
  39.4 1.5 copy-done.7
  40.9 3.3 %fusion.34 = f32[384,512]{1,0:T(8,128)} fusion(bf16[384,2048]{1,0:T(8,128)(2,1)} %bitcast.2, bf16[2048,512]{1,0:T(8,128)(2,1)S(1)} %bitcast.103), kind=kOutput, calls=%fused_computation.120 | convolution fusion | flops 805306368 | bytes 4456448 | tf_op jit(solution)/shard_map/dot_general | solution.py:202
  44.2 1.8 concatenate.32
  46.1 2.5 %constant_dynamic-slice_fusion.5 = (f32[2,1,114688]{2,1,0:T(1,128)}, f32[2,1,114688]{2,1,0:T(1,128)S(1)}) fusion(f32[2,2,114688]{2,1,0:T(2,128)S(1)} %constant_dynamic-update-slice_fusion, s32[]{:T(128)S(6)} %select_n.185, s32[]{:T(128)S(6)} %select_n.186), kind=kLoop, calls=%fused_computation.93 | loop fusion | bytes 3670024 | tf_op jit(solution)/shard_map/jit(dynamic_index_in_dim)/dynamic_slice | solution.py:100
  49.4 3.9 %multiply_convert_fusion = bf16[4,16,2,64,256]{4,3,2,1,0:T(8,128)(2,1)} fusion(f32[4,16,2,256]{3,2,1,0:T(2,128)S(1)} %mul.145, bf16[4,16,2,64,256]{4,3,2,1,0:T(8,128)(2,1)S(1)} %bitcast.96, pred[4,16]{1,0:T(4,128)(4,1)S(1)} %compare_and_fusion.1), kind=kLoop, calls=%fused_computation.5 | loop fusion | flops 8388608 | bytes 8519744 | tf_op jit(solution)/shard_map/convert_element_type | solution.py:190
  53.4 5.1 %all-to-all-start.1 = ((bf16[4,16,2,64,256]{4,3,2,1,0:T(8,128)(2,1)}), bf16[4,16,2,64,256]{4,3,2,1,0:T(8,128)(2,1)}, u32[]{:S(2)}, u32[]{:S(2)}) async-start(bf16[4,16,2,64,256]{4,3,2,1,0:T(8,128)(2,1)} %multiply_convert_fusion), calls=%async_computation.1 | async-start | bytes 8388608 | tf_op jit(solution)/shard_map/all_to_all | solution.py:191
  60.4 1.8 collective-permute-start.1
  62.4 53.9 %collective-permute-done.1 = f32[114688]{0:T(1024)S(1)} collective-permute-done((f32[114688]{0:T(1024)S(1)}, f32[114688]{0:T(1024)S(1)}, u32[]{:S(2)}, u32[]{:S(2)}) %collective-permute-start.1) | collective-permute-done | bytes 458784 | tf_op jit(solution)/shard_map/ppermute | solution.py:106
  117.9 5.5 %collective-permute-done.2 = bf16[114688]{0:T(1024)(128)(2,1)S(1)} collective-permute-done((bf16[114688]{0:T(1024)(128)(2,1)S(1)}, bf16[114688]{0:T(1024)(128)(2,1)S(1)}, u32[]{:S(2)}, u32[]{:S(2)}) %collective-permute-start.2) | collective-permute-done | bytes 229408 | tf_op jit(solution)/shard_map/ppermute | solution.py:109
  127.6 2.9 %gather_fusion.4 = bf16[32,2,64,256]{3,2,1,0:T(8,128)(2,1)S(1)} fusion(bf16[64,2,64,256]{3,2,1,0:T(8,128)(2,1)} %bitcast.16, s32[1024]{0:T(1024)S(1)} %get-tuple-element.31), kind=kCustom, calls=%fused_computation.4 | custom fusion | bytes 4194432 | tf_op jit(solution)/shard_map/jit(_take)/gather | solution.py:219
  133.5 2.4 %gather_fusion.1 = bf16[2,2,114688]{2,1,0:T(2,128)(2,1)S(1)} fusion(bf16[2,2,114688]{2,0,1:T(2,128)(2,1)S(1)} %pad_maximum_fusion.3, s32[1024]{0:T(1024)S(1)} %get-tuple-element.32), kind=kCustom, calls=%fused_computation.1 | custom fusion | bytes 1835016 | tf_op jit(solution)/shard_map/jit(_take)/gather | solution.py:92
  139.4 2.3 %reshape.309.q_ref = bf16[128,2048]{1,0:T(8,128)(2,1)} reshape(bf16[4,65536]{1,0:T(4,128)(2,1)} %slice.102) | data formatting | bytes 1048576 | tf_op jit(solution)/shard_map/reshape | solution.py:211
  146.8 16.2 %shard_map.113 = (f32[128,2048]{1,0:T(8,128)}, f32[16,128,1]{2,1,0:T(8,128)}, f32[16,128,1]{2,1,0:T(8,128)}) custom-call(s32[1,32]{1,0:T(1,128)} %iota_add_fusion.rank_ref, bf16[128,2048]{1,0:T(8,128)(2,1)} %reshape.309.q_ref, bf16[2080,256]{1,0:T(8,128)(2,1)} %pad_maximum_fusion.1.k_ref, bf16[2080,256]{1,0:T(8,128)(2,1)} %pad_maximum_fusion.2.v_ref), custom_call_target="tpu_custom_call" | custom-call | tf_op jit(solution)/shard_map/pallas_call | solution.py:60
  162.9 1.7 reduce.2
  164.6 1.6 reduce.3
  167.3 1.6 collective-permute-done.4
  170.4 2.1 %concatenate.40 = f32[2,32,2080]{2,1,0:T(8,128)} concatenate(f32[2,32,2048]{2,1,0:T(8,128)} %fusion.12, f32[2,32,16]{2,1,0:T(8,128)S(1)} %get-tuple-element.14, f32[2,32,16]{2,1,0:T(8,128)S(1)} %get-tuple-element.11), dimensions={2} | concatenate | bytes 1064960 | tf_op jit(solution)/shard_map/concatenate | solution.py:131
  174.5 8.1 %collective-permute-done.5 = f32[32,2080]{1,0:T(8,128)S(1)} collective-permute-done((f32[32,2080]{1,0:T(8,128)S(1)}, f32[32,2080]{1,0:T(8,128)S(1)}, u32[]{:S(2)}, u32[]{:S(2)}) %collective-permute-start.5) | collective-permute-done | bytes 266272 | tf_op jit(solution)/shard_map/ppermute | solution.py:145
  (122 shorter events, 36.4 us)
Async XLA Ops:
  0.6 17.8 %copy-start = (bf16[48,2,64,256]{3,2,1,0:T(8,128)(2,1)S(1)}, bf16[48,2,64,256]{3,2,1,0:T(8,128)(2,1)}, u32[]{:S(2)}) copy-start(bf16[48,2,64,256]{3,2,1,0:T(8,128)(2,1)} %param.15) | copy-start | bytes 9437188
  0.6 5.0 %copy-start.3 = (bf16[64,8192]{1,0:T(8,128)(2,1)S(1)}, bf16[64,8192]{1,0:T(8,128)(2,1)}, u32[]{:S(2)}) copy-start(bf16[64,8192]{1,0:T(8,128)(2,1)} %param.11) | copy-start | bytes 3145732
  7.3 5.0 %copy-start.12 = (s32[128,1]{0,1:T(1,128)S(1)}, s32[128,1]{0,1:T(1,128)}, u32[]{:S(2)}) copy-start(s32[128,1]{0,1:T(1,128)} %param.17) | copy-start | bytes 1540
  7.3 6.0 %copy-start.11 = (s32[128]{0:T(128)S(1)}, s32[128]{0:T(128)}, u32[]{:S(2)}) copy-start(s32[128]{0:T(128)} %param.18) | copy-start | bytes 1540
  7.3 6.4 %copy-start.9 = (bf16[48,2,2]{0,2,1:T(2,128)(2,1)S(1)}, bf16[48,2,2]{0,2,1:T(2,128)(2,1)}, u32[]{:S(2)}) copy-start(bf16[48,2,2]{0,2,1:T(2,128)(2,1)} %param.16) | copy-start | bytes 1156
  7.3 25.3 %all-to-all-start = ((bf16[96,4,2048]{2,0,1:T(8,128)(2,1)}), bf16[96,4,2048]{2,0,1:T(8,128)(2,1)}, u32[]{:S(2)}, u32[]{:S(2)}) async-start(bf16[96,4,2048]{2,0,1:T(8,128)(2,1)} %bitcast.97), calls=%async_computation | async-start | bytes 3145728 | tf_op jit(solution)/shard_map/all_to_all | solution.py:196
  39.3 1.6 copy-start.7
  46.1 3.3 %copy-start.2 = (bf16[64,2,64,256]{3,2,1,0:T(8,128)(2,1)S(1)}, bf16[64,2,64,256]{3,2,1,0:T(8,128)(2,1)}, u32[]{:S(2)}) copy-start(bf16[64,2,64,256]{3,2,1,0:T(8,128)(2,1)} %gather_fusion.2) | copy-start | bytes 12582916
  49.3 9.3 %collective-permute-start = (f32[2,114688]{1,0:T(2,128)S(1)}, f32[2,114688]{1,0:T(2,128)S(1)}, u32[]{:S(2)}, u32[]{:S(2)}) collective-permute-start(f32[2,114688]{1,0:T(2,128)S(1)} %bitcast.109), channel_id=1, source_target_pairs={{0,4},{4,0},{8,12},{12,8},{1,5},{5,1},{9,13},{13,9},{2,6},{6,2},{1... | collective-permute-start | bytes 2752520 | tf_op jit(solution)/shard_map/ppermute | solution.py:102
  53.4 5.3 %copy-start.4 = (f32[2,1,114688]{2,1,0:T(1,128)S(1)}, f32[2,1,114688]{2,1,0:T(1,128)}, u32[]{:S(2)}) copy-start(f32[2,1,114688]{2,1,0:T(1,128)} %get-tuple-element.19) | copy-start | bytes 2752516
  53.4 74.2 %all-to-all-start.1 = ((bf16[4,16,2,64,256]{4,3,2,1,0:T(8,128)(2,1)}), bf16[4,16,2,64,256]{4,3,2,1,0:T(8,128)(2,1)}, u32[]{:S(2)}, u32[]{:S(2)}) async-start(bf16[4,16,2,64,256]{4,3,2,1,0:T(8,128)(2,1)} %multiply_convert_fusion), calls=%async_computation.1 | async-start | bytes 8388608 | tf_op jit(solution)/shard_map/all_to_all | solution.py:191
  58.6 3.7 %copy-start.10 = (s32[256]{0:T(256)S(1)}, s32[256]{0:T(256)}, u32[]{:S(2)}) copy-start(s32[256]{0:T(256)} %param.19) | copy-start | bytes 3076
  60.4 55.9 %collective-permute-start.1 = (f32[114688]{0:T(1024)S(1)}, f32[114688]{0:T(1024)S(1)}, u32[]{:S(2)}, u32[]{:S(2)}) collective-permute-start(f32[114688]{0:T(1024)S(1)} %bitcast.111), channel_id=1, source_target_pairs={{0,8},{4,12},{8,0},{12,4},{1,9},{5,13},{9,1},{13,5},{2,10},{6,14},... | collective-permute-start | bytes 1376264 | tf_op jit(solution)/shard_map/ppermute | solution.py:106
  116.3 7.1 %collective-permute-start.2 = (bf16[114688]{0:T(1024)(128)(2,1)S(1)}, bf16[114688]{0:T(1024)(128)(2,1)S(1)}, u32[]{:S(2)}, u32[]{:S(2)}) collective-permute-start(bf16[114688]{0:T(1024)(128)(2,1)S(1)} %add_convert_fusion), channel_id=1, source_target_pairs={{0,8},{4,12},{8,0},{12,4},{1,9},{5,13},{9,1},{13,5},{2,10},{6,14},... | collective-permute-start | bytes 688136 | tf_op jit(solution)/shard_map/ppermute | solution.py:109
  127.1 5.1 %collective-permute-start.3 = (bf16[2,114688]{1,0:T(2,128)(2,1)}, bf16[2,114688]{1,0:T(2,128)(2,1)S(1)}, u32[]{:S(2)}, u32[]{:S(2)}) collective-permute-start(bf16[2,114688]{1,0:T(2,128)(2,1)} %broadcast_select_fusion.1), channel_id=1, source_target_pairs={{0,4},{4,0},{8,12},{12,8},{1,5},{5,1},{9,13},{13,9},{2,6},{6,2},{1... | collective-permute-start | bytes 1376264 | tf_op jit(solution)/shard_map/ppermute | solution.py:113
  137.9 4.5 %copy-start.6 = (bf16[2,32,64,256]{3,2,1,0:T(8,128)(2,1)S(1)}, bf16[2,32,64,256]{3,2,1,0:T(8,128)(2,1)}, u32[]{:S(2)}) copy-start(bf16[2,32,64,256]{3,2,1,0:T(8,128)(2,1)} %copy.56) | copy-start | bytes 6291460
  143.3 1.3 copy-start.5
  162.9 3.4 %copy-start.8 = (f32[128,2048]{1,0:T(8,128)S(1)}, f32[128,2048]{1,0:T(8,128)}, u32[]{:S(2)}) copy-start(f32[128,2048]{1,0:T(8,128)} %get-tuple-element.5) | copy-start | bytes 3145732
  166.7 2.2 %collective-permute-start.4 = (f32[2,32,2080]{2,1,0:T(8,128)S(1)}, f32[2,32,2080]{2,1,0:T(8,128)S(1)}, u32[]{:S(2)}, u32[]{:S(2)}) collective-permute-start(f32[2,32,2080]{2,1,0:T(8,128)S(1)} %get-tuple-element.22), channel_id=1, source_target_pairs={{0,4},{4,0},{8,12},{12,8},{1,5},{5,1},{9,13},{13,9},{2,6},{6,2},{1... | collective-permute-start | bytes 1597448 | tf_op jit(solution)/shard_map/ppermute | solution.py:141
  170.4 13.5 %copy-start.1 = (bf16[48,2,64,256]{3,2,1,0:T(8,128)(2,1)S(1)}, bf16[48,2,64,256]{3,2,1,0:T(8,128)(2,1)}, u32[]{:S(2)}) copy-start(bf16[48,2,64,256]{3,2,1,0:T(8,128)(2,1)} %param.15) | copy-start | bytes 9437188
  173.6 9.0 %collective-permute-start.5 = (f32[32,2080]{1,0:T(8,128)S(1)}, f32[32,2080]{1,0:T(8,128)S(1)}, u32[]{:S(2)}, u32[]{:S(2)}) collective-permute-start(f32[32,2080]{1,0:T(8,128)S(1)} %get-tuple-element.26), channel_id=1, source_target_pairs={{0,8},{4,12},{8,0},{12,4},{1,9},{5,13},{9,1},{13,5},{2,10},{6,14},... | collective-permute-start | bytes 798728 | tf_op jit(solution)/shard_map/ppermute | solution.py:145

commit v4 on v3

--- a/solution.py
+++ b/solution.py
@@ -19,17 +19,20 @@
     return (floats * factor * norm_gain.astype(jnp.float32)).astype(jnp.bfloat16)
 
 
-def attn_kernel(rank_ref, q_ref, k_ref, v_ref, o_ref, m_ref, l_ref, *, score_scale, ctx_keys):
+def attn_kernel(
+    bias_ref, rank_ref, q_ref, kc_ref, kq_ref, vc_ref, vq_ref, o_ref, m_ref, l_ref, *, score_scale
+):
     tq = q_ref.shape[0]
     first = pl.program_id(0) * tq
     dims = (((1,), (1,)), ((), ()))
     queries = q_ref[...]
     ctx_scores = (
-        lax.dot_general(queries, k_ref[:ctx_keys, :], dims, preferred_element_type=jnp.float32)
+        lax.dot_general(queries, kc_ref[...], dims, preferred_element_type=jnp.float32)
         * score_scale
+        + bias_ref[...]
     )
     own_scores = (
-        lax.dot_general(queries, k_ref[ctx_keys:, :], dims, preferred_element_type=jnp.float32)
+        lax.dot_general(queries, kq_ref[...], dims, preferred_element_type=jnp.float32)
         * score_scale
     )
     token = first + lax.broadcasted_iota(jnp.int32, own_scores.shape, 0)
@@ -45,26 +48,28 @@
         own_weights, axis=1, keepdims=True
     )
     o_ref[...] = jnp.dot(
-        ctx_weights.astype(jnp.bfloat16), v_ref[:ctx_keys, :], preferred_element_type=jnp.float32
-    ) + jnp.dot(
-        own_weights.astype(jnp.bfloat16), v_ref[ctx_keys:, :], preferred_element_type=jnp.float32
-    )
-
-
-def attend(queries, keys, vals, key_rank, ctx_keys, group_size, score_scale):
+        ctx_weights.astype(jnp.bfloat16), vc_ref[...], preferred_element_type=jnp.float32
+    ) + jnp.dot(own_weights.astype(jnp.bfloat16), vq_ref[...], preferred_element_type=jnp.float32)
+
+
+def attend(queries, ctx_keys, own_keys, ctx_vals, own_vals, ctx_bias, key_rank, group_size, score_scale):
     tokens, q_width = queries.shape
-    key_count = keys.shape[0]
+    ctx_count = ctx_keys.shape[0]
+    own_count = own_keys.shape[0]
     heads = q_width // HD
     tq = min(tokens, 128)
     grid = (tokens // tq, heads)
     return pl.pallas_call(
-        functools.partial(attn_kernel, score_scale=score_scale, ctx_keys=ctx_keys),
+        functools.partial(attn_kernel, score_scale=score_scale),
         grid=grid,
         in_specs=[
-            pl.BlockSpec((1, key_count - ctx_keys), lambda i, n: (0, 0)),
+            pl.BlockSpec((1, ctx_count), lambda i, n: (0, 0)),
+            pl.BlockSpec((1, own_count), lambda i, n: (0, 0)),
             pl.BlockSpec((tq, HD), lambda i, n: (i, n)),
-            pl.BlockSpec((key_count, HD), lambda i, n: (0, n // group_size)),
-            pl.BlockSpec((key_count, HD), lambda i, n: (0, n // group_size)),
+            pl.BlockSpec((ctx_count, HD), lambda i, n: (0, n // group_size)),
+            pl.BlockSpec((own_count, HD), lambda i, n: (0, n // group_size)),
+            pl.BlockSpec((ctx_count, HD), lambda i, n: (0, n // group_size)),
+            pl.BlockSpec((own_count, HD), lambda i, n: (0, n // group_size)),
         ],
         out_specs=[
             pl.BlockSpec((tq, HD), lambda i, n: (i, n)),
@@ -76,7 +81,7 @@
             jax.ShapeDtypeStruct((heads, tokens, 1), jnp.float32),
             jax.ShapeDtypeStruct((heads, tokens, 1), jnp.float32),
         ],
-    )(key_rank, queries, keys, vals)
+    )(ctx_bias, key_rank, queries, ctx_keys, own_keys, ctx_vals, own_vals)
 
 
 def shift_pairs(shards, step):
@@ -189,6 +194,13 @@
         * send_scales.astype(jnp.float32)[:, :, None, :, None]
     ).astype(jnp.bfloat16).reshape((shards, capacity, 2, block_len, kv_width))
     got_blocks = lax.all_to_all(send_blocks, "ctx", split_axis=0, concat_axis=0, tiled=True)
+    ctx_dev = per_dev * block_len
+    slot_valid = jnp.any(chosen, axis=1)
+    slot_block = jnp.sum(jnp.where(chosen, positions[None, :, None], 0), axis=1)
+    slot_base = jnp.arange(shards)[:, None] * ctx_dev + slot_block * block_len
+    slot_pos = jnp.where(
+        slot_valid[:, :, None], slot_base[:, :, None] + jnp.arange(block_len), -1
+    ).reshape(-1)
 
     normed = jnp.concatenate(
         [rms_rows(question_hidden, norm_gain), rms_rows(recomp_hidden, norm_gain)], axis=0
@@ -219,7 +231,6 @@
     block_rows = jnp.take(
         got_blocks.reshape((shards * capacity, 2, block_len, kv_width)), flat_index, axis=0
     )
-    ctx_dev = per_dev * block_len
     cached = jnp.transpose(block_rows, (1, 0, 2, 3)).reshape(2, ctx_dev, kv_width)
 
     local_pos = recomp_pos - own_index * ctx_dev
@@ -231,12 +242,27 @@
     ).astype(jnp.bfloat16)
     kv_cache = jnp.where(hit[None, :, None], placed, cached)
 
-    key_local = jnp.concatenate([kv_cache[0], question_kv[:, 0]], axis=0)
-    val_local = jnp.concatenate([kv_cache[1], question_kv[:, 1]], axis=0)
+    slot_count = slot_pos.shape[0]
+    own_blocks = jnp.transpose(send_blocks, (2, 0, 1, 3, 4)).reshape(2, slot_count, kv_width)
+    owner_match = recomp_pos[None, :] == slot_pos[:, None]
+    owner_hit = jnp.any(owner_match, axis=1)
+    owner_placed = jnp.einsum(
+        "pi,ick->cpk", owner_match.astype(jnp.bfloat16), recomp_kv, preferred_element_type=jnp.float32
+    ).astype(jnp.bfloat16)
+    owner_kv = jnp.where(owner_hit[None, :, None], owner_placed, own_blocks)
+    ctx_bias = jnp.where(slot_pos >= 0, 0.0, neg_large).astype(jnp.float32)[None, :]
     key_rank = (own_index * q_rows + jnp.arange(q_rows)).astype(jnp.int32)[None, :]
 
     part_sums, part_max, part_total = attend(
-        every_query, key_local, val_local, key_rank, ctx_dev, group_size, score_scale
+        every_query,
+        owner_kv[0],
+        question_kv[:, 0],
+        owner_kv[1],
+        question_kv[:, 1],
+        ctx_bias,
+        key_rank,
+        group_size,
+        score_scale,
     )
 
     def by_token(value):

time: 185 us -> 182 us (0.984)
  waiting for transfers between devices: 80.5 us -> 36.1 us
  local copies, waits for them, and re-layouts: 39.2 us -> 56 us
  matrix products: 8.85 us -> 17.7 us
  Pallas kernels: 16.2 us -> 24.4 us
  other arithmetic: 24.5 us -> 32.6 us
    ppermute x1, waiting for transfers between devices: 53.9 us -> 25.2 us  [hier_reduce_gather(): total = total + lax.ppermute(send, 'ctx', shift_pairs(shards, step))]
    pallas_call x1, Pallas kernels: 16.2 us -> 24.4 us  [attend(): pl.pallas_call(functools.partial(attn_kernel, score_scale=score_scale), g...]
    ppermute x1, waiting for transfers between devices: 8.1 us -> 0.86 us  [hier_combine(): parts.append(lax.ppermute(send, 'ctx', shift_pairs(shards, step)))]
    all_to_all x1, waiting for transfers between devices: 11.4 us -> 4.29 us  [body(): lax.all_to_all(normed, 'ctx', split_axis=1, concat_axis=0, tiled=True)]
    transpose x0 -> x1, other arithmetic: none -> 6.23 us  [body(): jnp.transpose(send_blocks, (2, 0, 1, 3, 4)).reshape(2, slot_count, kv_width)]
    dot_general x0 -> x1, matrix products: none -> 6.04 us  [body(): jnp.einsum('pi,ick->cpk', owner_match.astype(jnp.bfloat16), recomp_kv, pr...]
    transpose x0 -> x1, local copies, waits for them, and re-layouts: none -> 4.76 us  [body(): jnp.transpose(send_blocks, (2, 0, 1, 3, 4)).reshape(2, slot_count, kv_width)]
    all_to_all x0 -> x1, local copies, waits for them, and re-layouts: none -> 4.75 us  [body(): lax.all_to_all(send_blocks, 'ctx', split_axis=0, concat_axis=0, tiled=True)]
  transfers between devices with their start and end apart: 8 -> 8, of which waited for: 5 -> 5; matrix products, arithmetic and copies ran while one was open for 14% -> 51% of each run, Pallas kernels for 0% -> 14%
where the time goes in v4:
time: 182 us; the launch traced here: 181 us
  local copies, waits for them, and re-layouts  56 us (31%)
  waiting for transfers between devices  36.1 us (20%)
  other arithmetic  32.6 us (18%)
  Pallas kernels  24.4 us (13%)
  matrix products  17.7 us (10%)
  starting transfers between devices  12.8 us (7%)
    ppermute x1, waiting for transfers between devices, hier_reduce_gather(): total = total + lax.ppermute(send, 'ctx', shift_pairs(shards, step))  25.2 us
    pallas_call x1, Pallas kernels, attend(): pl.pallas_call(functools.partial(attn_kernel, score_scale=score_scale), g...  24.4 us
    unnamed x29, local copies, waits for them, and re-layouts  11.6 us
    transpose x1, other arithmetic, body(): jnp.transpose(send_blocks, (2, 0, 1, 3, 4)).reshape(2, slot_count, kv_width)  6.23 us
    dot_general x1, matrix products, body(): jnp.einsum('pi,ick->cpk', owner_match.astype(jnp.bfloat16), recomp_kv, pr...  6.04 us
    all_to_all x1, starting transfers between devices, body(): lax.all_to_all(send_blocks, 'ctx', split_axis=0, concat_axis=0, tiled=True)  5.04 us
    transpose x1, local copies, waits for them, and re-layouts, body(): jnp.transpose(send_blocks, (2, 0, 1, 3, 4)).reshape(2, slot_count, kv_width)  4.76 us
    all_to_all x1, local copies, waits for them, and re-layouts, body(): lax.all_to_all(send_blocks, 'ctx', split_axis=0, concat_axis=0, tiled=True)  4.75 us
  transfers between devices with their start and end apart: 8, of which 5 were waited for; matrix products, arithmetic and copies ran while one was open for 51% of the time, Pallas kernels for 14%

profile of v4, /device:TPU:0, one launch (start us, length us, event | category | flops | bytes accessed | tf_op | source)
XLA Modules:
  0.0 180.8 jit_solution(4836309270498432616)
XLA Ops:
  7.3 4.5 %all-to-all-start = ((bf16[96,4,2048]{2,0,1:T(8,128)(2,1)}), bf16[96,4,2048]{2,0,1:T(8,128)(2,1)}, u32[]{:S(2)}, u32[]{:S(2)}) async-start(bf16[96,4,2048]{2,0,1:T(8,128)(2,1)} %bitcast.113), calls=%async_computation | async-start | bytes 3145728 | tf_op jit(solution)/shard_map/all_to_all | solution.py:208
  15.3 3.4 %copy.138 = bf16[256,8,2,256]{3,1,2,0:T(8,128)(2,1)} copy(bf16[256,8,2,256]{3,2,1,0:T(2,128)(2,1)} %bitcast.118) | data formatting | bytes 4194304
  18.7 2.8 %gather_fusion.2 = bf16[64,2,64,256]{3,2,1,0:T(8,128)(2,1)} fusion(bf16[48,2,64,256]{3,2,1,0:T(8,128)(2,1)S(1)} %copy-done, s32[1024]{0:T(1024)S(1)} %pad_clamp_fusion.1), kind=kCustom, calls=%fused_computation.2 | custom fusion | bytes 8388864 | tf_op jit(solution)/shard_map/jit(_take)/gather | solution.py:190
  21.5 4.1 %multiply_convert_fusion = bf16[4,16,2,64,256]{4,3,2,1,0:T(8,128)(2,1)S(1)} fusion(f32[4,16,2,256]{3,2,1,0:T(2,128)S(1)} %copy.115, bf16[4,16,2,64,256]{4,3,2,1,0:T(8,128)(2,1)} %bitcast.109, pred[4,16]{1,0:T(4,128)(4,1)S(1)} %compare_and_fusion.2), kind=kLoop, calls=%fused_computation.5 | loop fusion | flops 8388608 | bytes 8519744 | tf_op jit(solution)/shard_map/convert_element_type | solution.py:195
  25.5 2.5 %copy.122 = bf16[4,16,2,64,256]{4,3,1,2,0:T(8,128)(2,1)} copy(bf16[4,16,2,64,256]{4,3,2,1,0:T(8,128)(2,1)S(1)} %multiply_convert_fusion) | data formatting | bytes 8388608 | tf_op jit(solution)/shard_map/convert_element_type | solution.py:195
  28.3 4.3 %all-to-all-done = bf16[96,4,2048]{2,0,1:T(8,128)(2,1)} async-done(((bf16[96,4,2048]{2,0,1:T(8,128)(2,1)}), bf16[96,4,2048]{2,0,1:T(8,128)(2,1)}, u32[]{:S(2)}, u32[]{:S(2)}) %all-to-all-start) | async-done | bytes 1572896 | tf_op jit(solution)/shard_map/all_to_all | solution.py:208
  32.6 5.0 %all-to-all-start.1 = ((bf16[4,16,2,64,256]{4,3,1,2,0:T(8,128)(2,1)}), bf16[4,16,2,64,256]{4,3,1,2,0:T(8,128)(2,1)}, u32[]{:S(2)}, u32[]{:S(2)}) async-start(bf16[4,16,2,64,256]{4,3,1,2,0:T(8,128)(2,1)} %copy.122), calls=%async_computation.1 | async-start | bytes 8388608 | tf_op jit(solution)/shard_map/all_to_all | solution.py:196
  38.7 4.6 %fusion.38 = f32[128,2048]{1,0:T(8,128)S(1)} fusion(bf16[128,2048]{1,0:T(8,128)(2,1)S(1)} %bitcast.117, bf16[2048,2048]{1,0:T(8,128)(2,1)} %param.13), kind=kOutput, calls=%fused_computation.130 | convolution fusion | flops 1073741824 | bytes 9961472 | tf_op jit(solution)/shard_map/dot_general | solution.py:213
  45.9 3.3 %fusion.39 = f32[384,512]{1,0:T(8,128)} fusion(bf16[384,2048]{1,0:T(8,128)(2,1)} %bitcast.2, bf16[2048,512]{1,0:T(8,128)(2,1)S(1)} %bitcast.119), kind=kOutput, calls=%fused_computation.131 | convolution fusion | flops 805306368 | bytes 4456448 | tf_op jit(solution)/shard_map/dot_general | solution.py:214
  51.1 2.5 %constant_dynamic-slice_fusion.5 = (f32[2,1,114688]{2,1,0:T(1,128)}, f32[2,1,114688]{2,1,0:T(1,128)S(1)}) fusion(f32[2,2,114688]{2,1,0:T(2,128)S(1)} %constant_dynamic-update-slice_fusion, s32[]{:T(128)S(6)} %select_n.231, s32[]{:T(128)S(6)} %select_n.232), kind=kLoop, calls=%fused_computation.100 | loop fusion | bytes 3670024 | tf_op jit(solution)/shard_map/jit(dynamic_index_in_dim)/dynamic_slice | solution.py:105
  54.9 6.2 %fusion.46 = bf16[2,4,16,64,256]{4,3,0,2,1:T(8,128)(2,1)} fusion(f32[4,16,2,256]{3,2,1,0:T(2,128)S(1)} %copy.115, bf16[4,16,2,64,256]{4,3,2,1,0:T(8,128)(2,1)} %bitcast.110, pred[4,16]{1,0:T(4,128)(4,1)S(1)} %compare_and_fusion.2), kind=kLoop, calls=%fused_computation.132 | loop fusion | flops 8388608 | bytes 8519744 | tf_op jit(solution)/shard_map/transpose | solution.py:246
  65.4 4.8 %copy.116 = bf16[2,4,16,64,256]{4,3,2,1,0:T(8,128)(2,1)} copy(bf16[2,4,16,64,256]{4,3,0,2,1:T(8,128)(2,1)} %fusion.46) | data formatting | bytes 8388608 | tf_op jit(solution)/shard_map/transpose | solution.py:246
  70.2 25.2 %collective-permute-done.1 = f32[114688]{0:T(1024)S(1)} collective-permute-done((f32[114688]{0:T(1024)S(1)}, f32[114688]{0:T(1024)S(1)}, u32[]{:S(2)}, u32[]{:S(2)}) %collective-permute-start.1) | collective-permute-done | bytes 458784 | tf_op jit(solution)/shard_map/ppermute | solution.py:111
  98.1 4.4 %collective-permute-done.2 = bf16[114688]{0:T(1024)(128)(2,1)S(1)} collective-permute-done((bf16[114688]{0:T(1024)(128)(2,1)S(1)}, bf16[114688]{0:T(1024)(128)(2,1)S(1)}, u32[]{:S(2)}, u32[]{:S(2)}) %collective-permute-start.2) | collective-permute-done | bytes 229408 | tf_op jit(solution)/shard_map/ppermute | solution.py:114
  108.6 2.4 %gather_fusion.1 = bf16[2,2,114688]{2,1,0:T(2,128)(2,1)S(1)} fusion(bf16[2,2,114688]{2,0,1:T(2,128)(2,1)S(1)} %pad_maximum_fusion.1, s32[1024]{0:T(1024)S(1)} %get-tuple-element.48), kind=kCustom, calls=%fused_computation.1 | custom fusion | bytes 1835016 | tf_op jit(solution)/shard_map/jit(_take)/gather | solution.py:97
  116.5 6.0 %fusion.1 = bf16[2,4096,256]{2,1,0:T(8,128)(2,1)S(1)} fusion(bf16[2,4096,256]{2,1,0:T(8,128)(2,1)} %bitcast.115, bf16[256,2,256]{2,0,1:T(8,128)(2,1)S(1)} %bitcast.130, pred[4096]{0:T(1024)(128)(4,1)S(1)} %compare_reduce_fusion, s32[256]{0:T(256)S(1)} %copy-done.6, s32[4096]{0:T(1024)S(1)} %select_n.242), kind=kOutput, calls=%fused_computation.10 | convolution fusion | flops 1078984704 | bytes 8672256 | tf_op jit(solution)/shard_map/pi,ick->cpk/dot_general | solution.py:249
  122.6 2.4 %slice_bitcast_fusion = (bf16[4096,256]{1,0:T(8,128)(2,1)}, bf16[4096,256]{1,0:T(8,128)(2,1)}) fusion(bf16[2,4096,256]{2,1,0:T(8,128)(2,1)S(1)} %fusion.1), kind=kLoop, calls=%fused_computation.19 | loop fusion | bytes 8388608 | tf_op jit(solution)/shard_map/squeeze | solution.py:260
  124.9 24.4 %shard_map.113 = (f32[128,2048]{1,0:T(8,128)}, f32[16,128,1]{2,1,0:T(8,128)}, f32[16,128,1]{2,1,0:T(8,128)}) custom-call(f32[1,4096]{1,0:T(1,128)} %select_n.225.bias_ref, s32[1,32]{1,0:T(1,128)} %iota_add_fusion.rank_ref, bf16[128,2048]{1,0:T(8,128)(2,1)} %reshape.406.q_ref, bf16[4096,256]{1,0:T(8,128)(2,1)} %get-tuple-element.34.kc_ref, ...), custom_call_target="tpu_custom_call" | custom-call | tf_op jit(solution)/shard_map/pallas_call | solution.py:62
  154.5 4.7 %copy.123 = bf16[4,16,2,64,256]{4,3,2,1,0:T(8,128)(2,1)} copy(bf16[4,16,2,64,256]{4,3,1,2,0:T(8,128)(2,1)} %all-to-all-done.1) | data formatting | bytes 8388608 | tf_op jit(solution)/shard_map/all_to_all | solution.py:196
  159.3 2.9 %gather_fusion.4 = bf16[32,2,64,256]{3,2,1,0:T(8,128)(2,1)S(1)} fusion(bf16[64,2,64,256]{3,2,1,0:T(8,128)(2,1)} %bitcast.111, s32[1024]{0:T(1024)S(1)} %get-tuple-element.47), kind=kCustom, calls=%fused_computation.4 | custom fusion | bytes 4194432 | tf_op jit(solution)/shard_map/jit(_take)/gather | solution.py:231
  162.5 2.4 %copy.125 = bf16[2,2048,256]{1,2,0:T(8,128)(2,1)} copy(bf16[2,2048,256]{2,1,0:T(8,128)(2,1)S(1)} %bitcast.112) | data formatting | bytes 4194304 | tf_op jit(solution)/shard_map/reshape | solution.py:234
  169.0 3.7 %fusion.3 = bf16[2,2048,256]{1,2,0:T(8,128)(2,1)} fusion(bf16[2,2048,256]{1,2,0:T(8,128)(2,1)} %copy.125, bf16[256,2,256]{2,0,1:T(8,128)(2,1)S(1)} %bitcast.131, pred[2048]{0:T(1024)(128)(4,1)S(1)} %fusion.8, s32[256]{0:T(256)S(1)} %broadcast_subtract_fusion), kind=kOutput, calls=%fused_computation.13 | convolution fusion | flops 539492352 | bytes 4459520 | tf_op jit(solution)/shard_map/pi,ick->cpk/dot_general | solution.py:240
  172.8 4.1 %copy.126 = bf16[2,2048,256]{2,1,0:T(8,128)(2,1)} copy(bf16[2,2048,256]{1,2,0:T(8,128)(2,1)} %fusion.3) | data formatting | bytes 4194304
  179.0 1.9 %fusion.17 = bf16[32,2048]{1,0:T(8,128)(2,1)} fusion(f32[4,8,16,128]{3,2,1,0:T(8,128)S(1)} %bitcast.122, f32[4,8,16,128]{3,2,1,0:T(8,128)S(1)} %bitcast.124, f32[4,8,16,128]{3,2,1,0:T(8,128)S(1)} %bitcast.123, f32[32,2080]{1,0:T(8,128)} %collective-permute-done.5, f32[32,2080]{1,0:T(8,128)S(1)} %get-tuple-element.41), kind=kLoop, calls=%fused_computation.51 | loop fusion | flops 327680 | bytes 1441792 | tf_op jit(solution)/shard_map/convert_element_type | solution.py:278
  (132 shorter events, 47.2 us)
Async XLA Ops:
  0.6 18.0 %copy-start = (bf16[48,2,64,256]{3,2,1,0:T(8,128)(2,1)S(1)}, bf16[48,2,64,256]{3,2,1,0:T(8,128)(2,1)}, u32[]{:S(2)}) copy-start(bf16[48,2,64,256]{3,2,1,0:T(8,128)(2,1)} %param.15) | copy-start | bytes 9437188
  0.6 5.0 %copy-start.2 = (bf16[64,8192]{1,0:T(8,128)(2,1)S(1)}, bf16[64,8192]{1,0:T(8,128)(2,1)}, u32[]{:S(2)}) copy-start(bf16[64,8192]{1,0:T(8,128)(2,1)} %param.11) | copy-start | bytes 3145732
  7.3 5.1 %copy-start.9 = (s32[128,1]{0,1:T(1,128)S(1)}, s32[128,1]{0,1:T(1,128)}, u32[]{:S(2)}) copy-start(s32[128,1]{0,1:T(1,128)} %param.17) | copy-start | bytes 1540
  7.3 5.8 %copy-start.8 = (s32[128]{0:T(128)S(1)}, s32[128]{0:T(128)}, u32[]{:S(2)}) copy-start(s32[128]{0:T(128)} %param.18) | copy-start | bytes 1540
  7.3 6.5 %copy-start.7 = (bf16[48,2,2]{0,2,1:T(2,128)(2,1)S(1)}, bf16[48,2,2]{0,2,1:T(2,128)(2,1)}, u32[]{:S(2)}) copy-start(bf16[48,2,2]{0,2,1:T(2,128)(2,1)} %param.16) | copy-start | bytes 1156
  7.3 25.2 %all-to-all-start = ((bf16[96,4,2048]{2,0,1:T(8,128)(2,1)}), bf16[96,4,2048]{2,0,1:T(8,128)(2,1)}, u32[]{:S(2)}, u32[]{:S(2)}) async-start(bf16[96,4,2048]{2,0,1:T(8,128)(2,1)} %bitcast.113), calls=%async_computation | async-start | bytes 3145728 | tf_op jit(solution)/shard_map/all_to_all | solution.py:208
  32.6 122.0 %all-to-all-start.1 = ((bf16[4,16,2,64,256]{4,3,1,2,0:T(8,128)(2,1)}), bf16[4,16,2,64,256]{4,3,1,2,0:T(8,128)(2,1)}, u32[]{:S(2)}, u32[]{:S(2)}) async-start(bf16[4,16,2,64,256]{4,3,1,2,0:T(8,128)(2,1)} %copy.122), calls=%async_computation.1 | async-start | bytes 8388608 | tf_op jit(solution)/shard_map/all_to_all | solution.py:196
  44.3 1.6 copy-start.4
  54.3 6.8 %collective-permute-start = (f32[2,114688]{1,0:T(2,128)S(1)}, f32[2,114688]{1,0:T(2,128)S(1)}, u32[]{:S(2)}, u32[]{:S(2)}) collective-permute-start(f32[2,114688]{1,0:T(2,128)S(1)} %bitcast.125), channel_id=1, source_target_pairs={{0,4},{4,0},{8,12},{12,8},{1,5},{5,1},{9,13},{13,9},{2,6},{6,2},{1... | collective-permute-start | bytes 2752520 | tf_op jit(solution)/shard_map/ppermute | solution.py:107
  54.8 6.2 %copy-start.3 = (f32[2,1,114688]{2,1,0:T(1,128)S(1)}, f32[2,1,114688]{2,1,0:T(1,128)}, u32[]{:S(2)}) copy-start(f32[2,1,114688]{2,1,0:T(1,128)} %get-tuple-element.35) | copy-start | bytes 2752516
  62.8 32.5 %collective-permute-start.1 = (f32[114688]{0:T(1024)S(1)}, f32[114688]{0:T(1024)S(1)}, u32[]{:S(2)}, u32[]{:S(2)}) collective-permute-start(f32[114688]{0:T(1024)S(1)} %bitcast.127), channel_id=1, source_target_pairs={{0,8},{4,12},{8,0},{12,4},{1,9},{5,13},{9,1},{13,5},{2,10},{6,14},... | collective-permute-start | bytes 1376264 | tf_op jit(solution)/shard_map/ppermute | solution.py:111
  65.4 31.0 %copy-start.6 = (s32[256]{0:T(256)S(1)}, s32[256]{0:T(256)}, u32[]{:S(2)}) copy-start(s32[256]{0:T(256)} %param.19) | copy-start | bytes 3076
  95.4 7.1 %collective-permute-start.2 = (bf16[114688]{0:T(1024)(128)(2,1)S(1)}, bf16[114688]{0:T(1024)(128)(2,1)S(1)}, u32[]{:S(2)}, u32[]{:S(2)}) collective-permute-start(bf16[114688]{0:T(1024)(128)(2,1)S(1)} %add_convert_fusion), channel_id=1, source_target_pairs={{0,8},{4,12},{8,0},{12,4},{1,9},{5,13},{9,1},{13,5},{2,10},{6,14},... | collective-permute-start | bytes 688136 | tf_op jit(solution)/shard_map/ppermute | solution.py:114
  105.4 1.9 %collective-permute-start.3 = (bf16[2,114688]{1,0:T(2,128)(2,1)S(1)}, bf16[2,114688]{1,0:T(2,128)(2,1)S(1)}, u32[]{:S(2)}, u32[]{:S(2)}) collective-permute-start(bf16[2,114688]{1,0:T(2,128)(2,1)S(1)} %broadcast_select_fusion.1), channel_id=1, source_target_pairs={{0,4},{4,0},{8,12},{12,8},{1,5},{5,1},{9,13},{13,9},{2,6},{6,2},{1... | collective-permute-start | bytes 1376264 | tf_op jit(solution)/shard_map/ppermute | solution.py:118
  149.4 3.4 %copy-start.5 = (f32[128,2048]{1,0:T(8,128)S(1)}, f32[128,2048]{1,0:T(8,128)}, u32[]{:S(2)}) copy-start(f32[128,2048]{1,0:T(8,128)} %get-tuple-element.5) | copy-start | bytes 3145732
  154.0 10.9 %collective-permute-start.4 = (f32[2,32,2080]{2,1,0:T(8,128)}, f32[2,32,2080]{2,1,0:T(8,128)}, u32[]{:S(2)}, u32[]{:S(2)}) collective-permute-start(f32[2,32,2080]{2,1,0:T(8,128)} %get-tuple-element.38), channel_id=1, source_target_pairs={{0,4},{4,0},{8,12},{12,8},{1,5},{5,1},{9,13},{13,9},{2,6},{6,2},{1... | collective-permute-start | bytes 1597448 | tf_op jit(solution)/shard_map/ppermute | solution.py:146
  168.5 9.2 %collective-permute-start.5 = (f32[32,2080]{1,0:T(8,128)}, f32[32,2080]{1,0:T(8,128)}, u32[]{:S(2)}, u32[]{:S(2)}) collective-permute-start(f32[32,2080]{1,0:T(8,128)} %get-tuple-element.42), channel_id=1, source_target_pairs={{0,8},{4,12},{8,0},{12,4},{1,9},{5,13},{9,1},{13,5},{2,10},{6,14},... | collective-permute-start | bytes 798728 | tf_op jit(solution)/shard_map/ppermute | solution.py:150
  172.8 8.1 %copy-start.1 = (bf16[48,2,64,256]{3,2,1,0:T(8,128)(2,1)S(1)}, bf16[48,2,64,256]{3,2,1,0:T(8,128)(2,1)}, u32[]{:S(2)}) copy-start(bf16[48,2,64,256]{3,2,1,0:T(8,128)(2,1)} %param.15) | copy-start | bytes 9437188

commit v5 on v4

--- a/solution.py
+++ b/solution.py
@@ -26,8 +26,11 @@
     first = pl.program_id(0) * tq
     dims = (((1,), (1,)), ((), ()))
     queries = q_ref[...]
+    slots, block_len, width = kc_ref.shape
+    ctx_keys = kc_ref[...].reshape(slots * block_len, width)
+    ctx_vals = vc_ref[...].reshape(slots * block_len, width)
     ctx_scores = (
-        lax.dot_general(queries, kc_ref[...], dims, preferred_element_type=jnp.float32)
+        lax.dot_general(queries, ctx_keys, dims, preferred_element_type=jnp.float32)
         * score_scale
         + bias_ref[...]
     )
@@ -48,13 +51,15 @@
         own_weights, axis=1, keepdims=True
     )
     o_ref[...] = jnp.dot(
-        ctx_weights.astype(jnp.bfloat16), vc_ref[...], preferred_element_type=jnp.float32
+        ctx_weights.astype(jnp.bfloat16), ctx_vals, preferred_element_type=jnp.float32
     ) + jnp.dot(own_weights.astype(jnp.bfloat16), vq_ref[...], preferred_element_type=jnp.float32)
 
 
-def attend(queries, ctx_keys, own_keys, ctx_vals, own_vals, ctx_bias, key_rank, group_size, score_scale):
+def attend(queries, ctx_blocks, own_keys, own_vals, ctx_bias, key_rank, group_size, score_scale):
     tokens, q_width = queries.shape
-    ctx_count = ctx_keys.shape[0]
+    slots, double_len, _ = ctx_blocks.shape
+    block_len = double_len // 2
+    ctx_count = slots * block_len
     own_count = own_keys.shape[0]
     heads = q_width // HD
     tq = min(tokens, 128)
@@ -66,9 +71,9 @@
             pl.BlockSpec((1, ctx_count), lambda i, n: (0, 0)),
             pl.BlockSpec((1, own_count), lambda i, n: (0, 0)),
             pl.BlockSpec((tq, HD), lambda i, n: (i, n)),
-            pl.BlockSpec((ctx_count, HD), lambda i, n: (0, n // group_size)),
+            pl.BlockSpec((slots, block_len, HD), lambda i, n: (0, 0, n // group_size)),
             pl.BlockSpec((own_count, HD), lambda i, n: (0, n // group_size)),
-            pl.BlockSpec((ctx_count, HD), lambda i, n: (0, n // group_size)),
+            pl.BlockSpec((slots, block_len, HD), lambda i, n: (0, 1, n // group_size)),
             pl.BlockSpec((own_count, HD), lambda i, n: (0, n // group_size)),
         ],
         out_specs=[
@@ -81,7 +86,7 @@
             jax.ShapeDtypeStruct((heads, tokens, 1), jnp.float32),
             jax.ShapeDtypeStruct((heads, tokens, 1), jnp.float32),
         ],
-    )(ctx_bias, key_rank, queries, ctx_keys, own_keys, ctx_vals, own_vals)
+    )(ctx_bias, key_rank, queries, ctx_blocks, own_keys, ctx_blocks, own_vals)
 
 
 def shift_pairs(shards, step):
@@ -222,7 +227,6 @@
     summed = lax.dynamic_index_in_dim(gathered, own_index, 0, keepdims=False)
     every_query = gathered[:, :q_size].reshape(shards * q_rows, q_width)
     every_kv = gathered[:, q_size:].reshape(shards, row_count, 2, kv_width)
-    question_kv = summed[q_size:].reshape(row_count, 2, kv_width)[:q_rows]
     recomp_kv = every_kv[:, q_rows:].reshape(shards * r_rows, 2, kv_width)
 
     own_owner = lax.dynamic_index_in_dim(owners, own_index, 0, keepdims=False)
@@ -242,23 +246,17 @@
     ).astype(jnp.bfloat16)
     kv_cache = jnp.where(hit[None, :, None], placed, cached)
 
-    slot_count = slot_pos.shape[0]
-    own_blocks = jnp.transpose(send_blocks, (2, 0, 1, 3, 4)).reshape(2, slot_count, kv_width)
-    owner_match = recomp_pos[None, :] == slot_pos[:, None]
-    owner_hit = jnp.any(owner_match, axis=1)
-    owner_placed = jnp.einsum(
-        "pi,ick->cpk", owner_match.astype(jnp.bfloat16), recomp_kv, preferred_element_type=jnp.float32
-    ).astype(jnp.bfloat16)
-    owner_kv = jnp.where(owner_hit[None, :, None], owner_placed, own_blocks)
-    ctx_bias = jnp.where(slot_pos >= 0, 0.0, neg_large).astype(jnp.float32)[None, :]
-    key_rank = (own_index * q_rows + jnp.arange(q_rows)).astype(jnp.int32)[None, :]
+    replaced = jnp.any(recomp_pos[None, :] == slot_pos[:, None], axis=1)
+    ctx_bias = jnp.where((slot_pos >= 0) & ~replaced, 0.0, neg_large).astype(jnp.float32)[None, :]
+    own_kv = summed[q_size:].reshape(row_count, 2, kv_width)
+    own_row = jnp.arange(row_count)
+    key_rank = jnp.where(own_row < q_rows, own_index * q_rows + own_row, -1).astype(jnp.int32)[None, :]
 
     part_sums, part_max, part_total = attend(
         every_query,
-        owner_kv[0],
-        question_kv[:, 0],
-        owner_kv[1],
-        question_kv[:, 1],
+        send_blocks.reshape(shards * capacity, 2 * block_len, kv_width),
+        own_kv[:, 0],
+        own_kv[:, 1],
         ctx_bias,
         key_rank,
         group_size,

time: 182 us -> 170 us (0.934)
  waiting for transfers between devices: 36.1 us -> 23.6 us
  matrix products: 17.7 us -> 11.6 us
  local copies, waits for them, and re-layouts: 56 us -> 60.2 us
  other arithmetic: 32.6 us -> 35.2 us
    mul x3 -> x4, local copies, waits for them, and re-layouts: 0.42 us -> 17.3 us  [body(): send_codes.astype(jnp.float32)]
    ppermute x1, waiting for transfers between devices: 25.2 us -> 12.4 us  [hier_reduce_gather(): total = total + lax.ppermute(send, 'ctx', shift_pairs(shards, step))]
    convert_element_type x1 -> x2, other arithmetic: 4.07 us -> 13.3 us  [body(): send_blocks = (send_codes.astype(jnp.float32).reshape(shards * capacity,...]
    transpose x1 -> x0, other arithmetic: 6.23 us -> none  [body(): jnp.transpose(send_blocks, (2, 0, 1, 3, 4)).reshape(2, slot_count, kv_width)]
    dot_general x1 -> x0, matrix products: 6.04 us -> none  [body(): jnp.einsum('pi,ick->cpk', owner_match.astype(jnp.bfloat16), recomp_kv, pr...]
    transpose x1 -> x0, local copies, waits for them, and re-layouts: 4.76 us -> none  [body(): jnp.transpose(send_blocks, (2, 0, 1, 3, 4)).reshape(2, slot_count, kv_width)]
    all_to_all x1 -> x0, local copies, waits for them, and re-layouts: 4.75 us -> none  [body(): lax.all_to_all(send_blocks, 'ctx', split_axis=0, concat_axis=0, tiled=True)]
    convert_element_type x2 -> x0, local copies, waits for them, and re-layouts: 2.58 us -> none  [the longest x1 2.48 us: body(): send_blocks = (send_codes.astype(jnp.float32).reshape(shards * capacity,...]
  transfers between devices with their start and end apart: 8 -> 8, of which waited for: 5 -> 5; matrix products, arithmetic and copies ran while one was open for 51% -> 55% of each run, Pallas kernels for 14% -> 14%
where the time goes in v5:
time: 170 us; the launch traced here: 169 us
  local copies, waits for them, and re-layouts  60.2 us (35%)
  other arithmetic  35.2 us (21%)
  Pallas kernels  24.5 us (14%)
  waiting for transfers between devices  23.6 us (14%)
  starting transfers between devices  12.8 us (8%)
  matrix products  11.6 us (7%)
    pallas_call x1, Pallas kernels, attend(): pl.pallas_call(functools.partial(attn_kernel, score_scale=score_scale), g...  24.5 us
    mul x4, local copies, waits for them, and re-layouts, body(): send_codes.astype(jnp.float32)  17.3 us
    convert_element_type x2, other arithmetic, body(): send_blocks = (send_codes.astype(jnp.float32).reshape(shards * capacity,...  13.3 us
    ppermute x1, waiting for transfers between devices, hier_reduce_gather(): total = total + lax.ppermute(send, 'ctx', shift_pairs(shards, step))  12.4 us
    unnamed x33, local copies, waits for them, and re-layouts  12 us
    ppermute x1, waiting for transfers between devices, hier_reduce_gather(): lax.ppermute(rounded, 'ctx', shift_pairs(shards, step))  5.73 us
    all_to_all x1, starting transfers between devices, body(): lax.all_to_all(send_blocks, 'ctx', split_axis=0, concat_axis=0, tiled=True)  5.02 us
    dot_general x1, matrix products, body(): jnp.dot(question_part, w_query, preferred_element_type=jnp.float32)  4.63 us
  transfers between devices with their start and end apart: 8, of which 5 were waited for; matrix products, arithmetic and copies ran while one was open for 55% of the time, Pallas kernels for 14%

profile of v5, /device:TPU:0, one launch (start us, length us, event | category | flops | bytes accessed | tf_op | source)
XLA Modules:
  0.0 169.1 jit_solution(10687138524130037554)
XLA Ops:
  1.5 1.7 fusion.2
  6.4 4.5 %all-to-all-start = ((bf16[96,4,2048]{2,0,1:T(8,128)(2,1)}), bf16[96,4,2048]{2,0,1:T(8,128)(2,1)}, u32[]{:S(2)}, u32[]{:S(2)}) async-start(bf16[96,4,2048]{2,0,1:T(8,128)(2,1)} %bitcast.98), calls=%async_computation | async-start | bytes 3145728 | tf_op jit(solution)/shard_map/all_to_all | solution.py:213
  13.4 3.4 %copy.75 = bf16[256,8,2,256]{3,1,2,0:T(8,128)(2,1)} copy(bf16[256,8,2,256]{3,2,1,0:T(2,128)(2,1)} %bitcast.102) | data formatting | bytes 4194304
  17.6 2.8 %gather_fusion.2 = bf16[64,2,64,256]{3,2,1,0:T(8,128)(2,1)} fusion(bf16[48,2,64,256]{3,2,1,0:T(8,128)(2,1)S(1)} %copy-done, s32[1024]{0:T(1024)S(1)} %pad_clamp_fusion.1), kind=kCustom, calls=%fused_computation.2 | custom fusion | bytes 8388864 | tf_op jit(solution)/shard_map/jit(_take)/gather | solution.py:195
  22.3 6.1 %multiply_convert_fusion = bf16[4,16,2,64,256]{4,3,2,1,0:T(8,128)(2,1)} fusion(f32[4,16,2,256]{3,2,1,0:T(2,128)S(1)} %mul.192, bf16[4,16,2,64,256]{4,3,2,1,0:T(8,128)(2,1)} %bitcast.96, pred[4,16]{1,0:T(4,128)(4,1)S(1)} %compare_and_fusion), kind=kLoop, calls=%fused_computation.5 | loop fusion | flops 8388608 | bytes 8519744 | tf_op jit(solution)/shard_map/convert_element_type | solution.py:200
  28.4 3.3 %all-to-all-done = bf16[96,4,2048]{2,0,1:T(8,128)(2,1)} async-done(((bf16[96,4,2048]{2,0,1:T(8,128)(2,1)}), bf16[96,4,2048]{2,0,1:T(8,128)(2,1)}, u32[]{:S(2)}, u32[]{:S(2)}) %all-to-all-start) | async-done | bytes 1572896 | tf_op jit(solution)/shard_map/all_to_all | solution.py:213
  31.7 5.0 %all-to-all-start.1 = ((bf16[4,16,2,64,256]{4,3,2,1,0:T(8,128)(2,1)}), bf16[4,16,2,64,256]{4,3,2,1,0:T(8,128)(2,1)}, u32[]{:S(2)}, u32[]{:S(2)}) async-start(bf16[4,16,2,64,256]{4,3,2,1,0:T(8,128)(2,1)} %multiply_convert_fusion), calls=%async_computation.1 | async-start | bytes 8388608 | tf_op jit(solution)/shard_map/all_to_all | solution.py:201
  37.8 4.6 %fusion.34 = f32[128,2048]{1,0:T(8,128)S(1)} fusion(bf16[128,2048]{1,0:T(8,128)(2,1)S(1)} %bitcast.101, bf16[2048,2048]{1,0:T(8,128)(2,1)} %param.13), kind=kOutput, calls=%fused_computation.125 | convolution fusion | flops 1073741824 | bytes 9961472 | tf_op jit(solution)/shard_map/dot_general | solution.py:218
  45.0 3.3 %fusion.35 = f32[384,512]{1,0:T(8,128)} fusion(bf16[384,2048]{1,0:T(8,128)(2,1)} %bitcast.2, bf16[2048,512]{1,0:T(8,128)(2,1)S(1)} %bitcast.103), kind=kOutput, calls=%fused_computation.126 | convolution fusion | flops 805306368 | bytes 4456448 | tf_op jit(solution)/shard_map/dot_general | solution.py:219
  48.3 1.8 %concatenate.26 = f32[2,2,49152]{2,1,0:T(2,128)S(1)} reshape(f32[384,512]{1,0:T(8,128)} %fusion.35) | data formatting | bytes 1572864 | tf_op jit(solution)/shard_map/concatenate | solution.py:222
  50.2 2.5 %constant_dynamic-slice_fusion.5 = (f32[2,1,114688]{2,1,0:T(1,128)}, f32[2,1,114688]{2,1,0:T(1,128)S(1)}) fusion(f32[2,2,114688]{2,1,0:T(2,128)S(1)} %constant_dynamic-update-slice_fusion, s32[]{:T(128)S(6)} %select_n.239, s32[]{:T(128)S(6)} %select_n.240), kind=kLoop, calls=%fused_computation.97 | loop fusion | bytes 3670024 | tf_op jit(solution)/shard_map/jit(dynamic_index_in_dim)/dynamic_slice | solution.py:110
  53.9 5.4 %mul.169 = f32[64,2,64,2,128]{4,3,2,1,0:T(2,128)} broadcast(f32[64,2,2]{2,1,0:T(2,128)S(1)} %fusion.15), dimensions={0,1,3} | broadcast | bytes 8389632 | tf_op jit(solution)/shard_map/mul | solution.py:198
  59.3 11.6 %mul.170 = f32[64,128,256]{2,1,0:T(8,128)} reshape(f32[64,2,64,2,128]{4,3,2,1,0:T(2,128)} %mul.169) | data formatting | bytes 16777216 | tf_op jit(solution)/shard_map/mul | solution.py:198
  73.2 1.7 %collective-permute-start.1 = (f32[114688]{0:T(1024)S(1)}, f32[114688]{0:T(1024)S(1)}, u32[]{:S(2)}, u32[]{:S(2)}) collective-permute-start(f32[114688]{0:T(1024)S(1)} %bitcast.111), channel_id=1, source_target_pairs={{0,8},{4,12},{8,0},{12,4},{1,9},{5,13},{9,1},{13,5},{2,10},{6,14},... | collective-permute-start | bytes 1376264 | tf_op jit(solution)/shard_map/ppermute | solution.py:116
  74.9 7.2 %multiply_convert_fusion.1.kc_ref.vc_ref = bf16[64,128,256]{2,1,0:T(8,128)(2,1)} fusion(f32[64,128,256]{2,1,0:T(8,128)} %mul.170, bf16[64,2,64,256]{3,2,1,0:T(8,128)(2,1)S(1)} %copy-done.2, pred[64]{0:T(512)(128)(4,1)S(1)} %compare_and_fusion.2), kind=kLoop, calls=%fused_computation.6 | loop fusion | flops 8388608 | bytes 16777280 | tf_op jit(solution)/shard_map/convert_element_type | solution.py:200
  82.1 12.4 %collective-permute-done.1 = f32[114688]{0:T(1024)S(1)} collective-permute-done((f32[114688]{0:T(1024)S(1)}, f32[114688]{0:T(1024)S(1)}, u32[]{:S(2)}, u32[]{:S(2)}) %collective-permute-start.1) | collective-permute-done | bytes 458784 | tf_op jit(solution)/shard_map/ppermute | solution.py:116
  95.9 5.7 %collective-permute-done.2 = bf16[114688]{0:T(1024)(128)(2,1)S(1)} collective-permute-done((bf16[114688]{0:T(1024)(128)(2,1)S(1)}, bf16[114688]{0:T(1024)(128)(2,1)S(1)}, u32[]{:S(2)}, u32[]{:S(2)}) %collective-permute-start.2) | collective-permute-done | bytes 229408 | tf_op jit(solution)/shard_map/ppermute | solution.py:119
  107.7 2.4 %gather_fusion.1 = bf16[2,2,114688]{2,1,0:T(2,128)(2,1)S(1)} fusion(bf16[2,2,114688]{2,0,1:T(2,128)(2,1)S(1)} %pad_maximum_fusion.1, s32[1024]{0:T(1024)S(1)} %get-tuple-element.42), kind=kCustom, calls=%fused_computation.1 | custom fusion | bytes 1835016 | tf_op jit(solution)/shard_map/jit(_take)/gather | solution.py:102
  115.8 24.5 %shard_map.113 = (f32[128,2048]{1,0:T(8,128)}, f32[16,128,1]{2,1,0:T(8,128)}, f32[16,128,1]{2,1,0:T(8,128)}) custom-call(f32[1,4096]{1,0:T(1,128)} %and_select_fusion.bias_ref, s32[1,96]{1,0:T(1,128)} %compare_select_fusion.13.rank_ref, bf16[128,2048]{1,0:T(8,128)(2,1)} %reshape.422.q_ref, bf16[64,128,256]{2,1,0:T(8,128)(2,1)} %multiply_convert_fusion.1.kc_ref.vc_ref, ...), custom_call_target="tpu_custom_call" | custom-call | tf_op jit(solution)/shard_map/pallas_call | solution.py:67
  146.5 2.9 %gather_fusion.4 = bf16[32,2,64,256]{3,2,1,0:T(8,128)(2,1)S(1)} fusion(bf16[64,2,64,256]{3,2,1,0:T(8,128)(2,1)} %bitcast.28, s32[1024]{0:T(1024)S(1)} %get-tuple-element.41), kind=kCustom, calls=%fused_computation.4 | custom fusion | bytes 4194432 | tf_op jit(solution)/shard_map/jit(_take)/gather | solution.py:235
  149.7 2.4 %copy.64 = bf16[2,2048,256]{1,2,0:T(8,128)(2,1)} copy(bf16[2,2048,256]{2,1,0:T(8,128)(2,1)S(1)} %bitcast.97) | data formatting | bytes 4194304 | tf_op jit(solution)/shard_map/reshape | solution.py:238
  157.3 3.7 %fusion.1 = bf16[2,2048,256]{1,2,0:T(8,128)(2,1)} fusion(bf16[2,2048,256]{1,2,0:T(8,128)(2,1)} %copy.64, bf16[256,2,256]{2,0,1:T(8,128)(2,1)S(1)} %bitcast.114, pred[2048]{0:T(1024)(128)(4,1)S(1)} %fusion.6, s32[256]{0:T(256)S(1)} %broadcast_subtract_fusion), kind=kOutput, calls=%fused_computation.11 | convolution fusion | flops 539492352 | bytes 4459520 | tf_op jit(solution)/shard_map/pi,ick->cpk/dot_general | solution.py:244
  161.0 4.1 %copy.65 = bf16[2,2048,256]{2,1,0:T(8,128)(2,1)} copy(bf16[2,2048,256]{1,2,0:T(8,128)(2,1)} %fusion.1) | data formatting | bytes 4194304
  167.2 1.9 %fusion.13 = bf16[32,2048]{1,0:T(8,128)(2,1)} fusion(f32[4,8,16,128]{3,2,1,0:T(8,128)S(1)} %bitcast.106, f32[4,8,16,128]{3,2,1,0:T(8,128)S(1)} %bitcast.107, f32[4,8,16,128]{3,2,1,0:T(8,128)S(1)} %bitcast.108, f32[32,2080]{1,0:T(8,128)} %collective-permute-done.5, f32[32,2080]{1,0:T(8,128)S(1)} %get-tuple-element.35), kind=kLoop, calls=%fused_computation.45 | loop fusion | flops 327680 | bytes 1441792 | tf_op jit(solution)/shard_map/convert_element_type | solution.py:276
  (132 shorter events, 43.2 us)
Async XLA Ops:
  0.6 16.9 %copy-start = (bf16[48,2,64,256]{3,2,1,0:T(8,128)(2,1)S(1)}, bf16[48,2,64,256]{3,2,1,0:T(8,128)(2,1)}, u32[]{:S(2)}) copy-start(bf16[48,2,64,256]{3,2,1,0:T(8,128)(2,1)} %param.15) | copy-start | bytes 9437188
  0.6 3.8 %copy-start.3 = (bf16[64,8192]{1,0:T(8,128)(2,1)S(1)}, bf16[64,8192]{1,0:T(8,128)(2,1)}, u32[]{:S(2)}) copy-start(bf16[64,8192]{1,0:T(8,128)(2,1)} %param.11) | copy-start | bytes 3145732
  0.7 4.2 %copy-start.7 = (bf16[32,8192]{1,0:T(8,128)(2,1)S(1)}, bf16[32,8192]{1,0:T(8,128)(2,1)}, u32[]{:S(2)}) copy-start(bf16[32,8192]{1,0:T(8,128)(2,1)} %param.10) | copy-start | bytes 1572868
  6.4 4.6 %copy-start.10 = (s32[128]{0:T(128)S(1)}, s32[128]{0:T(128)}, u32[]{:S(2)}) copy-start(s32[128]{0:T(128)} %param.18) | copy-start | bytes 1540
  6.4 5.2 %copy-start.11 = (s32[128,1]{0,1:T(1,128)S(1)}, s32[128,1]{0,1:T(1,128)}, u32[]{:S(2)}) copy-start(s32[128,1]{0,1:T(1,128)} %param.17) | copy-start | bytes 1540
  6.4 25.3 %all-to-all-start = ((bf16[96,4,2048]{2,0,1:T(8,128)(2,1)}), bf16[96,4,2048]{2,0,1:T(8,128)(2,1)}, u32[]{:S(2)}, u32[]{:S(2)}) async-start(bf16[96,4,2048]{2,0,1:T(8,128)(2,1)} %bitcast.98), calls=%async_computation | async-start | bytes 3145728 | tf_op jit(solution)/shard_map/all_to_all | solution.py:213
  13.4 3.4 %copy-start.9 = (bf16[48,2,2]{0,2,1:T(2,128)(2,1)S(1)}, bf16[48,2,2]{0,2,1:T(2,128)(2,1)}, u32[]{:S(2)}) copy-start(bf16[48,2,2]{0,2,1:T(2,128)(2,1)} %param.16) | copy-start | bytes 1156
  17.5 3.3 %copy-start.8 = (s32[256]{0:T(256)S(1)}, s32[256]{0:T(256)}, u32[]{:S(2)}) copy-start(s32[256]{0:T(256)} %param.19) | copy-start | bytes 3076
  31.7 114.7 %all-to-all-start.1 = ((bf16[4,16,2,64,256]{4,3,2,1,0:T(8,128)(2,1)}), bf16[4,16,2,64,256]{4,3,2,1,0:T(8,128)(2,1)}, u32[]{:S(2)}, u32[]{:S(2)}) async-start(bf16[4,16,2,64,256]{4,3,2,1,0:T(8,128)(2,1)} %multiply_convert_fusion), calls=%async_computation.1 | async-start | bytes 8388608 | tf_op jit(solution)/shard_map/all_to_all | solution.py:201
  43.4 1.6 copy-start.6
  53.4 18.1 %collective-permute-start = (f32[2,114688]{1,0:T(2,128)S(1)}, f32[2,114688]{1,0:T(2,128)S(1)}, u32[]{:S(2)}, u32[]{:S(2)}) collective-permute-start(f32[2,114688]{1,0:T(2,128)S(1)} %bitcast.109), channel_id=1, source_target_pairs={{0,4},{4,0},{8,12},{12,8},{1,5},{5,1},{9,13},{13,9},{2,6},{6,2},{1... | collective-permute-start | bytes 2752520 | tf_op jit(solution)/shard_map/ppermute | solution.py:112
  59.3 12.2 %copy-start.4 = (f32[2,1,114688]{2,1,0:T(1,128)S(1)}, f32[2,1,114688]{2,1,0:T(1,128)}, u32[]{:S(2)}) copy-start(f32[2,1,114688]{2,1,0:T(1,128)} %get-tuple-element.29) | copy-start | bytes 2752516
  71.5 3.4 %copy-start.2 = (bf16[64,2,64,256]{3,2,1,0:T(8,128)(2,1)S(1)}, bf16[64,2,64,256]{3,2,1,0:T(8,128)(2,1)}, u32[]{:S(2)}) copy-start(bf16[64,2,64,256]{3,2,1,0:T(8,128)(2,1)} %gather_fusion.2) | copy-start | bytes 12582916
  73.2 21.2 %collective-permute-start.1 = (f32[114688]{0:T(1024)S(1)}, f32[114688]{0:T(1024)S(1)}, u32[]{:S(2)}, u32[]{:S(2)}) collective-permute-start(f32[114688]{0:T(1024)S(1)} %bitcast.111), channel_id=1, source_target_pairs={{0,8},{4,12},{8,0},{12,4},{1,9},{5,13},{9,1},{13,5},{2,10},{6,14},... | collective-permute-start | bytes 1376264 | tf_op jit(solution)/shard_map/ppermute | solution.py:116
  94.5 7.1 %collective-permute-start.2 = (bf16[114688]{0:T(1024)(128)(2,1)S(1)}, bf16[114688]{0:T(1024)(128)(2,1)S(1)}, u32[]{:S(2)}, u32[]{:S(2)}) collective-permute-start(bf16[114688]{0:T(1024)(128)(2,1)S(1)} %add_convert_fusion), channel_id=1, source_target_pairs={{0,8},{4,12},{8,0},{12,4},{1,9},{5,13},{9,1},{13,5},{2,10},{6,14},... | collective-permute-start | bytes 688136 | tf_op jit(solution)/shard_map/ppermute | solution.py:119
  104.5 1.9 %collective-permute-start.3 = (bf16[2,114688]{1,0:T(2,128)(2,1)S(1)}, bf16[2,114688]{1,0:T(2,128)(2,1)S(1)}, u32[]{:S(2)}, u32[]{:S(2)}) collective-permute-start(bf16[2,114688]{1,0:T(2,128)(2,1)S(1)} %broadcast_select_fusion.1), channel_id=1, source_target_pairs={{0,4},{4,0},{8,12},{12,8},{1,5},{5,1},{9,13},{13,9},{2,6},{6,2},{1... | collective-permute-start | bytes 1376264 | tf_op jit(solution)/shard_map/ppermute | solution.py:123
  146.0 7.0 %collective-permute-start.4 = (f32[2,32,2080]{2,1,0:T(8,128)}, f32[2,32,2080]{2,1,0:T(8,128)}, u32[]{:S(2)}, u32[]{:S(2)}) collective-permute-start(f32[2,32,2080]{2,1,0:T(8,128)} %get-tuple-element.32), channel_id=1, source_target_pairs={{0,4},{4,0},{8,12},{12,8},{1,5},{5,1},{9,13},{13,9},{2,6},{6,2},{1... | collective-permute-start | bytes 1597448 | tf_op jit(solution)/shard_map/ppermute | solution.py:151
  152.1 1.1 copy-start.5
  156.7 9.3 %collective-permute-start.5 = (f32[32,2080]{1,0:T(8,128)}, f32[32,2080]{1,0:T(8,128)}, u32[]{:S(2)}, u32[]{:S(2)}) collective-permute-start(f32[32,2080]{1,0:T(8,128)} %get-tuple-element.36), channel_id=1, source_target_pairs={{0,8},{4,12},{8,0},{12,4},{1,9},{5,13},{9,1},{13,5},{2,10},{6,14},... | collective-permute-start | bytes 798728 | tf_op jit(solution)/shard_map/ppermute | solution.py:155
  161.0 8.1 %copy-start.1 = (bf16[48,2,64,256]{3,2,1,0:T(8,128)(2,1)S(1)}, bf16[48,2,64,256]{3,2,1,0:T(8,128)(2,1)}, u32[]{:S(2)}) copy-start(bf16[48,2,64,256]{3,2,1,0:T(8,128)(2,1)} %param.15) | copy-start | bytes 9437188

commit v6 on v5

--- a/solution.py
+++ b/solution.py
@@ -198,6 +198,7 @@
         send_codes.astype(jnp.float32).reshape(shards * capacity, 2, block_len, kv_heads, HD)
         * send_scales.astype(jnp.float32)[:, :, None, :, None]
     ).astype(jnp.bfloat16).reshape((shards, capacity, 2, block_len, kv_width))
+    send_blocks = lax.optimization_barrier(send_blocks)
     got_blocks = lax.all_to_all(send_blocks, "ctx", split_axis=0, concat_axis=0, tiled=True)
     ctx_dev = per_dev * block_len
     slot_valid = jnp.any(chosen, axis=1)

time: 170 us -> 170 us (level)
  waiting for transfers between devices: 23.6 us -> 47.1 us
  local copies, waits for them, and re-layouts: 60.2 us -> 43.4 us
  other arithmetic: 35.2 us -> 28 us
    ppermute x1, waiting for transfers between devices: 12.4 us -> 34.7 us  [hier_reduce_gather(): total = total + lax.ppermute(send, 'ctx', shift_pairs(shards, step))]
    mul x4 -> x2, local copies, waits for them, and re-layouts: 17.3 us -> 0.35 us  [body(): send_codes.astype(jnp.float32)]
    convert_element_type x2 -> x1, other arithmetic: 13.3 us -> 6.13 us  [body(): send_blocks = (send_codes.astype(jnp.float32).reshape(shards * capacity,...]
    unnamed x33 -> x31, local copies, waits for them, and re-layouts: 12 us -> 12 us
  transfers between devices with their start and end apart: 8 -> 8, of which waited for: 5 -> 6; matrix products, arithmetic and copies ran while one was open for 55% -> 41% of each run, Pallas kernels for 14% -> 14%
where the time goes in v6:
time: 170 us; the launch traced here: 169 us
  waiting for transfers between devices  47.1 us (28%)
  local copies, waits for them, and re-layouts  43.4 us (26%)
  other arithmetic  28 us (16%)
  Pallas kernels  24.5 us (14%)
  starting transfers between devices  13.3 us (8%)
  matrix products  11.6 us (7%)
    ppermute x1, waiting for transfers between devices, hier_reduce_gather(): total = total + lax.ppermute(send, 'ctx', shift_pairs(shards, step))  34.7 us
    pallas_call x1, Pallas kernels, attend(): pl.pallas_call(functools.partial(attn_kernel, score_scale=score_scale), g...  24.5 us
    unnamed x31, local copies, waits for them, and re-layouts  12 us
    convert_element_type x1, other arithmetic, body(): send_blocks = (send_codes.astype(jnp.float32).reshape(shards * capacity,...  6.13 us
    ppermute x1, waiting for transfers between devices, hier_reduce_gather(): lax.ppermute(rounded, 'ctx', shift_pairs(shards, step))  5.77 us
    all_to_all x1, starting transfers between devices, body(): lax.all_to_all(send_blocks, 'ctx', split_axis=0, concat_axis=0, tiled=True)  4.84 us
    dot_general x1, matrix products, body(): jnp.dot(question_part, w_query, preferred_element_type=jnp.float32)  4.64 us
    all_to_all x1, starting transfers between devices, body(): lax.all_to_all(normed, 'ctx', split_axis=1, concat_axis=0, tiled=True)  4.52 us
  transfers between devices with their start and end apart: 8, of which 6 were waited for; matrix products, arithmetic and copies ran while one was open for 41% of the time, Pallas kernels for 14%

profile of v6, /device:TPU:0, one launch (start us, length us, event | category | flops | bytes accessed | tf_op | source)
XLA Modules:
  0.0 169.1 jit_solution(1784052088320800559)
XLA Ops:
  1.5 1.7 fusion.2
  6.4 4.5 %all-to-all-start = ((bf16[96,4,2048]{2,0,1:T(8,128)(2,1)}), bf16[96,4,2048]{2,0,1:T(8,128)(2,1)}, u32[]{:S(2)}, u32[]{:S(2)}) async-start(bf16[96,4,2048]{2,0,1:T(8,128)(2,1)} %bitcast.97), calls=%async_computation | async-start | bytes 3145728 | tf_op jit(solution)/shard_map/all_to_all | solution.py:214
  13.3 3.4 %copy.74 = bf16[256,8,2,256]{3,1,2,0:T(8,128)(2,1)} copy(bf16[256,8,2,256]{3,2,1,0:T(2,128)(2,1)} %bitcast.101) | data formatting | bytes 4194304
  18.0 2.8 %gather_fusion.2 = bf16[64,2,64,256]{3,2,1,0:T(8,128)(2,1)} fusion(bf16[48,2,64,256]{3,2,1,0:T(8,128)(2,1)S(1)} %copy-done, s32[1024]{0:T(1024)S(1)} %pad_clamp_fusion.1), kind=kCustom, calls=%fused_computation.2 | custom fusion | bytes 8388864 | tf_op jit(solution)/shard_map/jit(_take)/gather | solution.py:195
  20.8 6.1 %multiply_convert_fusion = bf16[4,16,2,64,256]{4,3,2,1,0:T(8,128)(2,1)} fusion(f32[4,16,2,256]{3,2,1,0:T(2,128)S(1)} %mul.163, bf16[4,16,2,64,256]{4,3,2,1,0:T(8,128)(2,1)} %bitcast.95, pred[4,16]{1,0:T(4,128)(4,1)S(1)} %compare_and_fusion.2), kind=kLoop, calls=%fused_computation.5 | loop fusion | flops 8388608 | bytes 8519744 | tf_op jit(solution)/shard_map/convert_element_type | solution.py:200
  28.3 3.3 %all-to-all-done = bf16[96,4,2048]{2,0,1:T(8,128)(2,1)} async-done(((bf16[96,4,2048]{2,0,1:T(8,128)(2,1)}), bf16[96,4,2048]{2,0,1:T(8,128)(2,1)}, u32[]{:S(2)}, u32[]{:S(2)}) %all-to-all-start) | async-done | bytes 1572896 | tf_op jit(solution)/shard_map/all_to_all | solution.py:214
  31.7 4.8 %all-to-all-start.1 = ((bf16[4,16,2,64,256]{4,3,2,1,0:T(8,128)(2,1)}), bf16[4,16,2,64,256]{4,3,2,1,0:T(8,128)(2,1)}, u32[]{:S(2)}, u32[]{:S(2)}) async-start(bf16[4,16,2,64,256]{4,3,2,1,0:T(8,128)(2,1)} %multiply_convert_fusion), calls=%async_computation.1 | async-start | bytes 8388608 | tf_op jit(solution)/shard_map/all_to_all | solution.py:202
  37.6 4.6 %fusion.34 = f32[128,2048]{1,0:T(8,128)S(1)} fusion(bf16[128,2048]{1,0:T(8,128)(2,1)S(1)} %bitcast.100, bf16[2048,2048]{1,0:T(8,128)(2,1)} %param.13), kind=kOutput, calls=%fused_computation.123 | convolution fusion | flops 1073741824 | bytes 9961472 | tf_op jit(solution)/shard_map/dot_general | solution.py:219
  43.5 1.5 copy-done.5
  45.0 3.3 %fusion.35 = f32[384,512]{1,0:T(8,128)} fusion(bf16[384,2048]{1,0:T(8,128)(2,1)} %bitcast.2, bf16[2048,512]{1,0:T(8,128)(2,1)S(1)} %bitcast.102), kind=kOutput, calls=%fused_computation.124 | convolution fusion | flops 805306368 | bytes 4456448 | tf_op jit(solution)/shard_map/dot_general | solution.py:220
  48.3 1.8 %concatenate.26 = f32[2,2,49152]{2,1,0:T(2,128)S(1)} reshape(f32[384,512]{1,0:T(8,128)} %fusion.35) | data formatting | bytes 1572864 | tf_op jit(solution)/shard_map/concatenate | solution.py:223
  50.2 2.5 %constant_dynamic-slice_fusion.5 = (f32[2,1,114688]{2,1,0:T(1,128)}, f32[2,1,114688]{2,1,0:T(1,128)S(1)}) fusion(f32[2,2,114688]{2,1,0:T(2,128)S(1)} %constant_dynamic-update-slice_fusion, s32[]{:T(128)S(6)} %select_n.236, s32[]{:T(128)S(6)} %select_n.237), kind=kLoop, calls=%fused_computation.95 | loop fusion | bytes 3670024 | tf_op jit(solution)/shard_map/jit(dynamic_index_in_dim)/dynamic_slice | solution.py:110
  57.7 2.0 %collective-permute-start.1 = (f32[114688]{0:T(1024)S(1)}, f32[114688]{0:T(1024)S(1)}, u32[]{:S(2)}, u32[]{:S(2)}) collective-permute-start(f32[114688]{0:T(1024)S(1)} %bitcast.110), channel_id=1, source_target_pairs={{0,8},{4,12},{8,0},{12,4},{1,9},{5,13},{9,1},{13,5},{2,10},{6,14},... | collective-permute-start | bytes 1376264 | tf_op jit(solution)/shard_map/ppermute | solution.py:116
  59.7 34.7 %collective-permute-done.1 = f32[114688]{0:T(1024)S(1)} collective-permute-done((f32[114688]{0:T(1024)S(1)}, f32[114688]{0:T(1024)S(1)}, u32[]{:S(2)}, u32[]{:S(2)}) %collective-permute-start.1) | collective-permute-done | bytes 458784 | tf_op jit(solution)/shard_map/ppermute | solution.py:116
  95.8 5.8 %collective-permute-done.2 = bf16[114688]{0:T(1024)(128)(2,1)S(1)} collective-permute-done((bf16[114688]{0:T(1024)(128)(2,1)S(1)}, bf16[114688]{0:T(1024)(128)(2,1)S(1)}, u32[]{:S(2)}, u32[]{:S(2)}) %collective-permute-start.2) | collective-permute-done | bytes 229408 | tf_op jit(solution)/shard_map/ppermute | solution.py:119
  107.7 2.6 %gather_fusion.1 = bf16[2,2,114688]{2,1,0:T(2,128)(2,1)S(1)} fusion(bf16[2,2,114688]{2,0,1:T(2,128)(2,1)S(1)} %pad_maximum_fusion.1, s32[1024]{0:T(1024)S(1)} %get-tuple-element.42), kind=kCustom, calls=%fused_computation.1 | custom fusion | bytes 1835016 | tf_op jit(solution)/shard_map/jit(_take)/gather | solution.py:102
  115.7 24.5 %shard_map.113 = (f32[128,2048]{1,0:T(8,128)}, f32[16,128,1]{2,1,0:T(8,128)}, f32[16,128,1]{2,1,0:T(8,128)}) custom-call(f32[1,4096]{1,0:T(1,128)} %and_select_fusion.bias_ref, s32[1,96]{1,0:T(1,128)} %compare_select_fusion.13.rank_ref, bf16[128,2048]{1,0:T(8,128)(2,1)} %reshape.423.q_ref, bf16[64,128,256]{2,1,0:T(8,128)(2,1)} %bitcast.93, ...), custom_call_target="tpu_custom_call" | custom-call | tf_op jit(solution)/shard_map/pallas_call | solution.py:67
  140.2 1.6 reduce.2
  141.8 1.6 reduce.3
  146.5 2.9 %gather_fusion.4 = bf16[32,2,64,256]{3,2,1,0:T(8,128)(2,1)S(1)} fusion(bf16[64,2,64,256]{3,2,1,0:T(8,128)(2,1)} %bitcast.28, s32[1024]{0:T(1024)S(1)} %get-tuple-element.41), kind=kCustom, calls=%fused_computation.4 | custom fusion | bytes 4194432 | tf_op jit(solution)/shard_map/jit(_take)/gather | solution.py:236
  149.8 2.4 %copy.63 = bf16[2,2048,256]{1,2,0:T(8,128)(2,1)} copy(bf16[2,2048,256]{2,1,0:T(8,128)(2,1)S(1)} %bitcast.96) | data formatting | bytes 4194304 | tf_op jit(solution)/shard_map/reshape | solution.py:239
  157.5 3.7 %fusion.1 = bf16[2,2048,256]{1,2,0:T(8,128)(2,1)} fusion(bf16[2,2048,256]{1,2,0:T(8,128)(2,1)} %copy.63, bf16[256,2,256]{2,0,1:T(8,128)(2,1)S(1)} %bitcast.113, pred[2048]{0:T(1024)(128)(4,1)S(1)} %fusion.6, s32[256]{0:T(256)S(1)} %broadcast_subtract_fusion), kind=kOutput, calls=%fused_computation.9 | convolution fusion | flops 539492352 | bytes 4459520 | tf_op jit(solution)/shard_map/pi,ick->cpk/dot_general | solution.py:245
  161.2 4.1 %copy.64 = bf16[2,2048,256]{2,1,0:T(8,128)(2,1)} copy(bf16[2,2048,256]{1,2,0:T(8,128)(2,1)} %fusion.1) | data formatting | bytes 4194304
  167.2 1.9 %fusion.13 = bf16[32,2048]{1,0:T(8,128)(2,1)} fusion(f32[4,8,16,128]{3,2,1,0:T(8,128)S(1)} %bitcast.105, f32[4,8,16,128]{3,2,1,0:T(8,128)S(1)} %bitcast.106, f32[4,8,16,128]{3,2,1,0:T(8,128)S(1)} %bitcast.107, f32[32,2080]{1,0:T(8,128)} %collective-permute-done.5, f32[32,2080]{1,0:T(8,128)S(1)} %get-tuple-element.35), kind=kLoop, calls=%fused_computation.43 | loop fusion | flops 327680 | bytes 1441792 | tf_op jit(solution)/shard_map/convert_element_type | solution.py:277
  (127 shorter events, 40.0 us)
Async XLA Ops:
  0.6 17.4 %copy-start = (bf16[48,2,64,256]{3,2,1,0:T(8,128)(2,1)S(1)}, bf16[48,2,64,256]{3,2,1,0:T(8,128)(2,1)}, u32[]{:S(2)}) copy-start(bf16[48,2,64,256]{3,2,1,0:T(8,128)(2,1)} %param.15) | copy-start | bytes 9437188
  0.6 3.8 %copy-start.2 = (bf16[64,8192]{1,0:T(8,128)(2,1)S(1)}, bf16[64,8192]{1,0:T(8,128)(2,1)}, u32[]{:S(2)}) copy-start(bf16[64,8192]{1,0:T(8,128)(2,1)} %param.11) | copy-start | bytes 3145732
  0.7 4.2 %copy-start.6 = (bf16[32,8192]{1,0:T(8,128)(2,1)S(1)}, bf16[32,8192]{1,0:T(8,128)(2,1)}, u32[]{:S(2)}) copy-start(bf16[32,8192]{1,0:T(8,128)(2,1)} %param.10) | copy-start | bytes 1572868
  6.4 4.6 %copy-start.9 = (s32[128]{0:T(128)S(1)}, s32[128]{0:T(128)}, u32[]{:S(2)}) copy-start(s32[128]{0:T(128)} %param.18) | copy-start | bytes 1540
  6.4 5.2 %copy-start.10 = (s32[128,1]{0,1:T(1,128)S(1)}, s32[128,1]{0,1:T(1,128)}, u32[]{:S(2)}) copy-start(s32[128,1]{0,1:T(1,128)} %param.17) | copy-start | bytes 1540
  6.4 25.3 %all-to-all-start = ((bf16[96,4,2048]{2,0,1:T(8,128)(2,1)}), bf16[96,4,2048]{2,0,1:T(8,128)(2,1)}, u32[]{:S(2)}, u32[]{:S(2)}) async-start(bf16[96,4,2048]{2,0,1:T(8,128)(2,1)} %bitcast.97), calls=%async_computation | async-start | bytes 3145728 | tf_op jit(solution)/shard_map/all_to_all | solution.py:214
  13.3 3.4 %copy-start.8 = (bf16[48,2,2]{0,2,1:T(2,128)(2,1)S(1)}, bf16[48,2,2]{0,2,1:T(2,128)(2,1)}, u32[]{:S(2)}) copy-start(bf16[48,2,2]{0,2,1:T(2,128)(2,1)} %param.16) | copy-start | bytes 1156
  20.8 6.1 %copy-start.7 = (s32[256]{0:T(256)S(1)}, s32[256]{0:T(256)}, u32[]{:S(2)}) copy-start(s32[256]{0:T(256)} %param.19) | copy-start | bytes 3076
  31.7 114.8 %all-to-all-start.1 = ((bf16[4,16,2,64,256]{4,3,2,1,0:T(8,128)(2,1)}), bf16[4,16,2,64,256]{4,3,2,1,0:T(8,128)(2,1)}, u32[]{:S(2)}, u32[]{:S(2)}) async-start(bf16[4,16,2,64,256]{4,3,2,1,0:T(8,128)(2,1)} %multiply_convert_fusion), calls=%async_computation.1 | async-start | bytes 8388608 | tf_op jit(solution)/shard_map/all_to_all | solution.py:202
  43.4 1.6 copy-start.5
  52.7 3.3 %copy-start.3 = (f32[2,1,114688]{2,1,0:T(1,128)S(1)}, f32[2,1,114688]{2,1,0:T(1,128)}, u32[]{:S(2)}) copy-start(f32[2,1,114688]{2,1,0:T(1,128)} %get-tuple-element.29) | copy-start | bytes 2752516
  53.4 2.6 %collective-permute-start = (f32[2,114688]{1,0:T(2,128)S(1)}, f32[2,114688]{1,0:T(2,128)S(1)}, u32[]{:S(2)}, u32[]{:S(2)}) collective-permute-start(f32[2,114688]{1,0:T(2,128)S(1)} %bitcast.108), channel_id=1, source_target_pairs={{0,4},{4,0},{8,12},{12,8},{1,5},{5,1},{9,13},{13,9},{2,6},{6,2},{1... | collective-permute-start | bytes 2752520 | tf_op jit(solution)/shard_map/ppermute | solution.py:112
  57.7 36.7 %collective-permute-start.1 = (f32[114688]{0:T(1024)S(1)}, f32[114688]{0:T(1024)S(1)}, u32[]{:S(2)}, u32[]{:S(2)}) collective-permute-start(f32[114688]{0:T(1024)S(1)} %bitcast.110), channel_id=1, source_target_pairs={{0,8},{4,12},{8,0},{12,4},{1,9},{5,13},{9,1},{13,5},{2,10},{6,14},... | collective-permute-start | bytes 1376264 | tf_op jit(solution)/shard_map/ppermute | solution.py:116
  94.5 7.1 %collective-permute-start.2 = (bf16[114688]{0:T(1024)(128)(2,1)S(1)}, bf16[114688]{0:T(1024)(128)(2,1)S(1)}, u32[]{:S(2)}, u32[]{:S(2)}) collective-permute-start(bf16[114688]{0:T(1024)(128)(2,1)S(1)} %add_convert_fusion), channel_id=1, source_target_pairs={{0,8},{4,12},{8,0},{12,4},{1,9},{5,13},{9,1},{13,5},{2,10},{6,14},... | collective-permute-start | bytes 688136 | tf_op jit(solution)/shard_map/ppermute | solution.py:119
  104.5 1.9 %collective-permute-start.3 = (bf16[2,114688]{1,0:T(2,128)(2,1)S(1)}, bf16[2,114688]{1,0:T(2,128)(2,1)S(1)}, u32[]{:S(2)}, u32[]{:S(2)}) collective-permute-start(bf16[2,114688]{1,0:T(2,128)(2,1)S(1)} %broadcast_select_fusion.1), channel_id=1, source_target_pairs={{0,4},{4,0},{8,12},{12,8},{1,5},{5,1},{9,13},{13,9},{2,6},{6,2},{1... | collective-permute-start | bytes 1376264 | tf_op jit(solution)/shard_map/ppermute | solution.py:123
  146.0 7.0 %collective-permute-start.4 = (f32[2,32,2080]{2,1,0:T(8,128)}, f32[2,32,2080]{2,1,0:T(8,128)}, u32[]{:S(2)}, u32[]{:S(2)}) collective-permute-start(f32[2,32,2080]{2,1,0:T(8,128)} %get-tuple-element.32), channel_id=1, source_target_pairs={{0,4},{4,0},{8,12},{12,8},{1,5},{5,1},{9,13},{13,9},{2,6},{6,2},{1... | collective-permute-start | bytes 1597448 | tf_op jit(solution)/shard_map/ppermute | solution.py:151
  152.2 1.1 copy-start.4
  156.7 9.2 %collective-permute-start.5 = (f32[32,2080]{1,0:T(8,128)}, f32[32,2080]{1,0:T(8,128)}, u32[]{:S(2)}, u32[]{:S(2)}) collective-permute-start(f32[32,2080]{1,0:T(8,128)} %get-tuple-element.36), channel_id=1, source_target_pairs={{0,8},{4,12},{8,0},{12,4},{1,9},{5,13},{9,1},{13,5},{2,10},{6,14},... | collective-permute-start | bytes 798728 | tf_op jit(solution)/shard_map/ppermute | solution.py:155
  161.2 7.9 %copy-start.1 = (bf16[48,2,64,256]{3,2,1,0:T(8,128)(2,1)S(1)}, bf16[48,2,64,256]{3,2,1,0:T(8,128)(2,1)}, u32[]{:S(2)}) copy-start(bf16[48,2,64,256]{3,2,1,0:T(8,128)(2,1)} %param.15) | copy-start | bytes 9437188

commit v7 on v6

--- a/solution.py
+++ b/solution.py
@@ -5,6 +5,7 @@
 from jax import lax
 from jax.experimental import pallas as pl
 from jax.sharding import PartitionSpec as P
+
 
 HD = 128
 
@@ -106,22 +107,35 @@
     chips = shards // 2
     core = own_index % 2
     chip = own_index // 2
-    by_core = partials.reshape(chips, 2, -1)
-    mine = lax.dynamic_index_in_dim(by_core, core, 1, keepdims=False)
-    other = lax.dynamic_index_in_dim(by_core, 1 - core, 1, keepdims=False)
-    chip_sum = mine + lax.ppermute(other, "ctx", core_pairs(shards))
-    total = lax.dynamic_index_in_dim(chip_sum, chip, 0, keepdims=False)
+    tree = jax.tree.map
+
+    def split(x):
+        return x.reshape((chips, 2) + x.shape[1:])
+
+    by_core = tree(split, partials)
+    mine = tree(lambda x: lax.dynamic_index_in_dim(x, core, 1, keepdims=False), by_core)
+    other = tree(lambda x: lax.dynamic_index_in_dim(x, 1 - core, 1, keepdims=False), by_core)
+    chip_sum = tree(jnp.add, mine, lax.ppermute(other, "ctx", core_pairs(shards)))
+    total = tree(lambda x: lax.dynamic_index_in_dim(x, chip, 0, keepdims=False), chip_sum)
     for step in range(1, chips):
-        send = lax.dynamic_index_in_dim(chip_sum, (chip + step) % chips, 0, keepdims=False)
-        total = total + lax.ppermute(send, "ctx", shift_pairs(shards, step))
-    rounded = total.astype(jnp.bfloat16)
+        send = tree(
+            lambda x: lax.dynamic_index_in_dim(x, (chip + step) % chips, 0, keepdims=False),
+            chip_sum,
+        )
+        total = tree(jnp.add, total, lax.ppermute(send, "ctx", shift_pairs(shards, step)))
+    rounded = tree(lambda x: x.astype(jnp.bfloat16), total)
     got = [rounded] + [
         lax.ppermute(rounded, "ctx", shift_pairs(shards, step)) for step in range(1, chips)
     ]
-    by_shift = jnp.stack(got)
-    by_chip = jnp.take(by_shift, (chip - jnp.arange(chips)) % chips, axis=0)
-    pair = jnp.stack([by_chip, lax.ppermute(by_chip, "ctx", core_pairs(shards))], axis=1)
-    return pick_core(pair, core).reshape(shards, -1)
+    order = (chip - jnp.arange(chips)) % chips
+    by_chip = tree(lambda *xs: jnp.take(jnp.stack(xs), order, axis=0), *got)
+    partner = lax.ppermute(by_chip, "ctx", core_pairs(shards))
+
+    def join(x, y):
+        pair = pick_core(jnp.stack([x, y], axis=1), core)
+        return pair.reshape((shards,) + pair.shape[2:])
+
+    return tree(join, by_chip, partner)
 
 
 def merge(parts, sums_width):
@@ -199,7 +213,6 @@
         * send_scales.astype(jnp.float32)[:, :, None, :, None]
     ).astype(jnp.bfloat16).reshape((shards, capacity, 2, block_len, kv_width))
     send_blocks = lax.optimization_barrier(send_blocks)
-    got_blocks = lax.all_to_all(send_blocks, "ctx", split_axis=0, concat_axis=0, tiled=True)
     ctx_dev = per_dev * block_len
     slot_valid = jnp.any(chosen, axis=1)
     slot_block = jnp.sum(jnp.where(chosen, positions[None, :, None], 0), axis=1)
@@ -215,19 +228,23 @@
     width_part = pieces.shape[1]
     arranged = pieces.reshape(shards, row_count, width_part)
     question_part = arranged[:, :q_rows, :].reshape(shards * q_rows, width_part)
-    kv_weight = w_keyval.reshape(w_keyval.shape[0], 2 * kv_width)
     query_part = jnp.dot(question_part, w_query, preferred_element_type=jnp.float32)
-    kv_part = jnp.dot(pieces, kv_weight, preferred_element_type=jnp.float32)
-
-    q_size = q_rows * q_width
-    partials = jnp.concatenate(
-        [query_part.reshape(shards, q_size), kv_part.reshape(shards, row_count * 2 * kv_width)],
-        axis=1,
-    )
-    gathered = hier_reduce_gather(partials, shards, own_index)
-    summed = lax.dynamic_index_in_dim(gathered, own_index, 0, keepdims=False)
-    every_query = gathered[:, :q_size].reshape(shards * q_rows, q_width)
-    every_kv = gathered[:, q_size:].reshape(shards, row_count, 2, kv_width)
+    kv_part = jnp.einsum("tk,kcn->tcn", pieces, w_keyval, preferred_element_type=jnp.float32)
+
+    every_query, every_kv = hier_reduce_gather(
+        (
+            query_part.reshape(shards, q_rows, q_width),
+            kv_part.reshape(shards, row_count, 2, kv_width),
+        ),
+        shards,
+        own_index,
+    )
+    send_later, every_query, every_kv = lax.optimization_barrier(
+        (send_blocks, every_query, every_kv)
+    )
+    got_blocks = lax.all_to_all(send_later, "ctx", split_axis=0, concat_axis=0, tiled=True)
+    every_query = every_query.reshape(shards * q_rows, q_width)
+    own_kv = lax.dynamic_index_in_dim(every_kv, own_index, 0, keepdims=False)
     recomp_kv = every_kv[:, q_rows:].reshape(shards * r_rows, 2, kv_width)
 
     own_owner = lax.dynamic_index_in_dim(owners, own_index, 0, keepdims=False)
@@ -249,7 +266,6 @@
 
     replaced = jnp.any(recomp_pos[None, :] == slot_pos[:, None], axis=1)
     ctx_bias = jnp.where((slot_pos >= 0) & ~replaced, 0.0, neg_large).astype(jnp.float32)[None, :]
-    own_kv = summed[q_size:].reshape(row_count, 2, kv_width)
     own_row = jnp.arange(row_count)
     key_rank = jnp.where(own_row < q_rows, own_index * q_rows + own_row, -1).astype(jnp.int32)[None, :]
 

time: 170 us -> 170 us (level)
  waiting for transfers between devices: 47.1 us -> 72.3 us
  local copies, waits for them, and re-layouts: 43.4 us -> 22.2 us
  other arithmetic: 28 us -> 22.4 us
  starting transfers between devices: 13.3 us -> 15.5 us
    ppermute x1, waiting for transfers between devices: 0.69 us -> 47.4 us  [hier_combine(): parts.append(lax.ppermute(send, 'ctx', shift_pairs(shards, step)))]
    ppermute x3 -> x6, waiting for transfers between devices: 37.3 us -> 10.1 us  [the longest x2 7.79 us: hier_reduce_gather(): lax.ppermute(send, 'ctx', shift_pairs(shards, step))]
    unnamed x31 -> x21, local copies, waits for them, and re-layouts: 12 us -> 4.61 us
    dynamic_slice x2 -> x0, local copies, waits for them, and re-layouts: 3.3 us -> none  [the longest x1 2.5 us: hier_reduce_gather(): mine = lax.dynamic_index_in_dim(by_core, core, 1, keepdims=False)]
    concatenate x3 -> x0, local copies, waits for them, and re-layouts: 3.02 us -> none  [body(): jnp.concatenate([query_part.reshape(shards, q_size), kv_part.reshape(shar...]
    gather x3 -> x4, local copies, waits for them, and re-layouts: 3.91 us -> 1.22 us  [pick_core(): return jnp.take(pair, jnp.arange(2) ^ core, axis=1)]
    all_to_all x1, waiting for transfers between devices: 3.32 us -> 5.89 us  [body(): lax.all_to_all(normed, 'ctx', split_axis=1, concat_axis=0, tiled=True)]
    another operation x2 -> x4, other arithmetic: 2.34 us -> 0.13 us  [the longest x2 0.09 us: join(): pair = pick_core(jnp.stack([x, y], axis=1), core)]
  transfers between devices with their start and end apart: 8 -> 12, of which waited for: 6 -> 9; matrix products, arithmetic and copies ran while one was open for 41% -> 16% of each run, Pallas kernels for 14% -> 0%
where the time goes in v7:
time: 170 us
  waiting for transfers between devices  72.3 us (43%)
  Pallas kernels  24.5 us (14%)
  other arithmetic  22.4 us (13%)
  local copies, waits for them, and re-layouts  22.2 us (13%)
  starting transfers between devices  15.5 us (9%)
  matrix products  11.5 us (7%)
    ppermute x1, waiting for transfers between devices, hier_combine(): parts.append(lax.ppermute(send, 'ctx', shift_pairs(shards, step)))  47.4 us
    pallas_call x1, Pallas kernels, attend(): pl.pallas_call(functools.partial(attn_kernel, score_scale=score_scale), g...  24.5 us
    ppermute x2, waiting for transfers between devices, hier_reduce_gather(): lax.ppermute(send, 'ctx', shift_pairs(shards, step))  7.79 us
    ppermute x2, waiting for transfers between devices, hier_reduce_gather(): lax.ppermute(rounded, 'ctx', shift_pairs(shards, step))  6.97 us
    convert_element_type x1, other arithmetic, body(): send_blocks = (send_codes.astype(jnp.float32).reshape(shards * capacity,...  6.12 us
    all_to_all x1, waiting for transfers between devices, body(): lax.all_to_all(normed, 'ctx', split_axis=1, concat_axis=0, tiled=True)  5.89 us
    all_to_all x1, starting transfers between devices, body(): lax.all_to_all(send_later, 'ctx', split_axis=0, concat_axis=0, tiled=True)  5.17 us
    dot_general x1, matrix products, body(): jnp.dot(question_part, w_query, preferred_element_type=jnp.float32)  4.63 us
  transfers between devices with their start and end apart: 12, of which 9 were waited for; matrix products, arithmetic and copies ran while one was open for 16% of the time, Pallas kernels for 0%

profile of v7, /device:TPU:0, one launch (start us, length us, event | category | flops | bytes accessed | tf_op | source)
XLA Modules:
  0.0 169.7 jit_solution(373262704881354574)
XLA Ops:
  1.5 1.7 fusion.4
  6.4 4.5 %all-to-all-start = ((bf16[96,4,2048]{2,0,1:T(8,128)(2,1)}), bf16[96,4,2048]{2,0,1:T(8,128)(2,1)}, u32[]{:S(2)}, u32[]{:S(2)}) async-start(bf16[96,4,2048]{2,0,1:T(8,128)(2,1)} %bitcast.137), calls=%async_computation | async-start | bytes 3145728 | tf_op jit(solution)/shard_map/all_to_all | solution.py:227
  16.2 2.8 %gather_fusion = bf16[64,2,64,256]{3,2,1,0:T(8,128)(2,1)} fusion(bf16[48,2,64,256]{3,2,1,0:T(8,128)(2,1)S(1)} %copy-done, s32[1024]{0:T(1024)S(1)} %pad_clamp_fusion.3), kind=kCustom, calls=%fused_computation | custom fusion | bytes 8388864 | tf_op jit(solution)/shard_map/jit(_take)/gather | solution.py:209
  19.0 6.1 %multiply_convert_fusion = bf16[4,16,2,64,256]{4,3,2,1,0:T(8,128)(2,1)} fusion(f32[4,16,2,256]{3,2,1,0:T(2,128)S(1)} %mul.153, bf16[4,16,2,64,256]{4,3,2,1,0:T(8,128)(2,1)} %bitcast.135, pred[4,16]{1,0:T(4,128)(4,1)S(1)} %compare_and_fusion.4), kind=kLoop, calls=%fused_computation.9 | loop fusion | flops 8388608 | bytes 8519744 | tf_op jit(solution)/shard_map/convert_element_type | solution.py:214
  25.8 5.9 %all-to-all-done = bf16[96,4,2048]{2,0,1:T(8,128)(2,1)} async-done(((bf16[96,4,2048]{2,0,1:T(8,128)(2,1)}), bf16[96,4,2048]{2,0,1:T(8,128)(2,1)}, u32[]{:S(2)}, u32[]{:S(2)}) %all-to-all-start) | async-done | bytes 1572896 | tf_op jit(solution)/shard_map/all_to_all | solution.py:227
  32.8 3.0 %fusion.7 = f32[2,2,96,2,256]{4,2,3,1,0:T(8,128)S(1)} fusion(bf16[2,2,96,2048,1]{3,2,4,1,0:T(8,128)(2,1)} %bitcast.21, bf16[2048,2,256,1,1]{2,1,0,4,3:T(2,128)(2,1)} %bitcast.158), kind=kOutput, calls=%fused_computation.19 | convolution fusion | flops 805306368 | bytes 4456448 | tf_op jit(solution)/shard_map/tk,kcn->tcn/dot_general | solution.py:232
  35.9 4.6 %fusion = f32[2,2,32,2048]{3,2,1,0:T(8,128)S(1)} fusion(bf16[2,2,32,2048]{3,2,1,0:T(8,128)(2,1)S(1)} %bitcast.139, bf16[2048,2048]{1,0:T(8,128)(2,1)} %param.13), kind=kOutput, calls=%fused_computation.7 | convolution fusion | flops 1073741824 | bytes 9961472 | tf_op jit(solution)/shard_map/dot_general | solution.py:231
  43.9 4.8 %collective-permute-done.5 = f32[96,2,256]{2,0,1:T(8,128)S(1)} collective-permute-done((f32[96,2,256]{2,0,1:T(8,128)S(1)}, f32[96,2,256]{2,0,1:T(8,128)S(1)}, u32[]{:S(2)}, u32[]{:S(2)}) %collective-permute-start.5) | collective-permute-done | bytes 196640 | tf_op jit(solution)/shard_map/ppermute | solution.py:125
  49.2 1.8 %collective-permute-start.1 = (f32[32,2048]{1,0:T(8,128)S(1)}, f32[32,2048]{1,0:T(8,128)S(1)}, u32[]{:S(2)}, u32[]{:S(2)}) collective-permute-start(f32[32,2048]{1,0:T(8,128)S(1)} %dynamic-slice_bitcast_fusion.6), channel_id=1, source_target_pairs={{0,8},{4,12},{8,0},{12,4},{1,9},{5,13},{9,1},{13,5},{2,10},{6,14},... | collective-permute-start | bytes 786440 | tf_op jit(solution)/shard_map/ppermute | solution.py:125
  51.0 3.6 %collective-permute-done.6 = bf16[96,2,256]{2,0,1:T(8,128)(2,1)S(1)} collective-permute-done((bf16[96,2,256]{2,0,1:T(8,128)(2,1)S(1)}, bf16[96,2,256]{2,0,1:T(8,128)(2,1)S(1)}, u32[]{:S(2)}, u32[]{:S(2)}) %collective-permute-start.6) | collective-permute-done | bytes 98336 | tf_op jit(solution)/shard_map/ppermute | solution.py:128
  55.4 3.0 %collective-permute-done.1 = f32[32,2048]{1,0:T(8,128)S(1)} collective-permute-done((f32[32,2048]{1,0:T(8,128)S(1)}, f32[32,2048]{1,0:T(8,128)S(1)}, u32[]{:S(2)}, u32[]{:S(2)}) %collective-permute-start.1) | collective-permute-done | bytes 262176 | tf_op jit(solution)/shard_map/ppermute | solution.py:125
  60.0 3.4 %collective-permute-done.2 = bf16[32,2048]{1,0:T(8,128)(2,1)S(1)} collective-permute-done((bf16[32,2048]{1,0:T(8,128)(2,1)S(1)}, bf16[32,2048]{1,0:T(8,128)(2,1)S(1)}, u32[]{:S(2)}, u32[]{:S(2)}) %collective-permute-start.2) | collective-permute-done | bytes 131104 | tf_op jit(solution)/shard_map/ppermute | solution.py:128
  64.3 1.4 collective-permute-done.3
  68.0 24.5 %shard_map.113 = (f32[128,2048]{1,0:T(8,128)}, f32[16,128,1]{2,1,0:T(8,128)}, f32[16,128,1]{2,1,0:T(8,128)}) custom-call(f32[1,4096]{1,0:T(1,128)} %and_select_fusion.bias_ref, s32[1,96]{1,0:T(1,128)} %compare_select_fusion.13.rank_ref, bf16[128,2048]{1,0:T(8,128)(2,1)} %bitcast.140, bf16[64,128,256]{2,1,0:T(8,128)(2,1)} %bitcast.133, ...), custom_call_target="tpu_custom_call" | custom-call | tf_op jit(solution)/shard_map/pallas_call | solution.py:68
  92.4 1.6 reduce.1
  94.1 1.6 reduce.2
  95.8 5.2 %all-to-all-start.1 = ((bf16[4,16,2,64,256]{4,3,2,1,0:T(8,128)(2,1)}), bf16[4,16,2,64,256]{4,3,2,1,0:T(8,128)(2,1)}, u32[]{:S(2)}, u32[]{:S(2)}) async-start(bf16[4,16,2,64,256]{4,3,2,1,0:T(8,128)(2,1)} %multiply_convert_fusion), calls=%async_computation.1 | async-start | bytes 8388608 | tf_op jit(solution)/shard_map/all_to_all | solution.py:245
  102.4 2.0 %collective-permute-done.8 = f32[2,32,2080]{2,1,0:T(8,128)S(1)} collective-permute-done((f32[2,32,2080]{2,1,0:T(8,128)}, f32[2,32,2080]{2,1,0:T(8,128)S(1)}, u32[]{:S(2)}, u32[]{:S(2)}) %collective-permute-start.8) | collective-permute-done | bytes 532512 | tf_op jit(solution)/shard_map/ppermute | solution.py:165
  105.3 1.7 %collective-permute-start.9 = (f32[32,2080]{1,0:T(8,128)S(1)}, f32[32,2080]{1,0:T(8,128)S(1)}, u32[]{:S(2)}, u32[]{:S(2)}) collective-permute-start(f32[32,2080]{1,0:T(8,128)S(1)} %get-tuple-element.36), channel_id=1, source_target_pairs={{0,8},{4,12},{8,0},{12,4},{1,9},{5,13},{9,1},{13,5},{2,10},{6,14},... | collective-permute-start | bytes 798728 | tf_op jit(solution)/shard_map/ppermute | solution.py:169
  107.5 47.4 %collective-permute-done.9 = f32[32,2080]{1,0:T(8,128)S(1)} collective-permute-done((f32[32,2080]{1,0:T(8,128)S(1)}, f32[32,2080]{1,0:T(8,128)S(1)}, u32[]{:S(2)}, u32[]{:S(2)}) %collective-permute-start.9) | collective-permute-done | bytes 266272 | tf_op jit(solution)/shard_map/ppermute | solution.py:169
  156.3 2.9 %gather_fusion.6 = bf16[32,2,64,256]{3,2,1,0:T(8,128)(2,1)S(1)} fusion(bf16[64,2,64,256]{3,2,1,0:T(8,128)(2,1)} %bitcast.52, s32[1024]{0:T(1024)S(1)} %pad_clamp_fusion), kind=kCustom, calls=%fused_computation.6 | custom fusion | bytes 4194432 | tf_op jit(solution)/shard_map/jit(_take)/gather | solution.py:253
  159.5 2.4 %copy.56 = bf16[2,2048,256]{1,2,0:T(8,128)(2,1)} copy(bf16[2,2048,256]{2,1,0:T(8,128)(2,1)S(1)} %bitcast.136) | data formatting | bytes 4194304 | tf_op jit(solution)/shard_map/reshape | solution.py:256
  161.9 3.9 %fusion.3 = bf16[2,2048,256]{1,2,0:T(8,128)(2,1)} fusion(bf16[2,2048,256]{1,2,0:T(8,128)(2,1)} %copy.56, bf16[256,2,256]{2,0,1:T(8,128)(2,1)S(1)} %bitcast.151, pred[2048]{0:T(1024)(128)(4,1)S(1)} %fusion.10, s32[256]{0:T(256)S(1)} %broadcast_subtract_fusion), kind=kOutput, calls=%fused_computation.13 | convolution fusion | flops 539492352 | bytes 4459520 | tf_op jit(solution)/shard_map/pi,ick->cpk/dot_general | solution.py:262
  165.8 3.9 %copy.57 = bf16[2,2048,256]{2,1,0:T(8,128)(2,1)} copy(bf16[2,2048,256]{1,2,0:T(8,128)(2,1)} %fusion.3) | data formatting | bytes 4194304
  (129 shorter events, 24.9 us)
Async XLA Ops:
  0.6 15.6 %copy-start = (bf16[48,2,64,256]{3,2,1,0:T(8,128)(2,1)S(1)}, bf16[48,2,64,256]{3,2,1,0:T(8,128)(2,1)}, u32[]{:S(2)}) copy-start(bf16[48,2,64,256]{3,2,1,0:T(8,128)(2,1)} %param.15) | copy-start | bytes 9437188
  0.6 3.8 %copy-start.2 = (bf16[64,8192]{1,0:T(8,128)(2,1)S(1)}, bf16[64,8192]{1,0:T(8,128)(2,1)}, u32[]{:S(2)}) copy-start(bf16[64,8192]{1,0:T(8,128)(2,1)} %param.11) | copy-start | bytes 3145732
  0.7 4.2 %copy-start.3 = (bf16[32,8192]{1,0:T(8,128)(2,1)S(1)}, bf16[32,8192]{1,0:T(8,128)(2,1)}, u32[]{:S(2)}) copy-start(bf16[32,8192]{1,0:T(8,128)(2,1)} %param.10) | copy-start | bytes 1572868
  6.4 4.6 %copy-start.7 = (s32[128]{0:T(128)S(1)}, s32[128]{0:T(128)}, u32[]{:S(2)}) copy-start(s32[128]{0:T(128)} %param.18) | copy-start | bytes 1540
  6.4 5.2 %copy-start.8 = (s32[128,1]{0,1:T(1,128)S(1)}, s32[128,1]{0,1:T(1,128)}, u32[]{:S(2)}) copy-start(s32[128,1]{0,1:T(1,128)} %param.17) | copy-start | bytes 1540
  6.4 7.2 %copy-start.5 = (s32[256]{0:T(256)S(1)}, s32[256]{0:T(256)}, u32[]{:S(2)}) copy-start(s32[256]{0:T(256)} %param.19) | copy-start | bytes 3076
  6.4 8.5 %copy-start.6 = (bf16[48,2,2]{0,2,1:T(2,128)(2,1)S(1)}, bf16[48,2,2]{0,2,1:T(2,128)(2,1)}, u32[]{:S(2)}) copy-start(bf16[48,2,2]{0,2,1:T(2,128)(2,1)} %param.16) | copy-start | bytes 1156
  6.4 25.3 %all-to-all-start = ((bf16[96,4,2048]{2,0,1:T(8,128)(2,1)}), bf16[96,4,2048]{2,0,1:T(8,128)(2,1)}, u32[]{:S(2)}, u32[]{:S(2)}) async-start(bf16[96,4,2048]{2,0,1:T(8,128)(2,1)} %bitcast.137), calls=%async_computation | async-start | bytes 3145728 | tf_op jit(solution)/shard_map/all_to_all | solution.py:227
  35.8 5.9 %collective-permute-start.4 = (f32[2,96,2,256]{3,1,2,0:T(8,128)S(1)}, f32[2,96,2,256]{3,1,2,0:T(8,128)S(1)}, u32[]{:S(2)}, u32[]{:S(2)}) collective-permute-start(f32[2,96,2,256]{3,1,2,0:T(8,128)S(1)} %dynamic-slice_bitcast_fusion.3), channel_id=1, source_target_pairs={{0,4},{4,0},{8,12},{12,8},{1,5},{5,1},{9,13},{13,9},{2,6},{6,2},{1... | collective-permute-start | bytes 1179656 | tf_op jit(solution)/shard_map/ppermute | solution.py:118
  40.6 2.2 %collective-permute-start = (f32[2,32,2048]{2,1,0:T(8,128)S(1)}, f32[2,32,2048]{2,1,0:T(8,128)}, u32[]{:S(2)}, u32[]{:S(2)}) collective-permute-start(f32[2,32,2048]{2,1,0:T(8,128)S(1)} %dynamic-slice_bitcast_fusion.2), channel_id=1, source_target_pairs={{0,4},{4,0},{8,12},{12,8},{1,5},{5,1},{9,13},{13,9},{2,6},{6,2},{1... | collective-permute-start | bytes 1572872 | tf_op jit(solution)/shard_map/ppermute | solution.py:118
  41.9 6.9 %collective-permute-start.5 = (f32[96,2,256]{2,0,1:T(8,128)S(1)}, f32[96,2,256]{2,0,1:T(8,128)S(1)}, u32[]{:S(2)}, u32[]{:S(2)}) collective-permute-start(f32[96,2,256]{2,0,1:T(8,128)S(1)} %dynamic-slice_bitcast_fusion.7), channel_id=1, source_target_pairs={{0,8},{4,12},{8,0},{12,4},{1,9},{5,13},{9,1},{13,5},{2,10},{6,14},... | collective-permute-start | bytes 589832 | tf_op jit(solution)/shard_map/ppermute | solution.py:125
  48.8 5.7 %collective-permute-start.6 = (bf16[96,2,256]{2,0,1:T(8,128)(2,1)S(1)}, bf16[96,2,256]{2,0,1:T(8,128)(2,1)S(1)}, u32[]{:S(2)}, u32[]{:S(2)}) collective-permute-start(bf16[96,2,256]{2,0,1:T(8,128)(2,1)S(1)} %fusion.22), channel_id=1, source_target_pairs={{0,8},{4,12},{8,0},{12,4},{1,9},{5,13},{9,1},{13,5},{2,10},{6,14},... | collective-permute-start | bytes 294920 | tf_op jit(solution)/shard_map/ppermute | solution.py:128
  49.2 9.2 %collective-permute-start.1 = (f32[32,2048]{1,0:T(8,128)S(1)}, f32[32,2048]{1,0:T(8,128)S(1)}, u32[]{:S(2)}, u32[]{:S(2)}) collective-permute-start(f32[32,2048]{1,0:T(8,128)S(1)} %dynamic-slice_bitcast_fusion.6), channel_id=1, source_target_pairs={{0,8},{4,12},{8,0},{12,4},{1,9},{5,13},{9,1},{13,5},{2,10},{6,14},... | collective-permute-start | bytes 786440 | tf_op jit(solution)/shard_map/ppermute | solution.py:125
  55.2 4.0 %collective-permute-start.7 = (bf16[2,96,2,256]{3,1,2,0:T(8,128)(2,1)S(1)}, bf16[2,96,2,256]{3,1,2,0:T(8,128)(2,1)S(1)}, u32[]{:S(2)}, u32[]{:S(2)}) collective-permute-start(bf16[2,96,2,256]{3,1,2,0:T(8,128)(2,1)S(1)} %broadcast_select_fusion.1), channel_id=1, source_target_pairs={{0,4},{4,0},{8,12},{12,8},{1,5},{5,1},{9,13},{13,9},{2,6},{6,2},{1... | collective-permute-start | bytes 589832 | tf_op jit(solution)/shard_map/ppermute | solution.py:132
  58.4 5.0 %collective-permute-start.2 = (bf16[32,2048]{1,0:T(8,128)(2,1)S(1)}, bf16[32,2048]{1,0:T(8,128)(2,1)S(1)}, u32[]{:S(2)}, u32[]{:S(2)}) collective-permute-start(bf16[32,2048]{1,0:T(8,128)(2,1)S(1)} %fusion.20), channel_id=1, source_target_pairs={{0,8},{4,12},{8,0},{12,4},{1,9},{5,13},{9,1},{13,5},{2,10},{6,14},... | collective-permute-start | bytes 393224 | tf_op jit(solution)/shard_map/ppermute | solution.py:128
  64.1 1.6 collective-permute-start.3
  95.8 5.2 %copy-start.4 = (f32[128,2048]{1,0:T(8,128)S(1)}, f32[128,2048]{1,0:T(8,128)}, u32[]{:S(2)}) copy-start(f32[128,2048]{1,0:T(8,128)} %get-tuple-element.10) | copy-start | bytes 3145732
  95.8 60.4 %all-to-all-start.1 = ((bf16[4,16,2,64,256]{4,3,2,1,0:T(8,128)(2,1)}), bf16[4,16,2,64,256]{4,3,2,1,0:T(8,128)(2,1)}, u32[]{:S(2)}, u32[]{:S(2)}) async-start(bf16[4,16,2,64,256]{4,3,2,1,0:T(8,128)(2,1)} %multiply_convert_fusion), calls=%async_computation.1 | async-start | bytes 8388608 | tf_op jit(solution)/shard_map/all_to_all | solution.py:245
  102.1 2.3 %collective-permute-start.8 = (f32[2,32,2080]{2,1,0:T(8,128)}, f32[2,32,2080]{2,1,0:T(8,128)S(1)}, u32[]{:S(2)}, u32[]{:S(2)}) collective-permute-start(f32[2,32,2080]{2,1,0:T(8,128)} %get-tuple-element.34), channel_id=1, source_target_pairs={{0,4},{4,0},{8,12},{12,8},{1,5},{5,1},{9,13},{13,9},{2,6},{6,2},{1... | collective-permute-start | bytes 1597448 | tf_op jit(solution)/shard_map/ppermute | solution.py:165
  105.3 49.5 %collective-permute-start.9 = (f32[32,2080]{1,0:T(8,128)S(1)}, f32[32,2080]{1,0:T(8,128)S(1)}, u32[]{:S(2)}, u32[]{:S(2)}) collective-permute-start(f32[32,2080]{1,0:T(8,128)S(1)} %get-tuple-element.36), channel_id=1, source_target_pairs={{0,8},{4,12},{8,0},{12,4},{1,9},{5,13},{9,1},{13,5},{2,10},{6,14},... | collective-permute-start | bytes 798728 | tf_op jit(solution)/shard_map/ppermute | solution.py:169
  161.9 7.8 %copy-start.1 = (bf16[48,2,64,256]{3,2,1,0:T(8,128)(2,1)S(1)}, bf16[48,2,64,256]{3,2,1,0:T(8,128)(2,1)}, u32[]{:S(2)}) copy-start(bf16[48,2,64,256]{3,2,1,0:T(8,128)(2,1)} %param.15) | copy-start | bytes 9437188

commit v8 on v7

--- a/solution.py
+++ b/solution.py
@@ -20,40 +20,38 @@
     return (floats * factor * norm_gain.astype(jnp.float32)).astype(jnp.bfloat16)
 
 
-def attn_kernel(
-    bias_ref, rank_ref, q_ref, kc_ref, kq_ref, vc_ref, vq_ref, o_ref, m_ref, l_ref, *, score_scale
-):
-    tq = q_ref.shape[0]
-    first = pl.program_id(0) * tq
-    dims = (((1,), (1,)), ((), ()))
-    queries = q_ref[...]
+def attn_kernel(bias_ref, rank_ref, q_ref, kc_ref, kq_ref, vc_ref, vq_ref, o_ref, m_ref, l_ref, *, score_scale, group):
     slots, block_len, width = kc_ref.shape
     ctx_keys = kc_ref[...].reshape(slots * block_len, width)
     ctx_vals = vc_ref[...].reshape(slots * block_len, width)
-    ctx_scores = (
-        lax.dot_general(queries, ctx_keys, dims, preferred_element_type=jnp.float32)
-        * score_scale
-        + bias_ref[...]
-    )
-    own_scores = (
-        lax.dot_general(queries, kq_ref[...], dims, preferred_element_type=jnp.float32)
-        * score_scale
-    )
-    token = first + lax.broadcasted_iota(jnp.int32, own_scores.shape, 0)
+    own_keys = kq_ref[...]
+    own_vals = vq_ref[...]
+    bias = bias_ref[...]
+    dims = (((1,), (1,)), ((), ()))
+    tq = q_ref.shape[0]
+    first = pl.program_id(0) * tq
+    token = first + lax.broadcasted_iota(jnp.int32, (tq, own_keys.shape[0]), 0)
     shown = rank_ref[...] <= token
-    own_masked = jnp.where(shown, own_scores, neg_large)
-    row_max = jnp.maximum(
-        jnp.max(ctx_scores, axis=1, keepdims=True), jnp.max(own_masked, axis=1, keepdims=True)
-    )
-    ctx_weights = jnp.exp(ctx_scores - row_max)
-    own_weights = jnp.where(shown, jnp.exp(own_masked - row_max), 0.0)
-    m_ref[...] = row_max
-    l_ref[...] = jnp.sum(ctx_weights, axis=1, keepdims=True) + jnp.sum(
-        own_weights, axis=1, keepdims=True
-    )
-    o_ref[...] = jnp.dot(
-        ctx_weights.astype(jnp.bfloat16), ctx_vals, preferred_element_type=jnp.float32
-    ) + jnp.dot(own_weights.astype(jnp.bfloat16), vq_ref[...], preferred_element_type=jnp.float32)
+    for g in range(group):
+        queries = q_ref[:, g * HD : (g + 1) * HD]
+        cs = (
+            lax.dot_general(queries, ctx_keys, dims, preferred_element_type=jnp.float32)
+            * score_scale
+            + bias
+        )
+        os_ = (
+            lax.dot_general(queries, own_keys, dims, preferred_element_type=jnp.float32)
+            * score_scale
+        )
+        om = jnp.where(shown, os_, neg_large)
+        mx = jnp.maximum(jnp.max(cs, axis=1, keepdims=True), jnp.max(om, axis=1, keepdims=True))
+        cw = jnp.exp(cs - mx)
+        ow = jnp.where(shown, jnp.exp(om - mx), 0.0)
+        m_ref[g] = mx
+        l_ref[g] = jnp.sum(cw, axis=1, keepdims=True) + jnp.sum(ow, axis=1, keepdims=True)
+        o_ref[:, g * HD : (g + 1) * HD] = jnp.dot(
+            cw.astype(jnp.bfloat16), ctx_vals, preferred_element_type=jnp.float32
+        ) + jnp.dot(ow.astype(jnp.bfloat16), own_vals, preferred_element_type=jnp.float32)
 
 
 def attend(queries, ctx_blocks, own_keys, own_vals, ctx_bias, key_rank, group_size, score_scale):
@@ -63,24 +61,24 @@
     ctx_count = slots * block_len
     own_count = own_keys.shape[0]
     heads = q_width // HD
+    kvh = heads // group_size
     tq = min(tokens, 128)
-    grid = (tokens // tq, heads)
     return pl.pallas_call(
-        functools.partial(attn_kernel, score_scale=score_scale),
-        grid=grid,
+        functools.partial(attn_kernel, score_scale=score_scale, group=group_size),
+        grid=(tokens // tq, kvh),
         in_specs=[
-            pl.BlockSpec((1, ctx_count), lambda i, n: (0, 0)),
-            pl.BlockSpec((1, own_count), lambda i, n: (0, 0)),
-            pl.BlockSpec((tq, HD), lambda i, n: (i, n)),
-            pl.BlockSpec((slots, block_len, HD), lambda i, n: (0, 0, n // group_size)),
-            pl.BlockSpec((own_count, HD), lambda i, n: (0, n // group_size)),
-            pl.BlockSpec((slots, block_len, HD), lambda i, n: (0, 1, n // group_size)),
-            pl.BlockSpec((own_count, HD), lambda i, n: (0, n // group_size)),
+            pl.BlockSpec((1, ctx_count), lambda i, h: (0, 0)),
+            pl.BlockSpec((1, own_count), lambda i, h: (0, 0)),
+            pl.BlockSpec((tq, HD * group_size), lambda i, h: (i, h)),
+            pl.BlockSpec((slots, block_len, HD), lambda i, h: (0, 0, h)),
+            pl.BlockSpec((own_count, HD), lambda i, h: (0, h)),
+            pl.BlockSpec((slots, block_len, HD), lambda i, h: (0, 1, h)),
+            pl.BlockSpec((own_count, HD), lambda i, h: (0, h)),
         ],
         out_specs=[
-            pl.BlockSpec((tq, HD), lambda i, n: (i, n)),
-            pl.BlockSpec((None, tq, 1), lambda i, n: (n, i, 0)),
-            pl.BlockSpec((None, tq, 1), lambda i, n: (n, i, 0)),
+            pl.BlockSpec((tq, HD * group_size), lambda i, h: (i, h)),
+            pl.BlockSpec((group_size, tq, 1), lambda i, h: (h, i, 0)),
+            pl.BlockSpec((group_size, tq, 1), lambda i, h: (h, i, 0)),
         ],
         out_shape=[
             jax.ShapeDtypeStruct((tokens, q_width), jnp.float32),

time: 170 us -> 166 us (0.976)
  Pallas kernels: 24.5 us -> 20.2 us
    pallas_call x1, Pallas kernels: 24.5 us -> 20.2 us  [attend(): pl.pallas_call(functools.partial(attn_kernel, score_scale=score_scale, gr...]
where the time goes in v8:
time: 166 us
  waiting for transfers between devices  72.3 us (44%)
  other arithmetic  22.4 us (13%)
  local copies, waits for them, and re-layouts  22.2 us (13%)
  Pallas kernels  20.2 us (12%)
  starting transfers between devices  15.5 us (9%)
  matrix products  11.6 us (7%)
    ppermute x1, waiting for transfers between devices, hier_combine(): parts.append(lax.ppermute(send, 'ctx', shift_pairs(shards, step)))  47.4 us
    pallas_call x1, Pallas kernels, attend(): pl.pallas_call(functools.partial(attn_kernel, score_scale=score_scale, gr...  20.2 us
    ppermute x2, waiting for transfers between devices, hier_reduce_gather(): lax.ppermute(send, 'ctx', shift_pairs(shards, step))  7.79 us
    ppermute x2, waiting for transfers between devices, hier_reduce_gather(): lax.ppermute(rounded, 'ctx', shift_pairs(shards, step))  6.97 us
    convert_element_type x1, other arithmetic, body(): send_blocks = (send_codes.astype(jnp.float32).reshape(shards * capacity,...  6.12 us
    all_to_all x1, waiting for transfers between devices, body(): lax.all_to_all(normed, 'ctx', split_axis=1, concat_axis=0, tiled=True)  5.89 us
    all_to_all x1, starting transfers between devices, body(): lax.all_to_all(send_later, 'ctx', split_axis=0, concat_axis=0, tiled=True)  5.21 us
    dot_general x1, matrix products, body(): jnp.dot(question_part, w_query, preferred_element_type=jnp.float32)  4.63 us
  transfers between devices with their start and end apart: 12, of which 9 were waited for; matrix products, arithmetic and copies ran while one was open for 16% of the time, Pallas kernels for 0%

profile of v8, /device:TPU:0, one launch (start us, length us, event | category | flops | bytes accessed | tf_op | source)
XLA Modules:
  0.0 165.5 jit_solution(2521239184060691015)
XLA Ops:
  1.5 1.7 %fusion.4 = f32[64]{0:T(128)S(1)} fusion(bf16[64,8192]{1,0:T(8,128)(2,1)} %param.11), kind=kLoop, calls=%fused_computation.16 | loop fusion | flops 1572800 | bytes 1048832 | tf_op jit(solution)/shard_map/reduce_sum | solution.py:19
  6.4 4.5 %all-to-all-start = ((bf16[96,4,2048]{2,0,1:T(8,128)(2,1)}), bf16[96,4,2048]{2,0,1:T(8,128)(2,1)}, u32[]{:S(2)}, u32[]{:S(2)}) async-start(bf16[96,4,2048]{2,0,1:T(8,128)(2,1)} %bitcast.137), calls=%async_computation | async-start | bytes 3145728 | tf_op jit(solution)/shard_map/all_to_all | solution.py:225
  16.2 2.8 %gather_fusion = bf16[64,2,64,256]{3,2,1,0:T(8,128)(2,1)} fusion(bf16[48,2,64,256]{3,2,1,0:T(8,128)(2,1)S(1)} %copy-done, s32[1024]{0:T(1024)S(1)} %pad_clamp_fusion.3), kind=kCustom, calls=%fused_computation | custom fusion | bytes 8388864 | tf_op jit(solution)/shard_map/jit(_take)/gather | solution.py:207
  19.0 6.1 %multiply_convert_fusion = bf16[4,16,2,64,256]{4,3,2,1,0:T(8,128)(2,1)} fusion(f32[4,16,2,256]{3,2,1,0:T(2,128)S(1)} %mul.153, bf16[4,16,2,64,256]{4,3,2,1,0:T(8,128)(2,1)} %bitcast.135, pred[4,16]{1,0:T(4,128)(4,1)S(1)} %compare_and_fusion.4), kind=kLoop, calls=%fused_computation.9 | loop fusion | flops 8388608 | bytes 8519744 | tf_op jit(solution)/shard_map/convert_element_type | solution.py:212
  25.8 5.9 %all-to-all-done = bf16[96,4,2048]{2,0,1:T(8,128)(2,1)} async-done(((bf16[96,4,2048]{2,0,1:T(8,128)(2,1)}), bf16[96,4,2048]{2,0,1:T(8,128)(2,1)}, u32[]{:S(2)}, u32[]{:S(2)}) %all-to-all-start) | async-done | bytes 1572896 | tf_op jit(solution)/shard_map/all_to_all | solution.py:225
  32.8 3.0 %fusion.7 = f32[2,2,96,2,256]{4,2,3,1,0:T(8,128)S(1)} fusion(bf16[2,2,96,2048,1]{3,2,4,1,0:T(8,128)(2,1)} %bitcast.21, bf16[2048,2,256,1,1]{2,1,0,4,3:T(2,128)(2,1)} %bitcast.158), kind=kOutput, calls=%fused_computation.19 | convolution fusion | flops 805306368 | bytes 4456448 | tf_op jit(solution)/shard_map/tk,kcn->tcn/dot_general | solution.py:230
  35.9 4.6 %fusion = f32[2,2,32,2048]{3,2,1,0:T(8,128)S(1)} fusion(bf16[2,2,32,2048]{3,2,1,0:T(8,128)(2,1)S(1)} %bitcast.139, bf16[2048,2048]{1,0:T(8,128)(2,1)} %param.13), kind=kOutput, calls=%fused_computation.7 | convolution fusion | flops 1073741824 | bytes 9961472 | tf_op jit(solution)/shard_map/dot_general | solution.py:229
  43.9 4.8 %collective-permute-done.5 = f32[96,2,256]{2,0,1:T(8,128)S(1)} collective-permute-done((f32[96,2,256]{2,0,1:T(8,128)S(1)}, f32[96,2,256]{2,0,1:T(8,128)S(1)}, u32[]{:S(2)}, u32[]{:S(2)}) %collective-permute-start.5) | collective-permute-done | bytes 196640 | tf_op jit(solution)/shard_map/ppermute | solution.py:123
  49.2 1.8 %collective-permute-start.1 = (f32[32,2048]{1,0:T(8,128)S(1)}, f32[32,2048]{1,0:T(8,128)S(1)}, u32[]{:S(2)}, u32[]{:S(2)}) collective-permute-start(f32[32,2048]{1,0:T(8,128)S(1)} %dynamic-slice_bitcast_fusion.6), channel_id=1, source_target_pairs={{0,8},{4,12},{8,0},{12,4},{1,9},{5,13},{9,1},{13,5},{2,10},{6,14},... | collective-permute-start | bytes 786440 | tf_op jit(solution)/shard_map/ppermute | solution.py:123
  51.0 3.6 %collective-permute-done.6 = bf16[96,2,256]{2,0,1:T(8,128)(2,1)S(1)} collective-permute-done((bf16[96,2,256]{2,0,1:T(8,128)(2,1)S(1)}, bf16[96,2,256]{2,0,1:T(8,128)(2,1)S(1)}, u32[]{:S(2)}, u32[]{:S(2)}) %collective-permute-start.6) | collective-permute-done | bytes 98336 | tf_op jit(solution)/shard_map/ppermute | solution.py:126
  55.4 3.0 %collective-permute-done.1 = f32[32,2048]{1,0:T(8,128)S(1)} collective-permute-done((f32[32,2048]{1,0:T(8,128)S(1)}, f32[32,2048]{1,0:T(8,128)S(1)}, u32[]{:S(2)}, u32[]{:S(2)}) %collective-permute-start.1) | collective-permute-done | bytes 262176 | tf_op jit(solution)/shard_map/ppermute | solution.py:123
  60.0 3.4 %collective-permute-done.2 = bf16[32,2048]{1,0:T(8,128)(2,1)S(1)} collective-permute-done((bf16[32,2048]{1,0:T(8,128)(2,1)S(1)}, bf16[32,2048]{1,0:T(8,128)(2,1)S(1)}, u32[]{:S(2)}, u32[]{:S(2)}) %collective-permute-start.2) | collective-permute-done | bytes 131104 | tf_op jit(solution)/shard_map/ppermute | solution.py:126
  64.3 1.4 collective-permute-done.3
  68.0 20.2 %shard_map.113 = (f32[128,2048]{1,0:T(8,128)}, f32[16,128,1]{2,1,0:T(8,128)}, f32[16,128,1]{2,1,0:T(8,128)}) custom-call(f32[1,4096]{1,0:T(1,128)} %and_select_fusion.bias_ref, s32[1,96]{1,0:T(1,128)} %compare_select_fusion.13.rank_ref, bf16[128,2048]{1,0:T(8,128)(2,1)} %bitcast.140, bf16[64,128,256]{2,1,0:T(8,128)(2,1)} %bitcast.133, ...), custom_call_target="tpu_custom_call" | custom-call | tf_op jit(solution)/shard_map/pallas_call | solution.py:66
  88.2 1.6 reduce.1
  89.9 1.6 reduce.2
  91.6 5.2 %all-to-all-start.1 = ((bf16[4,16,2,64,256]{4,3,2,1,0:T(8,128)(2,1)}), bf16[4,16,2,64,256]{4,3,2,1,0:T(8,128)(2,1)}, u32[]{:S(2)}, u32[]{:S(2)}) async-start(bf16[4,16,2,64,256]{4,3,2,1,0:T(8,128)(2,1)} %multiply_convert_fusion), calls=%async_computation.1 | async-start | bytes 8388608 | tf_op jit(solution)/shard_map/all_to_all | solution.py:243
  98.2 2.0 %collective-permute-done.8 = f32[2,32,2080]{2,1,0:T(8,128)S(1)} collective-permute-done((f32[2,32,2080]{2,1,0:T(8,128)}, f32[2,32,2080]{2,1,0:T(8,128)S(1)}, u32[]{:S(2)}, u32[]{:S(2)}) %collective-permute-start.8) | collective-permute-done | bytes 532512 | tf_op jit(solution)/shard_map/ppermute | solution.py:163
  101.1 1.7 %collective-permute-start.9 = (f32[32,2080]{1,0:T(8,128)S(1)}, f32[32,2080]{1,0:T(8,128)S(1)}, u32[]{:S(2)}, u32[]{:S(2)}) collective-permute-start(f32[32,2080]{1,0:T(8,128)S(1)} %get-tuple-element.36), channel_id=1, source_target_pairs={{0,8},{4,12},{8,0},{12,4},{1,9},{5,13},{9,1},{13,5},{2,10},{6,14},... | collective-permute-start | bytes 798728 | tf_op jit(solution)/shard_map/ppermute | solution.py:167
  103.2 47.4 %collective-permute-done.9 = f32[32,2080]{1,0:T(8,128)S(1)} collective-permute-done((f32[32,2080]{1,0:T(8,128)S(1)}, f32[32,2080]{1,0:T(8,128)S(1)}, u32[]{:S(2)}, u32[]{:S(2)}) %collective-permute-start.9) | collective-permute-done | bytes 266272 | tf_op jit(solution)/shard_map/ppermute | solution.py:167
  152.0 2.9 %gather_fusion.6 = bf16[32,2,64,256]{3,2,1,0:T(8,128)(2,1)S(1)} fusion(bf16[64,2,64,256]{3,2,1,0:T(8,128)(2,1)} %bitcast.52, s32[1024]{0:T(1024)S(1)} %pad_clamp_fusion), kind=kCustom, calls=%fused_computation.6 | custom fusion | bytes 4194432 | tf_op jit(solution)/shard_map/jit(_take)/gather | solution.py:251
  155.3 2.4 %copy.56 = bf16[2,2048,256]{1,2,0:T(8,128)(2,1)} copy(bf16[2,2048,256]{2,1,0:T(8,128)(2,1)S(1)} %bitcast.136) | data formatting | bytes 4194304 | tf_op jit(solution)/shard_map/reshape | solution.py:254
  157.7 3.9 %fusion.3 = bf16[2,2048,256]{1,2,0:T(8,128)(2,1)} fusion(bf16[2,2048,256]{1,2,0:T(8,128)(2,1)} %copy.56, bf16[256,2,256]{2,0,1:T(8,128)(2,1)S(1)} %bitcast.151, pred[2048]{0:T(1024)(128)(4,1)S(1)} %fusion.10, s32[256]{0:T(256)S(1)} %broadcast_subtract_fusion), kind=kOutput, calls=%fused_computation.13 | convolution fusion | flops 539492352 | bytes 4459520 | tf_op jit(solution)/shard_map/pi,ick->cpk/dot_general | solution.py:260
  161.6 3.9 %copy.57 = bf16[2,2048,256]{2,1,0:T(8,128)(2,1)} copy(bf16[2,2048,256]{1,2,0:T(8,128)(2,1)} %fusion.3) | data formatting | bytes 4194304
  (129 shorter events, 24.9 us)
Async XLA Ops:
  0.6 15.6 %copy-start = (bf16[48,2,64,256]{3,2,1,0:T(8,128)(2,1)S(1)}, bf16[48,2,64,256]{3,2,1,0:T(8,128)(2,1)}, u32[]{:S(2)}) copy-start(bf16[48,2,64,256]{3,2,1,0:T(8,128)(2,1)} %param.15) | copy-start | bytes 9437188
  0.6 3.8 %copy-start.2 = (bf16[64,8192]{1,0:T(8,128)(2,1)S(1)}, bf16[64,8192]{1,0:T(8,128)(2,1)}, u32[]{:S(2)}) copy-start(bf16[64,8192]{1,0:T(8,128)(2,1)} %param.11) | copy-start | bytes 3145732
  0.7 4.2 %copy-start.3 = (bf16[32,8192]{1,0:T(8,128)(2,1)S(1)}, bf16[32,8192]{1,0:T(8,128)(2,1)}, u32[]{:S(2)}) copy-start(bf16[32,8192]{1,0:T(8,128)(2,1)} %param.10) | copy-start | bytes 1572868
  6.4 4.6 %copy-start.7 = (s32[128]{0:T(128)S(1)}, s32[128]{0:T(128)}, u32[]{:S(2)}) copy-start(s32[128]{0:T(128)} %param.18) | copy-start | bytes 1540
  6.4 5.2 %copy-start.8 = (s32[128,1]{0,1:T(1,128)S(1)}, s32[128,1]{0,1:T(1,128)}, u32[]{:S(2)}) copy-start(s32[128,1]{0,1:T(1,128)} %param.17) | copy-start | bytes 1540
  6.4 7.2 %copy-start.5 = (s32[256]{0:T(256)S(1)}, s32[256]{0:T(256)}, u32[]{:S(2)}) copy-start(s32[256]{0:T(256)} %param.19) | copy-start | bytes 3076
  6.4 8.5 %copy-start.6 = (bf16[48,2,2]{0,2,1:T(2,128)(2,1)S(1)}, bf16[48,2,2]{0,2,1:T(2,128)(2,1)}, u32[]{:S(2)}) copy-start(bf16[48,2,2]{0,2,1:T(2,128)(2,1)} %param.16) | copy-start | bytes 1156
  6.4 25.3 %all-to-all-start = ((bf16[96,4,2048]{2,0,1:T(8,128)(2,1)}), bf16[96,4,2048]{2,0,1:T(8,128)(2,1)}, u32[]{:S(2)}, u32[]{:S(2)}) async-start(bf16[96,4,2048]{2,0,1:T(8,128)(2,1)} %bitcast.137), calls=%async_computation | async-start | bytes 3145728 | tf_op jit(solution)/shard_map/all_to_all | solution.py:225
  35.8 5.9 %collective-permute-start.4 = (f32[2,96,2,256]{3,1,2,0:T(8,128)S(1)}, f32[2,96,2,256]{3,1,2,0:T(8,128)S(1)}, u32[]{:S(2)}, u32[]{:S(2)}) collective-permute-start(f32[2,96,2,256]{3,1,2,0:T(8,128)S(1)} %dynamic-slice_bitcast_fusion.3), channel_id=1, source_target_pairs={{0,4},{4,0},{8,12},{12,8},{1,5},{5,1},{9,13},{13,9},{2,6},{6,2},{1... | collective-permute-start | bytes 1179656 | tf_op jit(solution)/shard_map/ppermute | solution.py:116
  40.6 2.2 %collective-permute-start = (f32[2,32,2048]{2,1,0:T(8,128)S(1)}, f32[2,32,2048]{2,1,0:T(8,128)}, u32[]{:S(2)}, u32[]{:S(2)}) collective-permute-start(f32[2,32,2048]{2,1,0:T(8,128)S(1)} %dynamic-slice_bitcast_fusion.2), channel_id=1, source_target_pairs={{0,4},{4,0},{8,12},{12,8},{1,5},{5,1},{9,13},{13,9},{2,6},{6,2},{1... | collective-permute-start | bytes 1572872 | tf_op jit(solution)/shard_map/ppermute | solution.py:116
  41.9 6.9 %collective-permute-start.5 = (f32[96,2,256]{2,0,1:T(8,128)S(1)}, f32[96,2,256]{2,0,1:T(8,128)S(1)}, u32[]{:S(2)}, u32[]{:S(2)}) collective-permute-start(f32[96,2,256]{2,0,1:T(8,128)S(1)} %dynamic-slice_bitcast_fusion.7), channel_id=1, source_target_pairs={{0,8},{4,12},{8,0},{12,4},{1,9},{5,13},{9,1},{13,5},{2,10},{6,14},... | collective-permute-start | bytes 589832 | tf_op jit(solution)/shard_map/ppermute | solution.py:123
  48.8 5.7 %collective-permute-start.6 = (bf16[96,2,256]{2,0,1:T(8,128)(2,1)S(1)}, bf16[96,2,256]{2,0,1:T(8,128)(2,1)S(1)}, u32[]{:S(2)}, u32[]{:S(2)}) collective-permute-start(bf16[96,2,256]{2,0,1:T(8,128)(2,1)S(1)} %fusion.22), channel_id=1, source_target_pairs={{0,8},{4,12},{8,0},{12,4},{1,9},{5,13},{9,1},{13,5},{2,10},{6,14},... | collective-permute-start | bytes 294920 | tf_op jit(solution)/shard_map/ppermute | solution.py:126
  49.2 9.2 %collective-permute-start.1 = (f32[32,2048]{1,0:T(8,128)S(1)}, f32[32,2048]{1,0:T(8,128)S(1)}, u32[]{:S(2)}, u32[]{:S(2)}) collective-permute-start(f32[32,2048]{1,0:T(8,128)S(1)} %dynamic-slice_bitcast_fusion.6), channel_id=1, source_target_pairs={{0,8},{4,12},{8,0},{12,4},{1,9},{5,13},{9,1},{13,5},{2,10},{6,14},... | collective-permute-start | bytes 786440 | tf_op jit(solution)/shard_map/ppermute | solution.py:123
  55.2 4.0 %collective-permute-start.7 = (bf16[2,96,2,256]{3,1,2,0:T(8,128)(2,1)S(1)}, bf16[2,96,2,256]{3,1,2,0:T(8,128)(2,1)S(1)}, u32[]{:S(2)}, u32[]{:S(2)}) collective-permute-start(bf16[2,96,2,256]{3,1,2,0:T(8,128)(2,1)S(1)} %broadcast_select_fusion.1), channel_id=1, source_target_pairs={{0,4},{4,0},{8,12},{12,8},{1,5},{5,1},{9,13},{13,9},{2,6},{6,2},{1... | collective-permute-start | bytes 589832 | tf_op jit(solution)/shard_map/ppermute | solution.py:130
  58.4 5.0 %collective-permute-start.2 = (bf16[32,2048]{1,0:T(8,128)(2,1)S(1)}, bf16[32,2048]{1,0:T(8,128)(2,1)S(1)}, u32[]{:S(2)}, u32[]{:S(2)}) collective-permute-start(bf16[32,2048]{1,0:T(8,128)(2,1)S(1)} %fusion.20), channel_id=1, source_target_pairs={{0,8},{4,12},{8,0},{12,4},{1,9},{5,13},{9,1},{13,5},{2,10},{6,14},... | collective-permute-start | bytes 393224 | tf_op jit(solution)/shard_map/ppermute | solution.py:126
  64.1 1.6 collective-permute-start.3
  91.6 5.2 %copy-start.4 = (f32[128,2048]{1,0:T(8,128)S(1)}, f32[128,2048]{1,0:T(8,128)}, u32[]{:S(2)}) copy-start(f32[128,2048]{1,0:T(8,128)} %get-tuple-element.10) | copy-start | bytes 3145732
  91.6 60.4 %all-to-all-start.1 = ((bf16[4,16,2,64,256]{4,3,2,1,0:T(8,128)(2,1)}), bf16[4,16,2,64,256]{4,3,2,1,0:T(8,128)(2,1)}, u32[]{:S(2)}, u32[]{:S(2)}) async-start(bf16[4,16,2,64,256]{4,3,2,1,0:T(8,128)(2,1)} %multiply_convert_fusion), calls=%async_computation.1 | async-start | bytes 8388608 | tf_op jit(solution)/shard_map/all_to_all | solution.py:243
  97.9 2.2 %collective-permute-start.8 = (f32[2,32,2080]{2,1,0:T(8,128)}, f32[2,32,2080]{2,1,0:T(8,128)S(1)}, u32[]{:S(2)}, u32[]{:S(2)}) collective-permute-start(f32[2,32,2080]{2,1,0:T(8,128)} %get-tuple-element.34), channel_id=1, source_target_pairs={{0,4},{4,0},{8,12},{12,8},{1,5},{5,1},{9,13},{13,9},{2,6},{6,2},{1... | collective-permute-start | bytes 1597448 | tf_op jit(solution)/shard_map/ppermute | solution.py:163
  101.1 49.5 %collective-permute-start.9 = (f32[32,2080]{1,0:T(8,128)S(1)}, f32[32,2080]{1,0:T(8,128)S(1)}, u32[]{:S(2)}, u32[]{:S(2)}) collective-permute-start(f32[32,2080]{1,0:T(8,128)S(1)} %get-tuple-element.36), channel_id=1, source_target_pairs={{0,8},{4,12},{8,0},{12,4},{1,9},{5,13},{9,1},{13,5},{2,10},{6,14},... | collective-permute-start | bytes 798728 | tf_op jit(solution)/shard_map/ppermute | solution.py:167
  157.7 7.8 %copy-start.1 = (bf16[48,2,64,256]{3,2,1,0:T(8,128)(2,1)S(1)}, bf16[48,2,64,256]{3,2,1,0:T(8,128)(2,1)}, u32[]{:S(2)}) copy-start(bf16[48,2,64,256]{3,2,1,0:T(8,128)(2,1)} %param.15) | copy-start | bytes 9437188

commit v9 on v8

--- a/solution.py
+++ b/solution.py
@@ -248,19 +248,19 @@
     own_owner = lax.dynamic_index_in_dim(owners, own_index, 0, keepdims=False)
     own_rank = lax.dynamic_index_in_dim(order_rank, own_index, 0, keepdims=False)
     flat_index = own_owner * capacity + own_rank
-    block_rows = jnp.take(
-        got_blocks.reshape((shards * capacity, 2, block_len, kv_width)), flat_index, axis=0
-    )
-    cached = jnp.transpose(block_rows, (1, 0, 2, 3)).reshape(2, ctx_dev, kv_width)
-
     local_pos = recomp_pos - own_index * ctx_dev
     match = local_pos[None, :] == jnp.arange(ctx_dev)[:, None]
     hit = jnp.any(match, axis=1)
     one_hot = match.astype(jnp.bfloat16)
-    placed = jnp.einsum(
-        "pi,ick->cpk", one_hot, recomp_kv, preferred_element_type=jnp.float32
-    ).astype(jnp.bfloat16)
-    kv_cache = jnp.where(hit[None, :, None], placed, cached)
+    by_slot = got_blocks.reshape((shards * capacity, 2, block_len, kv_width))
+    kv_parts = []
+    for c in range(2):
+        placed = jnp.dot(
+            one_hot, recomp_kv[:, c], preferred_element_type=jnp.float32
+        ).astype(jnp.bfloat16)
+        cached = jnp.take(by_slot[:, c], flat_index, axis=0).reshape(ctx_dev, kv_width)
+        kv_parts.append(jnp.where(hit[:, None], placed, cached))
+    kv_cache = jnp.stack(kv_parts)
 
     replaced = jnp.any(recomp_pos[None, :] == slot_pos[:, None], axis=1)
     ctx_bias = jnp.where((slot_pos >= 0) & ~replaced, 0.0, neg_large).astype(jnp.float32)[None, :]

time: 166 us -> 141 us (0.85)
  waiting for transfers between devices: 72.3 us -> 48.1 us
  other arithmetic: 22.4 us -> 25.2 us
  matrix products: 11.6 us -> 9.17 us
    ppermute x1, waiting for transfers between devices: 47.4 us -> 23.2 us  [hier_combine(): parts.append(lax.ppermute(send, 'ctx', shift_pairs(shards, step)))]
    squeeze x0 -> x1, local copies, waits for them, and re-layouts: none -> 4.14 us  [body(): by_slot[:, c]]
    unnamed x21 -> x20, local copies, waits for them, and re-layouts: 4.61 us -> 0.68 us
    dot_general x1 -> x2, matrix products: 3.88 us -> 1.5 us  [body(): jnp.dot(one_hot, recomp_kv[:, c], preferred_element_type=jnp.float32)]
    reshape x1 -> x0, local copies, waits for them, and re-layouts: 2.38 us -> none  [body(): jnp.transpose(block_rows, (1, 0, 2, 3)).reshape(2, ctx_dev, kv_width)]
    gather x1 -> x2, local copies, waits for them, and re-layouts: 2.87 us -> 3.79 us  [body(): jnp.take(by_slot[:, c], flat_index, axis=0).reshape(ctx_dev, kv_width)]
  transfers between devices with their start and end apart: 12 -> 12, of which waited for: 9 -> 9; matrix products, arithmetic and copies ran while one was open for 16% -> 22% of each run, Pallas kernels for 0% -> 14%
where the time goes in v9:
time: 141 us; the launch traced here: 140 us
  waiting for transfers between devices  48.1 us (34%)
  other arithmetic  25.2 us (18%)
  local copies, waits for them, and re-layouts  20.8 us (15%)
  Pallas kernels  20.1 us (14%)
  starting transfers between devices  15.5 us (11%)
  matrix products  9.17 us (7%)
    ppermute x1, waiting for transfers between devices, hier_combine(): parts.append(lax.ppermute(send, 'ctx', shift_pairs(shards, step)))  23.2 us
    pallas_call x1, Pallas kernels, attend(): pl.pallas_call(functools.partial(attn_kernel, score_scale=score_scale, gr...  20.1 us
    ppermute x2, waiting for transfers between devices, hier_reduce_gather(): lax.ppermute(send, 'ctx', shift_pairs(shards, step))  7.82 us
    ppermute x2, waiting for transfers between devices, hier_reduce_gather(): lax.ppermute(rounded, 'ctx', shift_pairs(shards, step))  6.97 us
    convert_element_type x1, other arithmetic, body(): send_blocks = (send_codes.astype(jnp.float32).reshape(shards * capacity,...  6.13 us
    all_to_all x1, waiting for transfers between devices, body(): lax.all_to_all(normed, 'ctx', split_axis=1, concat_axis=0, tiled=True)  5.89 us
    all_to_all x1, starting transfers between devices, body(): lax.all_to_all(send_later, 'ctx', split_axis=0, concat_axis=0, tiled=True)  5.02 us
    dot_general x1, matrix products, body(): jnp.dot(question_part, w_query, preferred_element_type=jnp.float32)  4.63 us
  transfers between devices with their start and end apart: 12, of which 9 were waited for; matrix products, arithmetic and copies ran while one was open for 22% of the time, Pallas kernels for 14%

profile of v9, /device:TPU:0, one launch (start us, length us, event | category | flops | bytes accessed | tf_op | source)
XLA Modules:
  0.0 140.1 jit_solution(842152919595644390)
XLA Ops:
  1.5 1.7 %fusion.6 = f32[64]{0:T(128)S(1)} fusion(bf16[64,8192]{1,0:T(8,128)(2,1)} %param.13), kind=kLoop, calls=%fused_computation.20 | loop fusion | flops 1572800 | bytes 1048832 | tf_op jit(solution)/shard_map/reduce_sum | solution.py:19
  6.4 4.5 %all-to-all-start = ((bf16[96,4,2048]{2,0,1:T(8,128)(2,1)}), bf16[96,4,2048]{2,0,1:T(8,128)(2,1)}, u32[]{:S(2)}, u32[]{:S(2)}) async-start(bf16[96,4,2048]{2,0,1:T(8,128)(2,1)} %bitcast.138), calls=%async_computation | async-start | bytes 3145728 | tf_op jit(solution)/shard_map/all_to_all | solution.py:225
  16.2 2.8 %gather_fusion = bf16[64,2,64,256]{3,2,1,0:T(8,128)(2,1)} fusion(bf16[48,2,64,256]{3,2,1,0:T(8,128)(2,1)S(1)} %copy-done, s32[1024]{0:T(1024)S(1)} %pad_clamp_fusion.3), kind=kCustom, calls=%fused_computation.2 | custom fusion | bytes 8388864 | tf_op jit(solution)/shard_map/jit(_take)/gather | solution.py:207
  19.0 6.1 %multiply_convert_fusion = bf16[4,16,2,64,256]{4,3,2,1,0:T(8,128)(2,1)} fusion(f32[4,16,2,256]{3,2,1,0:T(2,128)S(1)} %mul.143, bf16[4,16,2,64,256]{4,3,2,1,0:T(8,128)(2,1)} %bitcast.137, pred[4,16]{1,0:T(4,128)(4,1)S(1)} %compare_and_fusion.4), kind=kLoop, calls=%fused_computation.10 | loop fusion | flops 8388608 | bytes 8519744 | tf_op jit(solution)/shard_map/convert_element_type | solution.py:212
  25.8 5.9 %all-to-all-done = bf16[96,4,2048]{2,0,1:T(8,128)(2,1)} async-done(((bf16[96,4,2048]{2,0,1:T(8,128)(2,1)}), bf16[96,4,2048]{2,0,1:T(8,128)(2,1)}, u32[]{:S(2)}, u32[]{:S(2)}) %all-to-all-start) | async-done | bytes 1572896 | tf_op jit(solution)/shard_map/all_to_all | solution.py:225
  32.8 3.0 %fusion.9 = f32[2,2,96,2,256]{4,2,3,1,0:T(8,128)S(1)} fusion(bf16[2,2,96,2048,1]{3,2,4,1,0:T(8,128)(2,1)} %bitcast.21, bf16[2048,2,256,1,1]{2,1,0,4,3:T(2,128)(2,1)} %bitcast.162), kind=kOutput, calls=%fused_computation.26 | convolution fusion | flops 805306368 | bytes 4456448 | tf_op jit(solution)/shard_map/tk,kcn->tcn/dot_general | solution.py:230
  35.9 4.6 %fusion = f32[2,2,32,2048]{3,2,1,0:T(8,128)S(1)} fusion(bf16[2,2,32,2048]{3,2,1,0:T(8,128)(2,1)S(1)} %bitcast.140, bf16[2048,2048]{1,0:T(8,128)(2,1)} %param.15), kind=kOutput, calls=%fused_computation.8 | convolution fusion | flops 1073741824 | bytes 9961472 | tf_op jit(solution)/shard_map/dot_general | solution.py:229
  43.9 4.9 %collective-permute-done.5 = f32[96,2,256]{2,0,1:T(8,128)S(1)} collective-permute-done((f32[96,2,256]{2,0,1:T(8,128)S(1)}, f32[96,2,256]{2,0,1:T(8,128)S(1)}, u32[]{:S(2)}, u32[]{:S(2)}) %collective-permute-start.5) | collective-permute-done | bytes 196640 | tf_op jit(solution)/shard_map/ppermute | solution.py:123
  49.2 1.8 %collective-permute-start.1 = (f32[32,2048]{1,0:T(8,128)S(1)}, f32[32,2048]{1,0:T(8,128)S(1)}, u32[]{:S(2)}, u32[]{:S(2)}) collective-permute-start(f32[32,2048]{1,0:T(8,128)S(1)} %dynamic-slice_bitcast_fusion.6), channel_id=1, source_target_pairs={{0,8},{4,12},{8,0},{12,4},{1,9},{5,13},{9,1},{13,5},{2,10},{6,14},... | collective-permute-start | bytes 786440 | tf_op jit(solution)/shard_map/ppermute | solution.py:123
  51.0 3.6 %collective-permute-done.6 = bf16[96,2,256]{2,0,1:T(8,128)(2,1)S(1)} collective-permute-done((bf16[96,2,256]{2,0,1:T(8,128)(2,1)S(1)}, bf16[96,2,256]{2,0,1:T(8,128)(2,1)S(1)}, u32[]{:S(2)}, u32[]{:S(2)}) %collective-permute-start.6) | collective-permute-done | bytes 98336 | tf_op jit(solution)/shard_map/ppermute | solution.py:126
  55.4 3.0 %collective-permute-done.1 = f32[32,2048]{1,0:T(8,128)S(1)} collective-permute-done((f32[32,2048]{1,0:T(8,128)S(1)}, f32[32,2048]{1,0:T(8,128)S(1)}, u32[]{:S(2)}, u32[]{:S(2)}) %collective-permute-start.1) | collective-permute-done | bytes 262176 | tf_op jit(solution)/shard_map/ppermute | solution.py:123
  60.0 3.4 %collective-permute-done.2 = bf16[32,2048]{1,0:T(8,128)(2,1)S(1)} collective-permute-done((bf16[32,2048]{1,0:T(8,128)(2,1)S(1)}, bf16[32,2048]{1,0:T(8,128)(2,1)S(1)}, u32[]{:S(2)}, u32[]{:S(2)}) %collective-permute-start.2) | collective-permute-done | bytes 131104 | tf_op jit(solution)/shard_map/ppermute | solution.py:126
  67.4 5.0 %all-to-all-start.1 = ((bf16[4,16,2,64,256]{4,3,2,1,0:T(8,128)(2,1)}), bf16[4,16,2,64,256]{4,3,2,1,0:T(8,128)(2,1)}, u32[]{:S(2)}, u32[]{:S(2)}) async-start(bf16[4,16,2,64,256]{4,3,2,1,0:T(8,128)(2,1)} %multiply_convert_fusion), calls=%async_computation.1 | async-start | bytes 8388608 | tf_op jit(solution)/shard_map/all_to_all | solution.py:243
  73.1 20.1 %shard_map.113 = (f32[128,2048]{1,0:T(8,128)}, f32[16,128,1]{2,1,0:T(8,128)}, f32[16,128,1]{2,1,0:T(8,128)}) custom-call(f32[1,4096]{1,0:T(1,128)} %and_select_fusion.bias_ref, s32[1,96]{1,0:T(1,128)} %compare_select_fusion.12.rank_ref, bf16[128,2048]{1,0:T(8,128)(2,1)} %bitcast.141, bf16[64,128,256]{2,1,0:T(8,128)(2,1)} %bitcast.135, ...), custom_call_target="tpu_custom_call" | custom-call | tf_op jit(solution)/shard_map/pallas_call | solution.py:66
  93.1 1.7 %reduce.1 = f32[16,128]{1,0:T(8,128)S(1)} reduce(f32[16,128,1]{2,1,0:T(8,128)} %get-tuple-element.12, f32[]{:T(128)} %constant.215), dimensions={2}, to_apply=%get-tuple-element.12.reduce_sub_computation | reduce | bytes 16388 | tf_op jit(solution)/shard_map/pallas_call | solution.py:66
  94.9 1.6 %reduce.2 = f32[16,128]{1,0:T(8,128)S(1)} reduce(f32[16,128,1]{2,1,0:T(8,128)} %get-tuple-element.13, f32[]{:T(128)} %constant.215), dimensions={2}, to_apply=%get-tuple-element.13.reduce_sub_computation | reduce | bytes 16388 | tf_op jit(solution)/shard_map/pallas_call | solution.py:66
  98.0 1.9 %collective-permute-done.8 = f32[2,32,2080]{2,1,0:T(8,128)S(1)} collective-permute-done((f32[2,32,2080]{2,1,0:T(8,128)}, f32[2,32,2080]{2,1,0:T(8,128)S(1)}, u32[]{:S(2)}, u32[]{:S(2)}) %collective-permute-start.8) | collective-permute-done | bytes 532512 | tf_op jit(solution)/shard_map/ppermute | solution.py:163
  100.8 1.9 %collective-permute-start.9 = (f32[32,2080]{1,0:T(8,128)S(1)}, f32[32,2080]{1,0:T(8,128)S(1)}, u32[]{:S(2)}, u32[]{:S(2)}) collective-permute-start(f32[32,2080]{1,0:T(8,128)S(1)} %get-tuple-element.31), channel_id=1, source_target_pairs={{0,8},{4,12},{8,0},{12,4},{1,9},{5,13},{9,1},{13,5},{2,10},{6,14},... | collective-permute-start | bytes 798728 | tf_op jit(solution)/shard_map/ppermute | solution.py:167
  103.1 23.2 %collective-permute-done.9 = f32[32,2080]{1,0:T(8,128)S(1)} collective-permute-done((f32[32,2080]{1,0:T(8,128)S(1)}, f32[32,2080]{1,0:T(8,128)S(1)}, u32[]{:S(2)}, u32[]{:S(2)}) %collective-permute-start.9) | collective-permute-done | bytes 266272 | tf_op jit(solution)/shard_map/ppermute | solution.py:167
  127.7 4.1 %slice_bitcast_fusion.1 = (bf16[64,64,256]{2,1,0:T(8,128)(2,1)}, bf16[64,64,256]{2,1,0:T(8,128)(2,1)S(1)}) fusion(bf16[64,2,64,256]{3,2,1,0:T(8,128)(2,1)} %bitcast.51), kind=kLoop, calls=%fused_computation.24 | loop fusion | bytes 8388608 | tf_op jit(solution)/shard_map/squeeze | solution.py:261
  131.8 2.2 %gather_fusion.6 = bf16[32,64,256]{2,1,0:T(8,128)(2,1)S(1)} fusion(bf16[64,64,256]{2,1,0:T(8,128)(2,1)} %get-tuple-element.26, s32[1024]{0:T(1024)S(1)} %pad_clamp_fusion), kind=kCustom, calls=%fused_computation.clone | custom fusion | bytes 2097280 | tf_op jit(solution)/shard_map/jit(_take)/gather | solution.py:261
  134.0 1.6 %gather_fusion.7 = bf16[32,64,256]{2,1,0:T(8,128)(2,1)} fusion(bf16[64,64,256]{2,1,0:T(8,128)(2,1)S(1)} %get-tuple-element.27, s32[1024]{0:T(1024)S(1)} %pad_clamp_fusion), kind=kCustom, calls=%fused_computation.1.clone | custom fusion | bytes 2097280 | tf_op jit(solution)/shard_map/jit(_take)/gather | solution.py:261
  135.6 1.5 %broadcast_select_fusion.1 = (bf16[32,64,256]{2,1,0:T(8,128)(2,1)S(1)}, bf16[32,64,256]{2,1,0:T(8,128)(2,1)S(1)}) fusion(bf16[32,64,256]{2,1,0:T(8,128)(2,1)S(1)} %gather_fusion.6, pred[32]{0:T(512)(128)(4,1)S(1)} %get-tuple-element.17, bf16[32,64,256]{2,1,0:T(8,128)(2,1)} %gather_fusion.7), kind=kLoop, calls=%fused_computation.40 | loop fusion | flops 1048576 | bytes 4194336 | tf_op jit(solution)/shard_map/jit(_take)/select_n | solution.py:261
  138.6 1.5 %pad_maximum_fusion = bf16[2,2048,256]{2,1,0:T(8,128)(2,1)} fusion(bf16[1,2048,256]{2,1,0:T(8,128)(2,1)S(1)} %fusion.4, bf16[1,2048,256]{2,1,0:T(8,128)(2,1)S(1)} %fusion.5), kind=kLoop, calls=%fused_computation.25 | loop fusion | flops 1048576 | bytes 4194304 | tf_op jit(solution)/shard_map/stack | solution.py:263
  (129 shorter events, 27.5 us)
Async XLA Ops:
  0.6 15.6 %copy-start = (bf16[48,2,64,256]{3,2,1,0:T(8,128)(2,1)S(1)}, bf16[48,2,64,256]{3,2,1,0:T(8,128)(2,1)}, u32[]{:S(2)}) copy-start(bf16[48,2,64,256]{3,2,1,0:T(8,128)(2,1)} %param.17) | copy-start | bytes 9437188
  0.6 3.8 %copy-start.2 = (bf16[64,8192]{1,0:T(8,128)(2,1)S(1)}, bf16[64,8192]{1,0:T(8,128)(2,1)}, u32[]{:S(2)}) copy-start(bf16[64,8192]{1,0:T(8,128)(2,1)} %param.13) | copy-start | bytes 3145732
  0.7 4.2 %copy-start.3 = (bf16[32,8192]{1,0:T(8,128)(2,1)S(1)}, bf16[32,8192]{1,0:T(8,128)(2,1)}, u32[]{:S(2)}) copy-start(bf16[32,8192]{1,0:T(8,128)(2,1)} %param.12) | copy-start | bytes 1572868
  6.4 4.6 %copy-start.7 = (s32[128]{0:T(128)S(1)}, s32[128]{0:T(128)}, u32[]{:S(2)}) copy-start(s32[128]{0:T(128)} %param.20) | copy-start | bytes 1540
  6.4 5.2 %copy-start.8 = (s32[128,1]{0,1:T(1,128)S(1)}, s32[128,1]{0,1:T(1,128)}, u32[]{:S(2)}) copy-start(s32[128,1]{0,1:T(1,128)} %param.19) | copy-start | bytes 1540
  6.4 7.2 %copy-start.5 = (s32[256]{0:T(256)S(1)}, s32[256]{0:T(256)}, u32[]{:S(2)}) copy-start(s32[256]{0:T(256)} %param.21) | copy-start | bytes 3076
  6.4 8.5 %copy-start.6 = (bf16[48,2,2]{0,2,1:T(2,128)(2,1)S(1)}, bf16[48,2,2]{0,2,1:T(2,128)(2,1)}, u32[]{:S(2)}) copy-start(bf16[48,2,2]{0,2,1:T(2,128)(2,1)} %param.18) | copy-start | bytes 1156
  6.4 25.3 %all-to-all-start = ((bf16[96,4,2048]{2,0,1:T(8,128)(2,1)}), bf16[96,4,2048]{2,0,1:T(8,128)(2,1)}, u32[]{:S(2)}, u32[]{:S(2)}) async-start(bf16[96,4,2048]{2,0,1:T(8,128)(2,1)} %bitcast.138), calls=%async_computation | async-start | bytes 3145728 | tf_op jit(solution)/shard_map/all_to_all | solution.py:225
  35.8 6.0 %collective-permute-start.4 = (f32[2,96,2,256]{3,1,2,0:T(8,128)S(1)}, f32[2,96,2,256]{3,1,2,0:T(8,128)S(1)}, u32[]{:S(2)}, u32[]{:S(2)}) collective-permute-start(f32[2,96,2,256]{3,1,2,0:T(8,128)S(1)} %dynamic-slice_bitcast_fusion.3), channel_id=1, source_target_pairs={{0,4},{4,0},{8,12},{12,8},{1,5},{5,1},{9,13},{13,9},{2,6},{6,2},{1... | collective-permute-start | bytes 1179656 | tf_op jit(solution)/shard_map/ppermute | solution.py:116
  40.6 2.2 %collective-permute-start = (f32[2,32,2048]{2,1,0:T(8,128)S(1)}, f32[2,32,2048]{2,1,0:T(8,128)}, u32[]{:S(2)}, u32[]{:S(2)}) collective-permute-start(f32[2,32,2048]{2,1,0:T(8,128)S(1)} %dynamic-slice_bitcast_fusion.2), channel_id=1, source_target_pairs={{0,4},{4,0},{8,12},{12,8},{1,5},{5,1},{9,13},{13,9},{2,6},{6,2},{1... | collective-permute-start | bytes 1572872 | tf_op jit(solution)/shard_map/ppermute | solution.py:116
  41.9 6.9 %collective-permute-start.5 = (f32[96,2,256]{2,0,1:T(8,128)S(1)}, f32[96,2,256]{2,0,1:T(8,128)S(1)}, u32[]{:S(2)}, u32[]{:S(2)}) collective-permute-start(f32[96,2,256]{2,0,1:T(8,128)S(1)} %dynamic-slice_bitcast_fusion.7), channel_id=1, source_target_pairs={{0,8},{4,12},{8,0},{12,4},{1,9},{5,13},{9,1},{13,5},{2,10},{6,14},... | collective-permute-start | bytes 589832 | tf_op jit(solution)/shard_map/ppermute | solution.py:123
  48.8 5.7 %collective-permute-start.6 = (bf16[96,2,256]{2,0,1:T(8,128)(2,1)S(1)}, bf16[96,2,256]{2,0,1:T(8,128)(2,1)S(1)}, u32[]{:S(2)}, u32[]{:S(2)}) collective-permute-start(bf16[96,2,256]{2,0,1:T(8,128)(2,1)S(1)} %fusion.23), channel_id=1, source_target_pairs={{0,8},{4,12},{8,0},{12,4},{1,9},{5,13},{9,1},{13,5},{2,10},{6,14},... | collective-permute-start | bytes 294920 | tf_op jit(solution)/shard_map/ppermute | solution.py:126
  49.2 9.2 %collective-permute-start.1 = (f32[32,2048]{1,0:T(8,128)S(1)}, f32[32,2048]{1,0:T(8,128)S(1)}, u32[]{:S(2)}, u32[]{:S(2)}) collective-permute-start(f32[32,2048]{1,0:T(8,128)S(1)} %dynamic-slice_bitcast_fusion.6), channel_id=1, source_target_pairs={{0,8},{4,12},{8,0},{12,4},{1,9},{5,13},{9,1},{13,5},{2,10},{6,14},... | collective-permute-start | bytes 786440 | tf_op jit(solution)/shard_map/ppermute | solution.py:123
  55.2 4.0 %collective-permute-start.7 = (bf16[2,96,2,256]{3,1,2,0:T(8,128)(2,1)S(1)}, bf16[2,96,2,256]{3,1,2,0:T(8,128)(2,1)S(1)}, u32[]{:S(2)}, u32[]{:S(2)}) collective-permute-start(bf16[2,96,2,256]{3,1,2,0:T(8,128)(2,1)S(1)} %broadcast_select_fusion.3), channel_id=1, source_target_pairs={{0,4},{4,0},{8,12},{12,8},{1,5},{5,1},{9,13},{13,9},{2,6},{6,2},{1... | collective-permute-start | bytes 589832 | tf_op jit(solution)/shard_map/ppermute | solution.py:130
  58.4 5.0 %collective-permute-start.2 = (bf16[32,2048]{1,0:T(8,128)(2,1)S(1)}, bf16[32,2048]{1,0:T(8,128)(2,1)S(1)}, u32[]{:S(2)}, u32[]{:S(2)}) collective-permute-start(bf16[32,2048]{1,0:T(8,128)(2,1)S(1)} %fusion.21), channel_id=1, source_target_pairs={{0,8},{4,12},{8,0},{12,4},{1,9},{5,13},{9,1},{13,5},{2,10},{6,14},... | collective-permute-start | bytes 393224 | tf_op jit(solution)/shard_map/ppermute | solution.py:126
  64.1 1.6 %collective-permute-start.3 = (bf16[2,32,2048]{2,1,0:T(8,128)(2,1)S(1)}, bf16[2,32,2048]{2,1,0:T(8,128)(2,1)S(1)}, u32[]{:S(2)}, u32[]{:S(2)}) collective-permute-start(bf16[2,32,2048]{2,1,0:T(8,128)(2,1)S(1)} %broadcast_select_fusion.2), channel_id=1, source_target_pairs={{0,4},{4,0},{8,12},{12,8},{1,5},{5,1},{9,13},{13,9},{2,6},{6,2},{1... | collective-permute-start | bytes 786440 | tf_op jit(solution)/shard_map/ppermute | solution.py:130
  67.4 60.3 %all-to-all-start.1 = ((bf16[4,16,2,64,256]{4,3,2,1,0:T(8,128)(2,1)}), bf16[4,16,2,64,256]{4,3,2,1,0:T(8,128)(2,1)}, u32[]{:S(2)}, u32[]{:S(2)}) async-start(bf16[4,16,2,64,256]{4,3,2,1,0:T(8,128)(2,1)} %multiply_convert_fusion), calls=%async_computation.1 | async-start | bytes 8388608 | tf_op jit(solution)/shard_map/all_to_all | solution.py:243
  93.1 3.4 %copy-start.4 = (f32[128,2048]{1,0:T(8,128)S(1)}, f32[128,2048]{1,0:T(8,128)}, u32[]{:S(2)}) copy-start(f32[128,2048]{1,0:T(8,128)} %get-tuple-element.11) | copy-start | bytes 3145732
  97.7 2.2 %collective-permute-start.8 = (f32[2,32,2080]{2,1,0:T(8,128)}, f32[2,32,2080]{2,1,0:T(8,128)S(1)}, u32[]{:S(2)}, u32[]{:S(2)}) collective-permute-start(f32[2,32,2080]{2,1,0:T(8,128)} %get-tuple-element.29), channel_id=1, source_target_pairs={{0,4},{4,0},{8,12},{12,8},{1,5},{5,1},{9,13},{13,9},{2,6},{6,2},{1... | collective-permute-start | bytes 1597448 | tf_op jit(solution)/shard_map/ppermute | solution.py:163
  100.8 25.5 %collective-permute-start.9 = (f32[32,2080]{1,0:T(8,128)S(1)}, f32[32,2080]{1,0:T(8,128)S(1)}, u32[]{:S(2)}, u32[]{:S(2)}) collective-permute-start(f32[32,2080]{1,0:T(8,128)S(1)} %get-tuple-element.31), channel_id=1, source_target_pairs={{0,8},{4,12},{8,0},{12,4},{1,9},{5,13},{9,1},{13,5},{2,10},{6,14},... | collective-permute-start | bytes 798728 | tf_op jit(solution)/shard_map/ppermute | solution.py:167
  137.8 2.3 %copy-start.1 = (bf16[48,2,64,256]{3,2,1,0:T(8,128)(2,1)S(1)}, bf16[48,2,64,256]{3,2,1,0:T(8,128)(2,1)}, u32[]{:S(2)}) copy-start(bf16[48,2,64,256]{3,2,1,0:T(8,128)(2,1)} %param.17) | copy-start | bytes 9437188

commit v10 on v9

--- a/solution.py
+++ b/solution.py
@@ -240,14 +240,24 @@
     send_later, every_query, every_kv = lax.optimization_barrier(
         (send_blocks, every_query, every_kv)
     )
-    got_blocks = lax.all_to_all(send_later, "ctx", split_axis=0, concat_axis=0, tiled=True)
+    by_shift = [lax.dynamic_index_in_dim(send_later, own_index, 0, keepdims=False)]
+    for step in range(1, shards):
+        target = (own_index + step) % shards
+        by_shift.append(
+            lax.ppermute(
+                lax.dynamic_index_in_dim(send_later, target, 0, keepdims=False),
+                "ctx",
+                [(i, (i + step) % shards) for i in range(shards)],
+            )
+        )
+    got_blocks = jnp.stack(by_shift)
     every_query = every_query.reshape(shards * q_rows, q_width)
     own_kv = lax.dynamic_index_in_dim(every_kv, own_index, 0, keepdims=False)
     recomp_kv = every_kv[:, q_rows:].reshape(shards * r_rows, 2, kv_width)
 
     own_owner = lax.dynamic_index_in_dim(owners, own_index, 0, keepdims=False)
     own_rank = lax.dynamic_index_in_dim(order_rank, own_index, 0, keepdims=False)
-    flat_index = own_owner * capacity + own_rank
+    flat_index = ((own_index - own_owner) % shards) * capacity + own_rank
     local_pos = recomp_pos - own_index * ctx_dev
     match = local_pos[None, :] == jnp.arange(ctx_dev)[:, None]
     hit = jnp.any(match, axis=1)

time: 141 us -> 165 us (1.17)
  waiting for transfers between devices: 48.1 us -> 70.3 us
  starting transfers between devices: 15.5 us -> 11.4 us
  other arithmetic: 25.2 us -> 28.5 us
  local copies, waits for them, and re-layouts: 20.8 us -> 24.1 us
    ppermute x1, waiting for transfers between devices: 23.2 us -> 47.3 us  [hier_combine(): parts.append(lax.ppermute(send, 'ctx', shift_pairs(shards, step)))]
    all_to_all x1 -> x0, starting transfers between devices: 5.02 us -> none  [body(): lax.all_to_all(send_later, 'ctx', split_axis=0, concat_axis=0, tiled=True)]
    dynamic_slice x0 -> x1, local copies, waits for them, and re-layouts: none -> 4.04 us  [body(): lax.dynamic_index_in_dim(send_later, own_index, 0, keepdims=False)]
    squeeze x1, local copies, waits for them, and re-layouts: 4.14 us -> 1.85 us  [body(): by_slot[:, c]]
    another operation x0 -> x1, other arithmetic: none -> 2.12 us  [body(): got_blocks = jnp.stack(by_shift)]
    ppermute x0 -> x3, starting transfers between devices: none -> 2.01 us  [body(): lax.ppermute(lax.dynamic_index_in_dim(send_later, target, 0, keepdims=Fal...]
    ppermute x1, waiting for transfers between devices: 1.89 us -> 0.01 us  [hier_combine(): lax.ppermute(other, 'ctx', core_pairs(shards))]
  transfers between devices with their start and end apart: 12 -> 14, of which waited for: 9 -> 8; matrix products, arithmetic and copies ran while one was open for 22% -> 19% of each run, Pallas kernels for 14% -> 0%
where the time goes in v10:
time: 165 us
  waiting for transfers between devices  70.3 us (43%)
  other arithmetic  28.5 us (17%)
  local copies, waits for them, and re-layouts  24.1 us (15%)
  Pallas kernels  20.2 us (12%)
  starting transfers between devices  11.4 us (7%)
  matrix products  9.17 us (6%)
    ppermute x1, waiting for transfers between devices, hier_combine(): parts.append(lax.ppermute(send, 'ctx', shift_pairs(shards, step)))  47.3 us
    pallas_call x1, Pallas kernels, attend(): pl.pallas_call(functools.partial(attn_kernel, score_scale=score_scale, gr...  20.2 us
    ppermute x2, waiting for transfers between devices, hier_reduce_gather(): lax.ppermute(send, 'ctx', shift_pairs(shards, step))  7.81 us
    ppermute x2, waiting for transfers between devices, hier_reduce_gather(): lax.ppermute(rounded, 'ctx', shift_pairs(shards, step))  6.97 us
    convert_element_type x1, other arithmetic, body(): send_blocks = (send_codes.astype(jnp.float32).reshape(shards * capacity,...  6.13 us
    all_to_all x1, waiting for transfers between devices, body(): lax.all_to_all(normed, 'ctx', split_axis=1, concat_axis=0, tiled=True)  5.87 us
    dot_general x1, matrix products, body(): jnp.dot(question_part, w_query, preferred_element_type=jnp.float32)  4.63 us
    all_to_all x1, starting transfers between devices, body(): lax.all_to_all(normed, 'ctx', split_axis=1, concat_axis=0, tiled=True)  4.54 us
  transfers between devices with their start and end apart: 14, of which 8 were waited for; matrix products, arithmetic and copies ran while one was open for 19% of the time, Pallas kernels for 0%

profile of v10, /device:TPU:0, one launch (start us, length us, event | category | flops | bytes accessed | tf_op | source)
XLA Modules:
  0.0 164.9 jit_solution(13167351018417350650)
XLA Ops:
  1.5 1.7 %fusion.6 = f32[64]{0:T(128)S(1)} fusion(bf16[64,8192]{1,0:T(8,128)(2,1)} %param.13), kind=kLoop, calls=%fused_computation.21 | loop fusion | flops 1572800 | bytes 1048832 | tf_op jit(solution)/shard_map/reduce_sum | solution.py:19
  6.4 4.5 %all-to-all-start = ((bf16[96,4,2048]{2,0,1:T(8,128)(2,1)}), bf16[96,4,2048]{2,0,1:T(8,128)(2,1)}, u32[]{:S(2)}, u32[]{:S(2)}) async-start(bf16[96,4,2048]{2,0,1:T(8,128)(2,1)} %bitcast.159), calls=%async_computation | async-start | bytes 3145728 | tf_op jit(solution)/shard_map/all_to_all | solution.py:225
  16.2 2.8 %gather_fusion = bf16[64,2,64,256]{3,2,1,0:T(8,128)(2,1)} fusion(bf16[48,2,64,256]{3,2,1,0:T(8,128)(2,1)S(1)} %copy-done, s32[1024]{0:T(1024)S(1)} %pad_clamp_fusion.3), kind=kCustom, calls=%fused_computation.2 | custom fusion | bytes 8388864 | tf_op jit(solution)/shard_map/jit(_take)/gather | solution.py:207
  19.0 6.1 %multiply_convert_fusion = bf16[4,16,2,64,256]{4,3,2,1,0:T(8,128)(2,1)} fusion(f32[4,16,2,256]{3,2,1,0:T(2,128)S(1)} %mul.142, bf16[4,16,2,64,256]{4,3,2,1,0:T(8,128)(2,1)} %bitcast.157, pred[4,16]{1,0:T(4,128)(4,1)S(1)} %compare_and_fusion.4), kind=kLoop, calls=%fused_computation.10 | loop fusion | flops 8388608 | bytes 8519744 | tf_op jit(solution)/shard_map/convert_element_type | solution.py:212
  25.8 5.9 %all-to-all-done = bf16[96,4,2048]{2,0,1:T(8,128)(2,1)} async-done(((bf16[96,4,2048]{2,0,1:T(8,128)(2,1)}), bf16[96,4,2048]{2,0,1:T(8,128)(2,1)}, u32[]{:S(2)}, u32[]{:S(2)}) %all-to-all-start) | async-done | bytes 1572896 | tf_op jit(solution)/shard_map/all_to_all | solution.py:225
  32.7 3.0 %fusion.9 = f32[2,2,96,2,256]{4,2,3,1,0:T(8,128)S(1)} fusion(bf16[2,2,96,2048,1]{3,2,4,1,0:T(8,128)(2,1)} %bitcast.21, bf16[2048,2,256,1,1]{2,1,0,4,3:T(2,128)(2,1)} %bitcast.183), kind=kOutput, calls=%fused_computation.27 | convolution fusion | flops 805306368 | bytes 4456448 | tf_op jit(solution)/shard_map/tk,kcn->tcn/dot_general | solution.py:230
  35.9 4.6 %fusion = f32[2,2,32,2048]{3,2,1,0:T(8,128)S(1)} fusion(bf16[2,2,32,2048]{3,2,1,0:T(8,128)(2,1)S(1)} %bitcast.161, bf16[2048,2048]{1,0:T(8,128)(2,1)} %param.15), kind=kOutput, calls=%fused_computation.8 | convolution fusion | flops 1073741824 | bytes 9961472 | tf_op jit(solution)/shard_map/dot_general | solution.py:229
  43.9 4.8 %collective-permute-done.5 = f32[96,2,256]{2,0,1:T(8,128)S(1)} collective-permute-done((f32[96,2,256]{2,0,1:T(8,128)S(1)}, f32[96,2,256]{2,0,1:T(8,128)S(1)}, u32[]{:S(2)}, u32[]{:S(2)}) %collective-permute-start.5) | collective-permute-done | bytes 196640 | tf_op jit(solution)/shard_map/ppermute | solution.py:123
  49.2 1.8 %collective-permute-start.1 = (f32[32,2048]{1,0:T(8,128)S(1)}, f32[32,2048]{1,0:T(8,128)S(1)}, u32[]{:S(2)}, u32[]{:S(2)}) collective-permute-start(f32[32,2048]{1,0:T(8,128)S(1)} %dynamic-slice_bitcast_fusion.9), channel_id=1, source_target_pairs={{0,8},{4,12},{8,0},{12,4},{1,9},{5,13},{9,1},{13,5},{2,10},{6,14},... | collective-permute-start | bytes 786440 | tf_op jit(solution)/shard_map/ppermute | solution.py:123
  51.0 3.6 %collective-permute-done.6 = bf16[96,2,256]{2,0,1:T(8,128)(2,1)S(1)} collective-permute-done((bf16[96,2,256]{2,0,1:T(8,128)(2,1)S(1)}, bf16[96,2,256]{2,0,1:T(8,128)(2,1)S(1)}, u32[]{:S(2)}, u32[]{:S(2)}) %collective-permute-start.6) | collective-permute-done | bytes 98336 | tf_op jit(solution)/shard_map/ppermute | solution.py:126
  55.4 3.0 %collective-permute-done.1 = f32[32,2048]{1,0:T(8,128)S(1)} collective-permute-done((f32[32,2048]{1,0:T(8,128)S(1)}, f32[32,2048]{1,0:T(8,128)S(1)}, u32[]{:S(2)}, u32[]{:S(2)}) %collective-permute-start.1) | collective-permute-done | bytes 262176 | tf_op jit(solution)/shard_map/ppermute | solution.py:123
  60.0 3.4 %collective-permute-done.2 = bf16[32,2048]{1,0:T(8,128)(2,1)S(1)} collective-permute-done((bf16[32,2048]{1,0:T(8,128)(2,1)S(1)}, bf16[32,2048]{1,0:T(8,128)(2,1)S(1)}, u32[]{:S(2)}, u32[]{:S(2)}) %collective-permute-start.2) | collective-permute-done | bytes 131104 | tf_op jit(solution)/shard_map/ppermute | solution.py:126
  64.3 1.4 collective-permute-done.3
  68.0 20.2 %shard_map.113 = (f32[128,2048]{1,0:T(8,128)}, f32[16,128,1]{2,1,0:T(8,128)}, f32[16,128,1]{2,1,0:T(8,128)}) custom-call(f32[1,4096]{1,0:T(1,128)} %and_select_fusion.bias_ref, s32[1,96]{1,0:T(1,128)} %compare_select_fusion.14.rank_ref, bf16[128,2048]{1,0:T(8,128)(2,1)} %bitcast.162, bf16[64,128,256]{2,1,0:T(8,128)(2,1)} %bitcast.155, ...), custom_call_target="tpu_custom_call" | custom-call | tf_op jit(solution)/shard_map/pallas_call | solution.py:66
  88.2 1.7 %reduce.1 = f32[16,128]{1,0:T(8,128)S(1)} reduce(f32[16,128,1]{2,1,0:T(8,128)} %get-tuple-element.12, f32[]{:T(128)} %constant.250), dimensions={2}, to_apply=%get-tuple-element.12.reduce_sub_computation | reduce | bytes 16388 | tf_op jit(solution)/shard_map/pallas_call | solution.py:66
  90.0 1.6 reduce.2
  93.0 4.0 %constant_dynamic-slice_fusion.2 = (bf16[1,16,2,64,256]{4,3,2,1,0:T(8,128)(2,1)S(1)}, bf16[16,2,64,256]{3,2,1,0:T(8,128)(2,1)}, bf16[16,2,64,256]{3,2,1,0:T(8,128)(2,1)}, bf16[16,2,64,256]{3,2,1,0:T(8,128)(2,1)}) fusion(bf16[4,16,2,64,256]{4,3,2,1,0:T(8,128)(2,1)} %multiply_convert_fusion, s32[]{:T(128)S(6)} %select_n.301, s32[]{:T(128)S(6)} %select_n.307, ...), kind=kLoop, calls=%fused_computation.112 | loop fusion | bytes 8388624 | tf_op jit(solution)/shard_map/jit(dynamic_index_in_dim)/dynamic_slice | solution.py:243
  103.9 47.3 %collective-permute-done.9 = f32[32,2080]{1,0:T(8,128)S(1)} collective-permute-done((f32[32,2080]{1,0:T(8,128)S(1)}, f32[32,2080]{1,0:T(8,128)S(1)}, u32[]{:S(2)}, u32[]{:S(2)}) %collective-permute-start.9) | collective-permute-done | bytes 266272 | tf_op jit(solution)/shard_map/ppermute | solution.py:167
  152.6 2.1 %pad_maximum_fusion = bf16[4,16,2,64,256]{4,3,2,1,0:T(8,128)(2,1)S(1)} fusion(bf16[1,16,2,64,256]{4,3,2,1,0:T(8,128)(2,1)} %bitcast.57, bf16[1,16,2,64,256]{4,3,2,1,0:T(8,128)(2,1)} %bitcast.55, bf16[1,16,2,64,256]{4,3,2,1,0:T(8,128)(2,1)} %bitcast.53, bf16[1,16,2,64,256]{4,3,2,1,0:T(8,128)(2,1)S(1)} %get-tuple-element.28), kind=kLoop, calls=%fused_computation.11 | loop fusion | flops 6291456 | bytes 8388608 | tf_op jit(solution)/shard_map/stack | solution.py:253
  154.8 1.8 %slice_bitcast_fusion.1 = (bf16[64,64,256]{2,1,0:T(8,128)(2,1)}, bf16[64,64,256]{2,1,0:T(8,128)(2,1)S(1)}) fusion(bf16[64,2,64,256]{3,2,1,0:T(8,128)(2,1)S(1)} %bitcast.158), kind=kLoop, calls=%fused_computation.25 | loop fusion | bytes 8388608 | tf_op jit(solution)/shard_map/squeeze | solution.py:271
  156.6 2.2 %gather_fusion.6 = bf16[32,64,256]{2,1,0:T(8,128)(2,1)S(1)} fusion(bf16[64,64,256]{2,1,0:T(8,128)(2,1)} %get-tuple-element.26, s32[1024]{0:T(1024)S(1)} %pad_clamp_fusion), kind=kCustom, calls=%fused_computation.clone | custom fusion | bytes 2097280 | tf_op jit(solution)/shard_map/jit(_take)/gather | solution.py:271
  158.8 1.6 gather_fusion.7
  160.4 1.5 broadcast_select_fusion.1
  163.4 1.5 pad_maximum_fusion.1
  (137 shorter events, 31.5 us)
Async XLA Ops:
  0.6 15.6 %copy-start = (bf16[48,2,64,256]{3,2,1,0:T(8,128)(2,1)S(1)}, bf16[48,2,64,256]{3,2,1,0:T(8,128)(2,1)}, u32[]{:S(2)}) copy-start(bf16[48,2,64,256]{3,2,1,0:T(8,128)(2,1)} %param.17) | copy-start | bytes 9437188
  0.6 3.8 %copy-start.2 = (bf16[64,8192]{1,0:T(8,128)(2,1)S(1)}, bf16[64,8192]{1,0:T(8,128)(2,1)}, u32[]{:S(2)}) copy-start(bf16[64,8192]{1,0:T(8,128)(2,1)} %param.13) | copy-start | bytes 3145732
  0.7 4.2 %copy-start.3 = (bf16[32,8192]{1,0:T(8,128)(2,1)S(1)}, bf16[32,8192]{1,0:T(8,128)(2,1)}, u32[]{:S(2)}) copy-start(bf16[32,8192]{1,0:T(8,128)(2,1)} %param.12) | copy-start | bytes 1572868
  6.4 4.6 %copy-start.8 = (s32[128]{0:T(128)S(1)}, s32[128]{0:T(128)}, u32[]{:S(2)}) copy-start(s32[128]{0:T(128)} %param.20) | copy-start | bytes 1540
  6.4 5.2 %copy-start.9 = (s32[128,1]{0,1:T(1,128)S(1)}, s32[128,1]{0,1:T(1,128)}, u32[]{:S(2)}) copy-start(s32[128,1]{0,1:T(1,128)} %param.19) | copy-start | bytes 1540
  6.4 7.2 %copy-start.6 = (s32[256]{0:T(256)S(1)}, s32[256]{0:T(256)}, u32[]{:S(2)}) copy-start(s32[256]{0:T(256)} %param.21) | copy-start | bytes 3076
  6.4 8.5 %copy-start.7 = (bf16[48,2,2]{0,2,1:T(2,128)(2,1)S(1)}, bf16[48,2,2]{0,2,1:T(2,128)(2,1)}, u32[]{:S(2)}) copy-start(bf16[48,2,2]{0,2,1:T(2,128)(2,1)} %param.18) | copy-start | bytes 1156
  6.4 25.3 %all-to-all-start = ((bf16[96,4,2048]{2,0,1:T(8,128)(2,1)}), bf16[96,4,2048]{2,0,1:T(8,128)(2,1)}, u32[]{:S(2)}, u32[]{:S(2)}) async-start(bf16[96,4,2048]{2,0,1:T(8,128)(2,1)} %bitcast.159), calls=%async_computation | async-start | bytes 3145728 | tf_op jit(solution)/shard_map/all_to_all | solution.py:225
  35.8 6.0 %collective-permute-start.4 = (f32[2,96,2,256]{3,1,2,0:T(8,128)S(1)}, f32[2,96,2,256]{3,1,2,0:T(8,128)S(1)}, u32[]{:S(2)}, u32[]{:S(2)}) collective-permute-start(f32[2,96,2,256]{3,1,2,0:T(8,128)S(1)} %dynamic-slice_bitcast_fusion.6), channel_id=1, source_target_pairs={{0,4},{4,0},{8,12},{12,8},{1,5},{5,1},{9,13},{13,9},{2,6},{6,2},{1... | collective-permute-start | bytes 1179656 | tf_op jit(solution)/shard_map/ppermute | solution.py:116
  40.6 2.2 %collective-permute-start = (f32[2,32,2048]{2,1,0:T(8,128)S(1)}, f32[2,32,2048]{2,1,0:T(8,128)}, u32[]{:S(2)}, u32[]{:S(2)}) collective-permute-start(f32[2,32,2048]{2,1,0:T(8,128)S(1)} %dynamic-slice_bitcast_fusion.5), channel_id=1, source_target_pairs={{0,4},{4,0},{8,12},{12,8},{1,5},{5,1},{9,13},{13,9},{2,6},{6,2},{1... | collective-permute-start | bytes 1572872 | tf_op jit(solution)/shard_map/ppermute | solution.py:116
  41.9 6.9 %collective-permute-start.5 = (f32[96,2,256]{2,0,1:T(8,128)S(1)}, f32[96,2,256]{2,0,1:T(8,128)S(1)}, u32[]{:S(2)}, u32[]{:S(2)}) collective-permute-start(f32[96,2,256]{2,0,1:T(8,128)S(1)} %dynamic-slice_bitcast_fusion.10), channel_id=1, source_target_pairs={{0,8},{4,12},{8,0},{12,4},{1,9},{5,13},{9,1},{13,5},{2,10},{6,14},... | collective-permute-start | bytes 589832 | tf_op jit(solution)/shard_map/ppermute | solution.py:123
  48.8 5.7 %collective-permute-start.6 = (bf16[96,2,256]{2,0,1:T(8,128)(2,1)S(1)}, bf16[96,2,256]{2,0,1:T(8,128)(2,1)S(1)}, u32[]{:S(2)}, u32[]{:S(2)}) collective-permute-start(bf16[96,2,256]{2,0,1:T(8,128)(2,1)S(1)} %fusion.23), channel_id=1, source_target_pairs={{0,8},{4,12},{8,0},{12,4},{1,9},{5,13},{9,1},{13,5},{2,10},{6,14},... | collective-permute-start | bytes 294920 | tf_op jit(solution)/shard_map/ppermute | solution.py:126
  49.2 9.2 %collective-permute-start.1 = (f32[32,2048]{1,0:T(8,128)S(1)}, f32[32,2048]{1,0:T(8,128)S(1)}, u32[]{:S(2)}, u32[]{:S(2)}) collective-permute-start(f32[32,2048]{1,0:T(8,128)S(1)} %dynamic-slice_bitcast_fusion.9), channel_id=1, source_target_pairs={{0,8},{4,12},{8,0},{12,4},{1,9},{5,13},{9,1},{13,5},{2,10},{6,14},... | collective-permute-start | bytes 786440 | tf_op jit(solution)/shard_map/ppermute | solution.py:123
  55.2 4.0 %collective-permute-start.7 = (bf16[2,96,2,256]{3,1,2,0:T(8,128)(2,1)S(1)}, bf16[2,96,2,256]{3,1,2,0:T(8,128)(2,1)S(1)}, u32[]{:S(2)}, u32[]{:S(2)}) collective-permute-start(bf16[2,96,2,256]{3,1,2,0:T(8,128)(2,1)S(1)} %broadcast_select_fusion.3), channel_id=1, source_target_pairs={{0,4},{4,0},{8,12},{12,8},{1,5},{5,1},{9,13},{13,9},{2,6},{6,2},{1... | collective-permute-start | bytes 589832 | tf_op jit(solution)/shard_map/ppermute | solution.py:130
  58.4 5.0 %collective-permute-start.2 = (bf16[32,2048]{1,0:T(8,128)(2,1)S(1)}, bf16[32,2048]{1,0:T(8,128)(2,1)S(1)}, u32[]{:S(2)}, u32[]{:S(2)}) collective-permute-start(bf16[32,2048]{1,0:T(8,128)(2,1)S(1)} %fusion.21), channel_id=1, source_target_pairs={{0,8},{4,12},{8,0},{12,4},{1,9},{5,13},{9,1},{13,5},{2,10},{6,14},... | collective-permute-start | bytes 393224 | tf_op jit(solution)/shard_map/ppermute | solution.py:126
  64.1 1.6 collective-permute-start.3
  88.2 3.4 %copy-start.4 = (f32[128,2048]{1,0:T(8,128)S(1)}, f32[128,2048]{1,0:T(8,128)}, u32[]{:S(2)}) copy-start(f32[128,2048]{1,0:T(8,128)} %get-tuple-element.11) | copy-start | bytes 3145732
  92.8 6.2 %collective-permute-start.8 = (f32[2,32,2080]{2,1,0:T(8,128)}, f32[2,32,2080]{2,1,0:T(8,128)S(1)}, u32[]{:S(2)}, u32[]{:S(2)}) collective-permute-start(f32[2,32,2080]{2,1,0:T(8,128)} %get-tuple-element.33), channel_id=1, source_target_pairs={{0,4},{4,0},{8,12},{12,8},{1,5},{5,1},{9,13},{13,9},{2,6},{6,2},{1... | collective-permute-start | bytes 1597448 | tf_op jit(solution)/shard_map/ppermute | solution.py:163
  97.0 55.6 %collective-permute-start.12 = (bf16[16,2,64,256]{3,2,1,0:T(8,128)(2,1)}, bf16[16,2,64,256]{3,2,1,0:T(8,128)(2,1)}, u32[]{:S(2)}, u32[]{:S(2)}) collective-permute-start(bf16[16,2,64,256]{3,2,1,0:T(8,128)(2,1)} %get-tuple-element.29), channel_id=1, source_target_pairs={{0,12},{4,0},{8,4},{12,8},{1,13},{5,1},{9,5},{13,9},{2,14},{6,2},{... | collective-permute-start | bytes 3145736 | tf_op jit(solution)/shard_map/ppermute | solution.py:247
  97.8 54.9 %collective-permute-start.11 = (bf16[16,2,64,256]{3,2,1,0:T(8,128)(2,1)}, bf16[16,2,64,256]{3,2,1,0:T(8,128)(2,1)}, u32[]{:S(2)}, u32[]{:S(2)}) collective-permute-start(bf16[16,2,64,256]{3,2,1,0:T(8,128)(2,1)} %get-tuple-element.30), channel_id=1, source_target_pairs={{0,8},{4,12},{8,0},{12,4},{1,9},{5,13},{9,1},{13,5},{2,10},{6,14},... | collective-permute-start | bytes 3145736 | tf_op jit(solution)/shard_map/ppermute | solution.py:247
  99.0 53.6 %collective-permute-start.10 = (bf16[16,2,64,256]{3,2,1,0:T(8,128)(2,1)}, bf16[16,2,64,256]{3,2,1,0:T(8,128)(2,1)}, u32[]{:S(2)}, u32[]{:S(2)}) collective-permute-start(bf16[16,2,64,256]{3,2,1,0:T(8,128)(2,1)} %get-tuple-element.31), channel_id=1, source_target_pairs={{0,4},{4,8},{8,12},{12,0},{1,5},{5,9},{9,13},{13,1},{2,6},{6,10},{... | collective-permute-start | bytes 3145736 | tf_op jit(solution)/shard_map/ppermute | solution.py:247
  99.0 0.8 copy-start.5
  102.6 48.6 %collective-permute-start.9 = (f32[32,2080]{1,0:T(8,128)S(1)}, f32[32,2080]{1,0:T(8,128)S(1)}, u32[]{:S(2)}, u32[]{:S(2)}) collective-permute-start(f32[32,2080]{1,0:T(8,128)S(1)} %get-tuple-element.35), channel_id=1, source_target_pairs={{0,8},{4,12},{8,0},{12,4},{1,9},{5,13},{9,1},{13,5},{2,10},{6,14},... | collective-permute-start | bytes 798728 | tf_op jit(solution)/shard_map/ppermute | solution.py:167
  162.6 2.3 %copy-start.1 = (bf16[48,2,64,256]{3,2,1,0:T(8,128)(2,1)S(1)}, bf16[48,2,64,256]{3,2,1,0:T(8,128)(2,1)}, u32[]{:S(2)}) copy-start(bf16[48,2,64,256]{3,2,1,0:T(8,128)(2,1)} %param.17) | copy-start | bytes 9437188

commit v11 on v10

--- a/solution.py
+++ b/solution.py
@@ -223,6 +223,13 @@
         [rms_rows(question_hidden, norm_gain), rms_rows(recomp_hidden, norm_gain)], axis=0
     )
     pieces = lax.all_to_all(normed, "ctx", split_axis=1, concat_axis=0, tiled=True)
+    early_step = min(2, shards - 1)
+    send_early, pieces = lax.optimization_barrier((send_blocks, pieces))
+    early_blocks = lax.ppermute(
+        lax.dynamic_index_in_dim(send_early, (own_index + early_step) % shards, 0, keepdims=False),
+        "ctx",
+        [(i, (i + early_step) % shards) for i in range(shards)],
+    )
     width_part = pieces.shape[1]
     arranged = pieces.reshape(shards, row_count, width_part)
     question_part = arranged[:, :q_rows, :].reshape(shards * q_rows, width_part)
@@ -242,6 +249,9 @@
     )
     by_shift = [lax.dynamic_index_in_dim(send_later, own_index, 0, keepdims=False)]
     for step in range(1, shards):
+        if step == early_step:
+            by_shift.append(early_blocks)
+            continue
         target = (own_index + step) % shards
         by_shift.append(
             lax.ppermute(

time: 165 us -> 164 us (level)
  waiting for transfers between devices: 70.3 us -> 66.8 us
  local copies, waits for them, and re-layouts: 24.1 us -> 26 us
    ppermute x1, waiting for transfers between devices: 47.3 us -> 43.8 us  [hier_combine(): parts.append(lax.ppermute(send, 'ctx', shift_pairs(shards, step)))]
    squeeze x0 -> x1, local copies, waits for them, and re-layouts: none -> 2.33 us  [body(): lax.dynamic_index_in_dim(send_early, (own_index + early_step) % shards, 0...]
  transfers between devices with their start and end apart: 14 -> 14, of which waited for: 8 -> 8; matrix products, arithmetic and copies ran while one was open for 19% -> 20% of each run, Pallas kernels for 0% -> 0%
where the time goes in v11:
time: 164 us; the launch traced here: 163 us
  waiting for transfers between devices  66.8 us (41%)
  other arithmetic  28.5 us (17%)
  local copies, waits for them, and re-layouts  26 us (16%)
  Pallas kernels  20.2 us (12%)
  starting transfers between devices  11.1 us (7%)
  matrix products  9.17 us (6%)
    ppermute x1, waiting for transfers between devices, hier_combine(): parts.append(lax.ppermute(send, 'ctx', shift_pairs(shards, step)))  43.8 us
    pallas_call x1, Pallas kernels, attend(): pl.pallas_call(functools.partial(attn_kernel, score_scale=score_scale, gr...  20.2 us
    ppermute x2, waiting for transfers between devices, hier_reduce_gather(): lax.ppermute(send, 'ctx', shift_pairs(shards, step))  7.81 us
    ppermute x2, waiting for transfers between devices, hier_reduce_gather(): lax.ppermute(rounded, 'ctx', shift_pairs(shards, step))  6.97 us
    convert_element_type x1, other arithmetic, body(): send_blocks = (send_codes.astype(jnp.float32).reshape(shards * capacity,...  6.13 us
    all_to_all x1, waiting for transfers between devices, body(): lax.all_to_all(normed, 'ctx', split_axis=1, concat_axis=0, tiled=True)  5.88 us
    dot_general x1, matrix products, body(): jnp.dot(question_part, w_query, preferred_element_type=jnp.float32)  4.63 us
    all_to_all x1, starting transfers between devices, body(): lax.all_to_all(normed, 'ctx', split_axis=1, concat_axis=0, tiled=True)  4.54 us
  transfers between devices with their start and end apart: 14, of which 8 were waited for; matrix products, arithmetic and copies ran while one was open for 20% of the time, Pallas kernels for 0%

profile of v11, /device:TPU:0, one launch (start us, length us, event | category | flops | bytes accessed | tf_op | source)
XLA Modules:
  0.0 163.0 jit_solution(16776646984682164609)
XLA Ops:
  1.5 1.7 %fusion.6 = f32[64]{0:T(128)S(1)} fusion(bf16[64,8192]{1,0:T(8,128)(2,1)} %param.13), kind=kLoop, calls=%fused_computation.21 | loop fusion | flops 1572800 | bytes 1048832 | tf_op jit(solution)/shard_map/reduce_sum | solution.py:19
  6.4 4.5 %all-to-all-start = ((bf16[96,4,2048]{2,0,1:T(8,128)(2,1)}), bf16[96,4,2048]{2,0,1:T(8,128)(2,1)}, u32[]{:S(2)}, u32[]{:S(2)}) async-start(bf16[96,4,2048]{2,0,1:T(8,128)(2,1)} %bitcast.158), calls=%async_computation | async-start | bytes 3145728 | tf_op jit(solution)/shard_map/all_to_all | solution.py:225
  16.2 2.8 %gather_fusion = bf16[64,2,64,256]{3,2,1,0:T(8,128)(2,1)} fusion(bf16[48,2,64,256]{3,2,1,0:T(8,128)(2,1)S(1)} %copy-done, s32[1024]{0:T(1024)S(1)} %pad_clamp_fusion.3), kind=kCustom, calls=%fused_computation.2 | custom fusion | bytes 8388864 | tf_op jit(solution)/shard_map/jit(_take)/gather | solution.py:207
  19.0 6.1 %multiply_convert_fusion = bf16[4,16,2,64,256]{4,3,2,1,0:T(8,128)(2,1)} fusion(f32[4,16,2,256]{3,2,1,0:T(2,128)S(1)} %mul.142, bf16[4,16,2,64,256]{4,3,2,1,0:T(8,128)(2,1)} %bitcast.157, pred[4,16]{1,0:T(4,128)(4,1)S(1)} %compare_and_fusion.4), kind=kLoop, calls=%fused_computation.10 | loop fusion | flops 8388608 | bytes 8519744 | tf_op jit(solution)/shard_map/convert_element_type | solution.py:212
  25.8 5.9 %all-to-all-done = bf16[96,4,2048]{2,0,1:T(8,128)(2,1)} async-done(((bf16[96,4,2048]{2,0,1:T(8,128)(2,1)}), bf16[96,4,2048]{2,0,1:T(8,128)(2,1)}, u32[]{:S(2)}, u32[]{:S(2)}) %all-to-all-start) | async-done | bytes 1572896 | tf_op jit(solution)/shard_map/all_to_all | solution.py:225
  32.7 3.0 %fusion.9 = f32[384,2,256]{2,0,1:T(8,128)S(1)} fusion(bf16[2048,2,256]{2,1,0:T(2,128)(2,1)} %param.16, bf16[384,2048]{1,0:T(8,128)(2,1)} %bitcast.3), kind=kOutput, calls=%fused_computation.27 | convolution fusion | flops 805306368 | bytes 4456448 | tf_op jit(solution)/shard_map/tk,kcn->tcn/dot_general | solution.py:237
  35.9 4.6 %fusion = f32[2,2,32,2048]{3,2,1,0:T(8,128)S(1)} fusion(bf16[2,2,32,2048]{3,2,1,0:T(8,128)(2,1)S(1)} %bitcast.160, bf16[2048,2048]{1,0:T(8,128)(2,1)} %param.15), kind=kOutput, calls=%fused_computation.8 | convolution fusion | flops 1073741824 | bytes 9961472 | tf_op jit(solution)/shard_map/dot_general | solution.py:236
  43.9 4.8 %collective-permute-done.5 = f32[96,2,256]{2,0,1:T(8,128)S(1)} collective-permute-done((f32[96,2,256]{2,0,1:T(8,128)S(1)}, f32[96,2,256]{2,0,1:T(8,128)S(1)}, u32[]{:S(2)}, u32[]{:S(2)}) %collective-permute-start.5) | collective-permute-done | bytes 196640 | tf_op jit(solution)/shard_map/ppermute | solution.py:123
  49.2 1.8 %collective-permute-start.1 = (f32[32,2048]{1,0:T(8,128)S(1)}, f32[32,2048]{1,0:T(8,128)S(1)}, u32[]{:S(2)}, u32[]{:S(2)}) collective-permute-start(f32[32,2048]{1,0:T(8,128)S(1)} %dynamic-slice_bitcast_fusion.9), channel_id=1, source_target_pairs={{0,8},{4,12},{8,0},{12,4},{1,9},{5,13},{9,1},{13,5},{2,10},{6,14},... | collective-permute-start | bytes 786440 | tf_op jit(solution)/shard_map/ppermute | solution.py:123
  51.0 3.6 %collective-permute-done.6 = bf16[96,2,256]{2,0,1:T(8,128)(2,1)S(1)} collective-permute-done((bf16[96,2,256]{2,0,1:T(8,128)(2,1)S(1)}, bf16[96,2,256]{2,0,1:T(8,128)(2,1)S(1)}, u32[]{:S(2)}, u32[]{:S(2)}) %collective-permute-start.6) | collective-permute-done | bytes 98336 | tf_op jit(solution)/shard_map/ppermute | solution.py:126
  55.4 3.0 %collective-permute-done.1 = f32[32,2048]{1,0:T(8,128)S(1)} collective-permute-done((f32[32,2048]{1,0:T(8,128)S(1)}, f32[32,2048]{1,0:T(8,128)S(1)}, u32[]{:S(2)}, u32[]{:S(2)}) %collective-permute-start.1) | collective-permute-done | bytes 262176 | tf_op jit(solution)/shard_map/ppermute | solution.py:123
  60.0 3.4 %collective-permute-done.2 = bf16[32,2048]{1,0:T(8,128)(2,1)S(1)} collective-permute-done((bf16[32,2048]{1,0:T(8,128)(2,1)S(1)}, bf16[32,2048]{1,0:T(8,128)(2,1)S(1)}, u32[]{:S(2)}, u32[]{:S(2)}) %collective-permute-start.2) | collective-permute-done | bytes 131104 | tf_op jit(solution)/shard_map/ppermute | solution.py:126
  68.0 20.2 %shard_map.113 = (f32[128,2048]{1,0:T(8,128)}, f32[16,128,1]{2,1,0:T(8,128)}, f32[16,128,1]{2,1,0:T(8,128)}) custom-call(f32[1,4096]{1,0:T(1,128)} %and_select_fusion.bias_ref, s32[1,96]{1,0:T(1,128)} %compare_select_fusion.14.rank_ref, bf16[128,2048]{1,0:T(8,128)(2,1)} %bitcast.161, bf16[64,128,256]{2,1,0:T(8,128)(2,1)} %bitcast.154, ...), custom_call_target="tpu_custom_call" | custom-call | tf_op jit(solution)/shard_map/pallas_call | solution.py:66
  88.2 1.7 %reduce.1 = f32[16,128]{1,0:T(8,128)S(1)} reduce(f32[16,128,1]{2,1,0:T(8,128)} %get-tuple-element.15, f32[]{:T(128)} %constant.250), dimensions={2}, to_apply=%get-tuple-element.15.reduce_sub_computation | reduce | bytes 16388 | tf_op jit(solution)/shard_map/pallas_call | solution.py:66
  90.0 1.6 reduce.2
  92.9 2.3 %dynamic-slice_bitcast_fusion.1 = bf16[16,2,64,256]{3,2,1,0:T(8,128)(2,1)} fusion(bf16[4,16,2,64,256]{4,3,2,1,0:T(8,128)(2,1)} %multiply_convert_fusion, s32[]{:T(128)S(6)} %select_n.305), kind=kLoop, calls=%fused_computation.40 | loop fusion | bytes 2097156 | tf_op jit(solution)/shard_map/jit(dynamic_index_in_dim)/squeeze | solution.py:229
  96.0 3.6 %constant_dynamic-slice_fusion.2 = (bf16[1,16,2,64,256]{4,3,2,1,0:T(8,128)(2,1)S(1)}, bf16[16,2,64,256]{3,2,1,0:T(8,128)(2,1)}, bf16[16,2,64,256]{3,2,1,0:T(8,128)(2,1)}) fusion(bf16[4,16,2,64,256]{4,3,2,1,0:T(8,128)(2,1)} %multiply_convert_fusion, s32[]{:T(128)S(6)} %select_n.301, s32[]{:T(128)S(6)} %select_n.307, s32[]{:T(128)S(6)} %select_n.303), kind=kLoop, calls=%fused_computation.113 | loop fusion | bytes 6291468 | tf_op jit(solution)/shard_map/jit(dynamic_index_in_dim)/dynamic_slice | solution.py:250
  105.5 43.8 %collective-permute-done.9 = f32[32,2080]{1,0:T(8,128)S(1)} collective-permute-done((f32[32,2080]{1,0:T(8,128)S(1)}, f32[32,2080]{1,0:T(8,128)S(1)}, u32[]{:S(2)}, u32[]{:S(2)}) %collective-permute-start.9) | collective-permute-done | bytes 266272 | tf_op jit(solution)/shard_map/ppermute | solution.py:167
  150.7 2.1 %pad_maximum_fusion = bf16[4,16,2,64,256]{4,3,2,1,0:T(8,128)(2,1)S(1)} fusion(bf16[1,16,2,64,256]{4,3,2,1,0:T(8,128)(2,1)} %bitcast.57, bf16[1,16,2,64,256]{4,3,2,1,0:T(8,128)(2,1)} %bitcast.55, bf16[1,16,2,64,256]{4,3,2,1,0:T(8,128)(2,1)} %bitcast.53, bf16[1,16,2,64,256]{4,3,2,1,0:T(8,128)(2,1)S(1)} %get-tuple-element.32), kind=kLoop, calls=%fused_computation.11 | loop fusion | flops 6291456 | bytes 8388608 | tf_op jit(solution)/shard_map/stack | solution.py:263
  152.9 1.8 %slice_bitcast_fusion.1 = (bf16[64,64,256]{2,1,0:T(8,128)(2,1)}, bf16[64,64,256]{2,1,0:T(8,128)(2,1)S(1)}) fusion(bf16[64,2,64,256]{3,2,1,0:T(8,128)(2,1)S(1)} %bitcast.156), kind=kLoop, calls=%fused_computation.25 | loop fusion | bytes 8388608 | tf_op jit(solution)/shard_map/squeeze | solution.py:281
  154.7 2.2 %gather_fusion.6 = bf16[32,64,256]{2,1,0:T(8,128)(2,1)S(1)} fusion(bf16[64,64,256]{2,1,0:T(8,128)(2,1)} %get-tuple-element.30, s32[1024]{0:T(1024)S(1)} %pad_clamp_fusion), kind=kCustom, calls=%fused_computation.clone | custom fusion | bytes 2097280 | tf_op jit(solution)/shard_map/jit(_take)/gather | solution.py:281
  156.9 1.6 gather_fusion.7
  158.5 1.5 broadcast_select_fusion.1
  161.5 1.5 pad_maximum_fusion.1
  (138 shorter events, 32.6 us)
Async XLA Ops:
  0.6 15.6 %copy-start = (bf16[48,2,64,256]{3,2,1,0:T(8,128)(2,1)S(1)}, bf16[48,2,64,256]{3,2,1,0:T(8,128)(2,1)}, u32[]{:S(2)}) copy-start(bf16[48,2,64,256]{3,2,1,0:T(8,128)(2,1)} %param.17) | copy-start | bytes 9437188
  0.6 3.8 %copy-start.2 = (bf16[64,8192]{1,0:T(8,128)(2,1)S(1)}, bf16[64,8192]{1,0:T(8,128)(2,1)}, u32[]{:S(2)}) copy-start(bf16[64,8192]{1,0:T(8,128)(2,1)} %param.13) | copy-start | bytes 3145732
  0.7 4.2 %copy-start.3 = (bf16[32,8192]{1,0:T(8,128)(2,1)S(1)}, bf16[32,8192]{1,0:T(8,128)(2,1)}, u32[]{:S(2)}) copy-start(bf16[32,8192]{1,0:T(8,128)(2,1)} %param.12) | copy-start | bytes 1572868
  6.4 4.6 %copy-start.8 = (s32[128]{0:T(128)S(1)}, s32[128]{0:T(128)}, u32[]{:S(2)}) copy-start(s32[128]{0:T(128)} %param.20) | copy-start | bytes 1540
  6.4 5.2 %copy-start.9 = (s32[128,1]{0,1:T(1,128)S(1)}, s32[128,1]{0,1:T(1,128)}, u32[]{:S(2)}) copy-start(s32[128,1]{0,1:T(1,128)} %param.19) | copy-start | bytes 1540
  6.4 7.2 %copy-start.6 = (s32[256]{0:T(256)S(1)}, s32[256]{0:T(256)}, u32[]{:S(2)}) copy-start(s32[256]{0:T(256)} %param.21) | copy-start | bytes 3076
  6.4 8.5 %copy-start.7 = (bf16[48,2,2]{0,2,1:T(2,128)(2,1)S(1)}, bf16[48,2,2]{0,2,1:T(2,128)(2,1)}, u32[]{:S(2)}) copy-start(bf16[48,2,2]{0,2,1:T(2,128)(2,1)} %param.18) | copy-start | bytes 1156
  6.4 25.3 %all-to-all-start = ((bf16[96,4,2048]{2,0,1:T(8,128)(2,1)}), bf16[96,4,2048]{2,0,1:T(8,128)(2,1)}, u32[]{:S(2)}, u32[]{:S(2)}) async-start(bf16[96,4,2048]{2,0,1:T(8,128)(2,1)} %bitcast.158), calls=%async_computation | async-start | bytes 3145728 | tf_op jit(solution)/shard_map/all_to_all | solution.py:225
  35.8 6.0 %collective-permute-start.4 = (f32[2,96,2,256]{3,1,0,2:T(8,128)S(1)}, f32[2,96,2,256]{3,1,0,2:T(8,128)S(1)}, u32[]{:S(2)}, u32[]{:S(2)}) collective-permute-start(f32[2,96,2,256]{3,1,0,2:T(8,128)S(1)} %dynamic-slice_bitcast_fusion.6), channel_id=1, source_target_pairs={{0,4},{4,0},{8,12},{12,8},{1,5},{5,1},{9,13},{13,9},{2,6},{6,2},{1... | collective-permute-start | bytes 1179656 | tf_op jit(solution)/shard_map/ppermute | solution.py:116
  40.6 2.2 %collective-permute-start = (f32[2,32,2048]{2,1,0:T(8,128)S(1)}, f32[2,32,2048]{2,1,0:T(8,128)}, u32[]{:S(2)}, u32[]{:S(2)}) collective-permute-start(f32[2,32,2048]{2,1,0:T(8,128)S(1)} %dynamic-slice_bitcast_fusion.5), channel_id=1, source_target_pairs={{0,4},{4,0},{8,12},{12,8},{1,5},{5,1},{9,13},{13,9},{2,6},{6,2},{1... | collective-permute-start | bytes 1572872 | tf_op jit(solution)/shard_map/ppermute | solution.py:116
  41.9 6.9 %collective-permute-start.5 = (f32[96,2,256]{2,0,1:T(8,128)S(1)}, f32[96,2,256]{2,0,1:T(8,128)S(1)}, u32[]{:S(2)}, u32[]{:S(2)}) collective-permute-start(f32[96,2,256]{2,0,1:T(8,128)S(1)} %dynamic-slice_bitcast_fusion.10), channel_id=1, source_target_pairs={{0,8},{4,12},{8,0},{12,4},{1,9},{5,13},{9,1},{13,5},{2,10},{6,14},... | collective-permute-start | bytes 589832 | tf_op jit(solution)/shard_map/ppermute | solution.py:123
  48.8 5.7 %collective-permute-start.6 = (bf16[96,2,256]{2,0,1:T(8,128)(2,1)S(1)}, bf16[96,2,256]{2,0,1:T(8,128)(2,1)S(1)}, u32[]{:S(2)}, u32[]{:S(2)}) collective-permute-start(bf16[96,2,256]{2,0,1:T(8,128)(2,1)S(1)} %fusion.24), channel_id=1, source_target_pairs={{0,8},{4,12},{8,0},{12,4},{1,9},{5,13},{9,1},{13,5},{2,10},{6,14},... | collective-permute-start | bytes 294920 | tf_op jit(solution)/shard_map/ppermute | solution.py:126
  49.2 9.2 %collective-permute-start.1 = (f32[32,2048]{1,0:T(8,128)S(1)}, f32[32,2048]{1,0:T(8,128)S(1)}, u32[]{:S(2)}, u32[]{:S(2)}) collective-permute-start(f32[32,2048]{1,0:T(8,128)S(1)} %dynamic-slice_bitcast_fusion.9), channel_id=1, source_target_pairs={{0,8},{4,12},{8,0},{12,4},{1,9},{5,13},{9,1},{13,5},{2,10},{6,14},... | collective-permute-start | bytes 786440 | tf_op jit(solution)/shard_map/ppermute | solution.py:123
  55.2 4.0 %collective-permute-start.7 = (bf16[2,96,2,256]{3,1,2,0:T(8,128)(2,1)S(1)}, bf16[2,96,2,256]{3,1,2,0:T(8,128)(2,1)S(1)}, u32[]{:S(2)}, u32[]{:S(2)}) collective-permute-start(bf16[2,96,2,256]{3,1,2,0:T(8,128)(2,1)S(1)} %broadcast_select_fusion.3), channel_id=1, source_target_pairs={{0,4},{4,0},{8,12},{12,8},{1,5},{5,1},{9,13},{13,9},{2,6},{6,2},{1... | collective-permute-start | bytes 589832 | tf_op jit(solution)/shard_map/ppermute | solution.py:130
  58.4 5.0 %collective-permute-start.2 = (bf16[32,2048]{1,0:T(8,128)(2,1)S(1)}, bf16[32,2048]{1,0:T(8,128)(2,1)S(1)}, u32[]{:S(2)}, u32[]{:S(2)}) collective-permute-start(bf16[32,2048]{1,0:T(8,128)(2,1)S(1)} %fusion.22), channel_id=1, source_target_pairs={{0,8},{4,12},{8,0},{12,4},{1,9},{5,13},{9,1},{13,5},{2,10},{6,14},... | collective-permute-start | bytes 393224 | tf_op jit(solution)/shard_map/ppermute | solution.py:126
  64.1 1.6 collective-permute-start.3
  88.2 3.4 %copy-start.4 = (f32[128,2048]{1,0:T(8,128)S(1)}, f32[128,2048]{1,0:T(8,128)}, u32[]{:S(2)}) copy-start(f32[128,2048]{1,0:T(8,128)} %get-tuple-element.14) | copy-start | bytes 3145732
  92.8 7.8 %collective-permute-start.8 = (f32[2,32,2080]{2,1,0:T(8,128)}, f32[2,32,2080]{2,1,0:T(8,128)S(1)}, u32[]{:S(2)}, u32[]{:S(2)}) collective-permute-start(f32[2,32,2080]{2,1,0:T(8,128)} %get-tuple-element.36), channel_id=1, source_target_pairs={{0,4},{4,0},{8,12},{12,8},{1,5},{5,1},{9,13},{13,9},{2,6},{6,2},{1... | collective-permute-start | bytes 1597448 | tf_op jit(solution)/shard_map/ppermute | solution.py:163
  95.3 55.5 %collective-permute-start.11 = (bf16[16,2,64,256]{3,2,1,0:T(8,128)(2,1)}, bf16[16,2,64,256]{3,2,1,0:T(8,128)(2,1)}, u32[]{:S(2)}, u32[]{:S(2)}) collective-permute-start(bf16[16,2,64,256]{3,2,1,0:T(8,128)(2,1)} %dynamic-slice_bitcast_fusion.1), channel_id=1, source_target_pairs={{0,8},{4,12},{8,0},{12,4},{1,9},{5,13},{9,1},{13,5},{2,10},{6,14},... | collective-permute-start | bytes 3145736 | tf_op jit(solution)/shard_map/ppermute | solution.py:228
  99.7 51.1 %collective-permute-start.12 = (bf16[16,2,64,256]{3,2,1,0:T(8,128)(2,1)}, bf16[16,2,64,256]{3,2,1,0:T(8,128)(2,1)}, u32[]{:S(2)}, u32[]{:S(2)}) collective-permute-start(bf16[16,2,64,256]{3,2,1,0:T(8,128)(2,1)} %get-tuple-element.33), channel_id=1, source_target_pairs={{0,12},{4,0},{8,4},{12,8},{1,13},{5,1},{9,5},{13,9},{2,14},{6,2},{... | collective-permute-start | bytes 3145736 | tf_op jit(solution)/shard_map/ppermute | solution.py:257
  100.6 50.1 %collective-permute-start.10 = (bf16[16,2,64,256]{3,2,1,0:T(8,128)(2,1)}, bf16[16,2,64,256]{3,2,1,0:T(8,128)(2,1)}, u32[]{:S(2)}, u32[]{:S(2)}) collective-permute-start(bf16[16,2,64,256]{3,2,1,0:T(8,128)(2,1)} %get-tuple-element.34), channel_id=1, source_target_pairs={{0,4},{4,8},{8,12},{12,0},{1,5},{5,9},{9,13},{13,1},{2,6},{6,10},{... | collective-permute-start | bytes 3145736 | tf_op jit(solution)/shard_map/ppermute | solution.py:257
  100.6 0.8 copy-start.5
  104.2 45.1 %collective-permute-start.9 = (f32[32,2080]{1,0:T(8,128)S(1)}, f32[32,2080]{1,0:T(8,128)S(1)}, u32[]{:S(2)}, u32[]{:S(2)}) collective-permute-start(f32[32,2080]{1,0:T(8,128)S(1)} %get-tuple-element.38), channel_id=1, source_target_pairs={{0,8},{4,12},{8,0},{12,4},{1,9},{5,13},{9,1},{13,5},{2,10},{6,14},... | collective-permute-start | bytes 798728 | tf_op jit(solution)/shard_map/ppermute | solution.py:167
  160.8 2.3 %copy-start.1 = (bf16[48,2,64,256]{3,2,1,0:T(8,128)(2,1)S(1)}, bf16[48,2,64,256]{3,2,1,0:T(8,128)(2,1)}, u32[]{:S(2)}) copy-start(bf16[48,2,64,256]{3,2,1,0:T(8,128)(2,1)} %param.17) | copy-start | bytes 9437188

commit v12 on v10

--- a/solution.py
+++ b/solution.py
@@ -162,9 +162,20 @@
     other = lax.dynamic_index_in_dim(by_core, 1 - core, 1, keepdims=False)
     chip_merged = merge([mine, lax.ppermute(other, "ctx", core_pairs(shards))], sums_width)
     parts = [lax.dynamic_index_in_dim(chip_merged, chip, 0, keepdims=False)]
+    heads = (sent.shape[-1] - sums_width) // 2
     for step in range(1, chips):
         send = lax.dynamic_index_in_dim(chip_merged, (chip + step) % chips, 0, keepdims=False)
-        parts.append(lax.ppermute(send, "ctx", shift_pairs(shards, step)))
+        stats = send[..., sums_width:]
+        totals = stats[..., heads:]
+        lead = send.shape[:-1]
+        normed = (
+            send[..., :sums_width].reshape(lead + (heads, HD)) / totals[..., None]
+        ).astype(jnp.bfloat16)
+        got_normed, got_stats = lax.ppermute((normed, stats), "ctx", shift_pairs(shards, step))
+        got_sums = (got_normed.astype(jnp.float32) * got_stats[..., heads:, None]).reshape(
+            lead + (sums_width,)
+        )
+        parts.append(jnp.concatenate([got_sums, got_stats], axis=-1))
     return merge(parts, sums_width)
 
 

time: 165 us -> 163 us (0.988)
  waiting for transfers between devices: 70.3 us -> 66.1 us
    ppermute x1 -> x2, waiting for transfers between devices: 47.3 us -> 43.1 us  [hier_combine(): lax.ppermute((normed, stats), 'ctx', shift_pairs(shards, step))]
  transfers between devices with their start and end apart: 14 -> 15, of which waited for: 8 -> 9; matrix products, arithmetic and copies ran while one was open for 19% -> 20% of each run, Pallas kernels for 0% -> 0%
where the time goes in v12:
time: 163 us; the launch traced here: 162 us
  waiting for transfers between devices  66.1 us (41%)
  other arithmetic  28.1 us (17%)
  local copies, waits for them, and re-layouts  24.7 us (15%)
  Pallas kernels  20.2 us (12%)
  starting transfers between devices  12.7 us (8%)
  matrix products  9.18 us (6%)
    ppermute x2, waiting for transfers between devices, hier_combine(): lax.ppermute((normed, stats), 'ctx', shift_pairs(shards, step))  43.1 us
    pallas_call x1, Pallas kernels, attend(): pl.pallas_call(functools.partial(attn_kernel, score_scale=score_scale, gr...  20.2 us
    ppermute x2, waiting for transfers between devices, hier_reduce_gather(): lax.ppermute(send, 'ctx', shift_pairs(shards, step))  7.82 us
    ppermute x2, waiting for transfers between devices, hier_reduce_gather(): lax.ppermute(rounded, 'ctx', shift_pairs(shards, step))  6.96 us
    convert_element_type x1, other arithmetic, body(): send_blocks = (send_codes.astype(jnp.float32).reshape(shards * capacity,...  6.13 us
    all_to_all x1, waiting for transfers between devices, body(): lax.all_to_all(normed, 'ctx', split_axis=1, concat_axis=0, tiled=True)  5.85 us
    dot_general x1, matrix products, body(): jnp.dot(question_part, w_query, preferred_element_type=jnp.float32)  4.64 us
    all_to_all x1, starting transfers between devices, body(): lax.all_to_all(normed, 'ctx', split_axis=1, concat_axis=0, tiled=True)  4.52 us
  transfers between devices with their start and end apart: 15, of which 9 were waited for; matrix products, arithmetic and copies ran while one was open for 20% of the time, Pallas kernels for 0%

profile of v12, /device:TPU:0, one launch (start us, length us, event | category | flops | bytes accessed | tf_op | source)
XLA Modules:
  0.0 162.3 jit_solution(12941195927620395661)
XLA Ops:
  1.5 1.7 %fusion.6 = f32[64]{0:T(128)S(1)} fusion(bf16[64,8192]{1,0:T(8,128)(2,1)} %param.13), kind=kLoop, calls=%fused_computation.21 | loop fusion | flops 1572800 | bytes 1048832 | tf_op jit(solution)/shard_map/reduce_sum | solution.py:19
  6.4 4.5 %all-to-all-start = ((bf16[96,4,2048]{2,0,1:T(8,128)(2,1)}), bf16[96,4,2048]{2,0,1:T(8,128)(2,1)}, u32[]{:S(2)}, u32[]{:S(2)}) async-start(bf16[96,4,2048]{2,0,1:T(8,128)(2,1)} %bitcast.162), calls=%async_computation | async-start | bytes 3145728 | tf_op jit(solution)/shard_map/all_to_all | solution.py:236
  16.2 2.8 %gather_fusion = bf16[64,2,64,256]{3,2,1,0:T(8,128)(2,1)} fusion(bf16[48,2,64,256]{3,2,1,0:T(8,128)(2,1)S(1)} %copy-done, s32[1024]{0:T(1024)S(1)} %pad_clamp_fusion.3), kind=kCustom, calls=%fused_computation.2 | custom fusion | bytes 8388864 | tf_op jit(solution)/shard_map/jit(_take)/gather | solution.py:218
  19.1 6.1 %multiply_convert_fusion = bf16[4,16,2,64,256]{4,3,2,1,0:T(8,128)(2,1)} fusion(f32[4,16,2,256]{3,2,1,0:T(2,128)S(1)} %mul.144, bf16[4,16,2,64,256]{4,3,2,1,0:T(8,128)(2,1)} %bitcast.160, pred[4,16]{1,0:T(4,128)(4,1)S(1)} %compare_and_fusion.4), kind=kLoop, calls=%fused_computation.10 | loop fusion | flops 8388608 | bytes 8519744 | tf_op jit(solution)/shard_map/convert_element_type | solution.py:223
  25.8 5.9 %all-to-all-done = bf16[96,4,2048]{2,0,1:T(8,128)(2,1)} async-done(((bf16[96,4,2048]{2,0,1:T(8,128)(2,1)}), bf16[96,4,2048]{2,0,1:T(8,128)(2,1)}, u32[]{:S(2)}, u32[]{:S(2)}) %all-to-all-start) | async-done | bytes 1572896 | tf_op jit(solution)/shard_map/all_to_all | solution.py:236
  32.8 3.0 %fusion.9 = f32[2,2,96,2,256]{4,2,3,1,0:T(8,128)S(1)} fusion(bf16[2,2,96,2048,1]{3,2,4,1,0:T(8,128)(2,1)} %bitcast.21, bf16[2048,2,256,1,1]{2,1,0,4,3:T(2,128)(2,1)} %bitcast.185), kind=kOutput, calls=%fused_computation.27 | convolution fusion | flops 805306368 | bytes 4456448 | tf_op jit(solution)/shard_map/tk,kcn->tcn/dot_general | solution.py:241
  35.9 4.6 %fusion = f32[2,2,32,2048]{3,2,1,0:T(8,128)S(1)} fusion(bf16[2,2,32,2048]{3,2,1,0:T(8,128)(2,1)S(1)} %bitcast.164, bf16[2048,2048]{1,0:T(8,128)(2,1)} %param.15), kind=kOutput, calls=%fused_computation.8 | convolution fusion | flops 1073741824 | bytes 9961472 | tf_op jit(solution)/shard_map/dot_general | solution.py:240
  44.0 4.9 %collective-permute-done.5 = f32[96,2,256]{2,0,1:T(8,128)S(1)} collective-permute-done((f32[96,2,256]{2,0,1:T(8,128)S(1)}, f32[96,2,256]{2,0,1:T(8,128)S(1)}, u32[]{:S(2)}, u32[]{:S(2)}) %collective-permute-start.5) | collective-permute-done | bytes 196640 | tf_op jit(solution)/shard_map/ppermute | solution.py:123
  49.2 1.8 %collective-permute-start.1 = (f32[32,2048]{1,0:T(8,128)S(1)}, f32[32,2048]{1,0:T(8,128)S(1)}, u32[]{:S(2)}, u32[]{:S(2)}) collective-permute-start(f32[32,2048]{1,0:T(8,128)S(1)} %dynamic-slice_bitcast_fusion.9), channel_id=1, source_target_pairs={{0,8},{4,12},{8,0},{12,4},{1,9},{5,13},{9,1},{13,5},{2,10},{6,14},... | collective-permute-start | bytes 786440 | tf_op jit(solution)/shard_map/ppermute | solution.py:123
  51.0 3.6 %collective-permute-done.6 = bf16[96,2,256]{2,0,1:T(8,128)(2,1)S(1)} collective-permute-done((bf16[96,2,256]{2,0,1:T(8,128)(2,1)S(1)}, bf16[96,2,256]{2,0,1:T(8,128)(2,1)S(1)}, u32[]{:S(2)}, u32[]{:S(2)}) %collective-permute-start.6) | collective-permute-done | bytes 98336 | tf_op jit(solution)/shard_map/ppermute | solution.py:126
  55.4 3.0 %collective-permute-done.1 = f32[32,2048]{1,0:T(8,128)S(1)} collective-permute-done((f32[32,2048]{1,0:T(8,128)S(1)}, f32[32,2048]{1,0:T(8,128)S(1)}, u32[]{:S(2)}, u32[]{:S(2)}) %collective-permute-start.1) | collective-permute-done | bytes 262176 | tf_op jit(solution)/shard_map/ppermute | solution.py:123
  60.0 3.4 %collective-permute-done.2 = bf16[32,2048]{1,0:T(8,128)(2,1)S(1)} collective-permute-done((bf16[32,2048]{1,0:T(8,128)(2,1)S(1)}, bf16[32,2048]{1,0:T(8,128)(2,1)S(1)}, u32[]{:S(2)}, u32[]{:S(2)}) %collective-permute-start.2) | collective-permute-done | bytes 131104 | tf_op jit(solution)/shard_map/ppermute | solution.py:126
  68.0 20.2 %shard_map.113 = (f32[128,2048]{1,0:T(8,128)}, f32[16,128,1]{2,1,0:T(8,128)}, f32[16,128,1]{2,1,0:T(8,128)}) custom-call(f32[1,4096]{1,0:T(1,128)} %and_select_fusion.bias_ref, s32[1,96]{1,0:T(1,128)} %compare_select_fusion.14.rank_ref, bf16[128,2048]{1,0:T(8,128)(2,1)} %bitcast.165, bf16[64,128,256]{2,1,0:T(8,128)(2,1)} %bitcast.158, ...), custom_call_target="tpu_custom_call" | custom-call | tf_op jit(solution)/shard_map/pallas_call | solution.py:66
  88.3 1.7 %reduce.1 = f32[16,128]{1,0:T(8,128)S(1)} reduce(f32[16,128,1]{2,1,0:T(8,128)} %get-tuple-element.12, f32[]{:T(128)} %constant.250), dimensions={2}, to_apply=%get-tuple-element.12.reduce_sub_computation | reduce | bytes 16388 | tf_op jit(solution)/shard_map/pallas_call | solution.py:66
  90.0 1.6 reduce.2
  93.4 4.1 %constant_dynamic-slice_fusion.2 = (bf16[1,16,2,64,256]{4,3,2,1,0:T(8,128)(2,1)S(1)}, bf16[16,2,64,256]{3,2,1,0:T(8,128)(2,1)}, bf16[16,2,64,256]{3,2,1,0:T(8,128)(2,1)}, bf16[16,2,64,256]{3,2,1,0:T(8,128)(2,1)}) fusion(bf16[4,16,2,64,256]{4,3,2,1,0:T(8,128)(2,1)} %multiply_convert_fusion, s32[]{:T(128)S(6)} %select_n.301, s32[]{:T(128)S(6)} %select_n.307, ...), kind=kLoop, calls=%fused_computation.115 | loop fusion | bytes 8388624 | tf_op jit(solution)/shard_map/jit(dynamic_index_in_dim)/dynamic_slice | solution.py:254
  105.7 40.8 %collective-permute-done.9 = f32[32,32]{1,0:T(8,128)S(1)} collective-permute-done((f32[32,32]{1,0:T(8,128)S(1)}, f32[32,32]{1,0:T(8,128)S(1)}, u32[]{:S(2)}, u32[]{:S(2)}) %collective-permute-start.9) | collective-permute-done | bytes 4128 | tf_op jit(solution)/shard_map/ppermute | solution.py:174
  146.6 2.3 %collective-permute-done.10 = bf16[32,16,128]{2,1,0:T(8,128)(2,1)S(1)} collective-permute-done((bf16[32,16,128]{2,1,0:T(8,128)(2,1)S(1)}, bf16[32,16,128]{2,1,0:T(8,128)(2,1)S(1)}, u32[]{:S(2)}, u32[]{:S(2)}) %collective-permute-start.10) | collective-permute-done | bytes 131104 | tf_op jit(solution)/shard_map/ppermute | solution.py:174
  150.0 2.1 %pad_maximum_fusion = bf16[4,16,2,64,256]{4,3,2,1,0:T(8,128)(2,1)S(1)} fusion(bf16[1,16,2,64,256]{4,3,2,1,0:T(8,128)(2,1)} %bitcast.57, bf16[1,16,2,64,256]{4,3,2,1,0:T(8,128)(2,1)} %bitcast.55, bf16[1,16,2,64,256]{4,3,2,1,0:T(8,128)(2,1)} %bitcast.53, bf16[1,16,2,64,256]{4,3,2,1,0:T(8,128)(2,1)S(1)} %get-tuple-element.28), kind=kLoop, calls=%fused_computation.11 | loop fusion | flops 6291456 | bytes 8388608 | tf_op jit(solution)/shard_map/stack | solution.py:264
  152.1 1.8 %slice_bitcast_fusion.1 = (bf16[64,64,256]{2,1,0:T(8,128)(2,1)}, bf16[64,64,256]{2,1,0:T(8,128)(2,1)S(1)}) fusion(bf16[64,2,64,256]{3,2,1,0:T(8,128)(2,1)S(1)} %bitcast.161), kind=kLoop, calls=%fused_computation.25 | loop fusion | bytes 8388608 | tf_op jit(solution)/shard_map/squeeze | solution.py:282
  154.0 2.2 %gather_fusion.6 = bf16[32,64,256]{2,1,0:T(8,128)(2,1)S(1)} fusion(bf16[64,64,256]{2,1,0:T(8,128)(2,1)} %get-tuple-element.26, s32[1024]{0:T(1024)S(1)} %pad_clamp_fusion), kind=kCustom, calls=%fused_computation.clone | custom fusion | bytes 2097280 | tf_op jit(solution)/shard_map/jit(_take)/gather | solution.py:282
  156.2 1.6 gather_fusion.7
  157.7 1.5 broadcast_select_fusion.1
  160.8 1.5 pad_maximum_fusion.1
  (147 shorter events, 34.3 us)
Async XLA Ops:
  0.6 15.6 %copy-start = (bf16[48,2,64,256]{3,2,1,0:T(8,128)(2,1)S(1)}, bf16[48,2,64,256]{3,2,1,0:T(8,128)(2,1)}, u32[]{:S(2)}) copy-start(bf16[48,2,64,256]{3,2,1,0:T(8,128)(2,1)} %param.17) | copy-start | bytes 9437188
  0.6 3.8 %copy-start.2 = (bf16[64,8192]{1,0:T(8,128)(2,1)S(1)}, bf16[64,8192]{1,0:T(8,128)(2,1)}, u32[]{:S(2)}) copy-start(bf16[64,8192]{1,0:T(8,128)(2,1)} %param.13) | copy-start | bytes 3145732
  0.7 4.2 %copy-start.3 = (bf16[32,8192]{1,0:T(8,128)(2,1)S(1)}, bf16[32,8192]{1,0:T(8,128)(2,1)}, u32[]{:S(2)}) copy-start(bf16[32,8192]{1,0:T(8,128)(2,1)} %param.12) | copy-start | bytes 1572868
  6.4 4.6 %copy-start.9 = (s32[128]{0:T(128)S(1)}, s32[128]{0:T(128)}, u32[]{:S(2)}) copy-start(s32[128]{0:T(128)} %param.20) | copy-start | bytes 1540
  6.4 5.2 %copy-start.10 = (s32[128,1]{0,1:T(1,128)S(1)}, s32[128,1]{0,1:T(1,128)}, u32[]{:S(2)}) copy-start(s32[128,1]{0,1:T(1,128)} %param.19) | copy-start | bytes 1540
  6.4 7.2 %copy-start.7 = (s32[256]{0:T(256)S(1)}, s32[256]{0:T(256)}, u32[]{:S(2)}) copy-start(s32[256]{0:T(256)} %param.21) | copy-start | bytes 3076
  6.4 8.5 %copy-start.8 = (bf16[48,2,2]{0,2,1:T(2,128)(2,1)S(1)}, bf16[48,2,2]{0,2,1:T(2,128)(2,1)}, u32[]{:S(2)}) copy-start(bf16[48,2,2]{0,2,1:T(2,128)(2,1)} %param.18) | copy-start | bytes 1156
  6.4 25.3 %all-to-all-start = ((bf16[96,4,2048]{2,0,1:T(8,128)(2,1)}), bf16[96,4,2048]{2,0,1:T(8,128)(2,1)}, u32[]{:S(2)}, u32[]{:S(2)}) async-start(bf16[96,4,2048]{2,0,1:T(8,128)(2,1)} %bitcast.162), calls=%async_computation | async-start | bytes 3145728 | tf_op jit(solution)/shard_map/all_to_all | solution.py:236
  35.8 6.0 %collective-permute-start.4 = (f32[2,96,2,256]{3,1,2,0:T(8,128)S(1)}, f32[2,96,2,256]{3,1,2,0:T(8,128)S(1)}, u32[]{:S(2)}, u32[]{:S(2)}) collective-permute-start(f32[2,96,2,256]{3,1,2,0:T(8,128)S(1)} %dynamic-slice_bitcast_fusion.6), channel_id=1, source_target_pairs={{0,4},{4,0},{8,12},{12,8},{1,5},{5,1},{9,13},{13,9},{2,6},{6,2},{1... | collective-permute-start | bytes 1179656 | tf_op jit(solution)/shard_map/ppermute | solution.py:116
  40.6 2.2 %collective-permute-start = (f32[2,32,2048]{2,1,0:T(8,128)S(1)}, f32[2,32,2048]{2,1,0:T(8,128)}, u32[]{:S(2)}, u32[]{:S(2)}) collective-permute-start(f32[2,32,2048]{2,1,0:T(8,128)S(1)} %dynamic-slice_bitcast_fusion.5), channel_id=1, source_target_pairs={{0,4},{4,0},{8,12},{12,8},{1,5},{5,1},{9,13},{13,9},{2,6},{6,2},{1... | collective-permute-start | bytes 1572872 | tf_op jit(solution)/shard_map/ppermute | solution.py:116
  41.9 6.9 %collective-permute-start.5 = (f32[96,2,256]{2,0,1:T(8,128)S(1)}, f32[96,2,256]{2,0,1:T(8,128)S(1)}, u32[]{:S(2)}, u32[]{:S(2)}) collective-permute-start(f32[96,2,256]{2,0,1:T(8,128)S(1)} %dynamic-slice_bitcast_fusion.10), channel_id=1, source_target_pairs={{0,8},{4,12},{8,0},{12,4},{1,9},{5,13},{9,1},{13,5},{2,10},{6,14},... | collective-permute-start | bytes 589832 | tf_op jit(solution)/shard_map/ppermute | solution.py:123
  48.8 5.7 %collective-permute-start.6 = (bf16[96,2,256]{2,0,1:T(8,128)(2,1)S(1)}, bf16[96,2,256]{2,0,1:T(8,128)(2,1)S(1)}, u32[]{:S(2)}, u32[]{:S(2)}) collective-permute-start(bf16[96,2,256]{2,0,1:T(8,128)(2,1)S(1)} %fusion.25), channel_id=1, source_target_pairs={{0,8},{4,12},{8,0},{12,4},{1,9},{5,13},{9,1},{13,5},{2,10},{6,14},... | collective-permute-start | bytes 294920 | tf_op jit(solution)/shard_map/ppermute | solution.py:126
  49.2 9.2 %collective-permute-start.1 = (f32[32,2048]{1,0:T(8,128)S(1)}, f32[32,2048]{1,0:T(8,128)S(1)}, u32[]{:S(2)}, u32[]{:S(2)}) collective-permute-start(f32[32,2048]{1,0:T(8,128)S(1)} %dynamic-slice_bitcast_fusion.9), channel_id=1, source_target_pairs={{0,8},{4,12},{8,0},{12,4},{1,9},{5,13},{9,1},{13,5},{2,10},{6,14},... | collective-permute-start | bytes 786440 | tf_op jit(solution)/shard_map/ppermute | solution.py:123
  55.3 4.0 %collective-permute-start.7 = (bf16[2,96,2,256]{3,1,2,0:T(8,128)(2,1)S(1)}, bf16[2,96,2,256]{3,1,2,0:T(8,128)(2,1)S(1)}, u32[]{:S(2)}, u32[]{:S(2)}) collective-permute-start(bf16[2,96,2,256]{3,1,2,0:T(8,128)(2,1)S(1)} %broadcast_select_fusion.3), channel_id=1, source_target_pairs={{0,4},{4,0},{8,12},{12,8},{1,5},{5,1},{9,13},{13,9},{2,6},{6,2},{1... | collective-permute-start | bytes 589832 | tf_op jit(solution)/shard_map/ppermute | solution.py:130
  58.4 5.0 %collective-permute-start.2 = (bf16[32,2048]{1,0:T(8,128)(2,1)S(1)}, bf16[32,2048]{1,0:T(8,128)(2,1)S(1)}, u32[]{:S(2)}, u32[]{:S(2)}) collective-permute-start(bf16[32,2048]{1,0:T(8,128)(2,1)S(1)} %fusion.23), channel_id=1, source_target_pairs={{0,8},{4,12},{8,0},{12,4},{1,9},{5,13},{9,1},{13,5},{2,10},{6,14},... | collective-permute-start | bytes 393224 | tf_op jit(solution)/shard_map/ppermute | solution.py:126
  60.0 33.4 %copy-start.4 = (bf16[4,96,2,256]{3,1,2,0:T(8,128)(2,1)}, bf16[4,96,2,256]{3,1,2,0:T(8,128)(2,1)S(1)}, u32[]{:S(2)}) copy-start(bf16[4,96,2,256]{3,1,2,0:T(8,128)(2,1)S(1)} %bitcast_select_fusion.1) | copy-start | bytes 1179652
  64.2 1.6 collective-permute-start.3
  92.9 6.7 %collective-permute-start.8 = (f32[2,32,2080]{2,1,0:T(8,128)}, f32[2,32,2080]{2,1,0:T(8,128)S(1)}, u32[]{:S(2)}, u32[]{:S(2)}) collective-permute-start(f32[2,32,2080]{2,1,0:T(8,128)} %get-tuple-element.33), channel_id=1, source_target_pairs={{0,4},{4,0},{8,12},{12,8},{1,5},{5,1},{9,13},{13,9},{2,6},{6,2},{1... | collective-permute-start | bytes 1597448 | tf_op jit(solution)/shard_map/ppermute | solution.py:163
  93.4 6.1 %slice-start = ((bf16[4,96,2,256]{3,1,2,0:T(8,128)(2,1)}), bf16[4,64,2,256]{3,1,2,0:T(8,128)(2,1)S(1)}, s32[]{:S(2)}) async-start(bf16[4,96,2,256]{3,1,2,0:T(8,128)(2,1)} %copy-done.4), calls=%async_computation.1 | async-start | bytes 524288 | tf_op jit(solution)/shard_map/slice | solution.py:267
  97.5 52.5 %collective-permute-start.13 = (bf16[16,2,64,256]{3,2,1,0:T(8,128)(2,1)}, bf16[16,2,64,256]{3,2,1,0:T(8,128)(2,1)}, u32[]{:S(2)}, u32[]{:S(2)}) collective-permute-start(bf16[16,2,64,256]{3,2,1,0:T(8,128)(2,1)} %get-tuple-element.29), channel_id=1, source_target_pairs={{0,12},{4,0},{8,4},{12,8},{1,13},{5,1},{9,5},{13,9},{2,14},{6,2},{... | collective-permute-start | bytes 3145736 | tf_op jit(solution)/shard_map/ppermute | solution.py:258
  98.3 51.7 %collective-permute-start.12 = (bf16[16,2,64,256]{3,2,1,0:T(8,128)(2,1)}, bf16[16,2,64,256]{3,2,1,0:T(8,128)(2,1)}, u32[]{:S(2)}, u32[]{:S(2)}) collective-permute-start(bf16[16,2,64,256]{3,2,1,0:T(8,128)(2,1)} %get-tuple-element.30), channel_id=1, source_target_pairs={{0,8},{4,12},{8,0},{12,4},{1,9},{5,13},{9,1},{13,5},{2,10},{6,14},... | collective-permute-start | bytes 3145736 | tf_op jit(solution)/shard_map/ppermute | solution.py:258
  99.5 50.5 %collective-permute-start.11 = (bf16[16,2,64,256]{3,2,1,0:T(8,128)(2,1)}, bf16[16,2,64,256]{3,2,1,0:T(8,128)(2,1)}, u32[]{:S(2)}, u32[]{:S(2)}) collective-permute-start(bf16[16,2,64,256]{3,2,1,0:T(8,128)(2,1)} %get-tuple-element.31), channel_id=1, source_target_pairs={{0,4},{4,8},{8,12},{12,0},{1,5},{5,9},{9,13},{13,1},{2,6},{6,10},{... | collective-permute-start | bytes 3145736 | tf_op jit(solution)/shard_map/ppermute | solution.py:258
  103.3 43.2 %collective-permute-start.9 = (f32[32,32]{1,0:T(8,128)S(1)}, f32[32,32]{1,0:T(8,128)S(1)}, u32[]{:S(2)}, u32[]{:S(2)}) collective-permute-start(f32[32,32]{1,0:T(8,128)S(1)} %slice.117), channel_id=1, source_target_pairs={{0,8},{4,12},{8,0},{12,4},{1,9},{5,13},{9,1},{13,5},{2,10},{6,14},... | collective-permute-start | bytes 12296 | tf_op jit(solution)/shard_map/ppermute | solution.py:174
  104.4 44.5 %collective-permute-start.10 = (bf16[32,16,128]{2,1,0:T(8,128)(2,1)S(1)}, bf16[32,16,128]{2,1,0:T(8,128)(2,1)S(1)}, u32[]{:S(2)}, u32[]{:S(2)}) collective-permute-start(bf16[32,16,128]{2,1,0:T(8,128)(2,1)S(1)} %fusion.18), channel_id=1, source_target_pairs={{0,8},{4,12},{8,0},{12,4},{1,9},{5,13},{9,1},{13,5},{2,10},{6,14},... | collective-permute-start | bytes 393224 | tf_op jit(solution)/shard_map/ppermute | solution.py:174
  (3 other events, 6.5 us)

commit v13 on v12

--- a/solution.py
+++ b/solution.py
@@ -233,7 +233,20 @@
     normed = jnp.concatenate(
         [rms_rows(question_hidden, norm_gain), rms_rows(recomp_hidden, norm_gain)], axis=0
     )
-    pieces = lax.all_to_all(normed, "ctx", split_axis=1, concat_axis=0, tiled=True)
+    width_share = normed.shape[1] // shards
+    from_shift = [lax.dynamic_slice_in_dim(normed, own_index * width_share, width_share, 1)]
+    for step in range(1, shards):
+        target = (own_index + step) % shards
+        from_shift.append(
+            lax.ppermute(
+                lax.dynamic_slice_in_dim(normed, target * width_share, width_share, 1),
+                "ctx",
+                [(i, (i + step) % shards) for i in range(shards)],
+            )
+        )
+    pieces = jnp.take(
+        jnp.stack(from_shift), (own_index - jnp.arange(shards)) % shards, axis=0
+    ).reshape(shards * row_count, width_share)
     width_part = pieces.shape[1]
     arranged = pieces.reshape(shards, row_count, width_part)
     question_part = arranged[:, :q_rows, :].reshape(shards * q_rows, width_part)

time: 163 us -> 184 us (1.13)
  other arithmetic: 28.1 us -> 48.1 us
  local copies, waits for them, and re-layouts: 24.7 us -> 31.5 us
  waiting for transfers between devices: 66.1 us -> 59.6 us
    all_to_all x1 -> x0, waiting for transfers between devices: 5.85 us -> none  [body(): lax.all_to_all(normed, 'ctx', split_axis=1, concat_axis=0, tiled=True)]
    all_to_all x1 -> x0, starting transfers between devices: 4.52 us -> none  [body(): lax.all_to_all(normed, 'ctx', split_axis=1, concat_axis=0, tiled=True)]
    another operation x0 -> x2, other arithmetic: none -> 3.9 us  [body(): jnp.stack(from_shift)]
    ppermute x0 -> x3, starting transfers between devices: none -> 3.2 us  [body(): lax.ppermute(lax.dynamic_slice_in_dim(normed, target * width_share, width...]
    mul x2, local copies, waits for them, and re-layouts: 0.35 us -> 2.57 us  [body(): send_codes.astype(jnp.float32)]
  transfers between devices with their start and end apart: 15 -> 17, of which waited for: 9 -> 8; matrix products, arithmetic and copies ran while one was open for 20% -> 30% of each run, Pallas kernels for 0% -> 0%
where the time goes in v13:
time: 184 us; the launch traced here: 183 us
  waiting for transfers between devices  59.6 us (32%)
  other arithmetic  48.1 us (26%)
  local copies, waits for them, and re-layouts  31.5 us (17%)
  Pallas kernels  20.2 us (11%)
  starting transfers between devices  13.5 us (7%)
  matrix products  8.81 us (5%)
    ppermute x2, waiting for transfers between devices, hier_combine(): lax.ppermute((normed, stats), 'ctx', shift_pairs(shards, step))  43.2 us
    pallas_call x1, Pallas kernels, attend(): pl.pallas_call(functools.partial(attn_kernel, score_scale=score_scale, gr...  20.2 us
    ppermute x2, waiting for transfers between devices, hier_reduce_gather(): lax.ppermute(send, 'ctx', shift_pairs(shards, step))  7.69 us
    ppermute x2, waiting for transfers between devices, hier_reduce_gather(): lax.ppermute(rounded, 'ctx', shift_pairs(shards, step))  6.96 us
    convert_element_type x1, other arithmetic, body(): send_blocks = (send_codes.astype(jnp.float32).reshape(shards * capacity,...  6.15 us
    dot_general x1, matrix products, body(): jnp.dot(question_part, w_query, preferred_element_type=jnp.float32)  4.71 us
    dynamic_slice x1, local copies, waits for them, and re-layouts, body(): lax.dynamic_index_in_dim(send_later, own_index, 0, keepdims=False)  4.08 us
    another operation x2, other arithmetic, body(): jnp.stack(from_shift)  3.9 us
  transfers between devices with their start and end apart: 17, of which 8 were waited for; matrix products, arithmetic and copies ran while one was open for 30% of the time, Pallas kernels for 0%

profile of v13, /device:TPU:0, one launch (start us, length us, event | category | flops | bytes accessed | tf_op | source)
XLA Modules:
  0.0 183.1 jit_solution(6735596871758269268)
XLA Ops:
  1.6 1.6 fusion.6
  6.8 2.5 %fusion.24 = (bf16[1,96,2048]{2,1,0:T(8,128)(2,1)S(1)}, bf16[96,2048]{1,0:T(8,128)(2,1)}, bf16[96,2048]{1,0:T(8,128)(2,1)}, bf16[96,2048]{1,0:T(8,128)(2,1)}) fusion(s32[]{:T(128)S(6)} %select_n.354, bf16[64,8192]{1,0:T(8,128)(2,1)} %fusion.8, bf16[32,8192]{1,0:T(8,128)(2,1)} %fusion.17, s32[]{:T(128)S(6)} %select_n.356, s32[]{:T(128)S(6)} %select_n.358, ...), kind=kLoop, calls=%fused_computation.69 | loop fusion | flops 3145728 | bytes 3145744 | tf_op jit(solution)/shard_map/stack | solution.py:248
  9.3 2.4 %collective-permute-start.2 = (bf16[96,2048]{1,0:T(8,128)(2,1)}, bf16[96,2048]{1,0:T(8,128)(2,1)}, u32[]{:S(2)}, u32[]{:S(2)}) collective-permute-start(bf16[96,2048]{1,0:T(8,128)(2,1)} %get-tuple-element.35), channel_id=1, source_target_pairs={{0,12},{4,0},{8,4},{12,8},{1,13},{5,1},{9,5},{13,9},{2,14},{6,2},{... | collective-permute-start | bytes 1179656 | tf_op jit(solution)/shard_map/ppermute | solution.py:241
  24.9 2.0 %compare_reduce_fusion = pred[4096]{0:T(1024)(128)(4,1)S(1)} fusion(s32[256]{0:T(256)} %param.21, s32[4096]{0:T(1024)S(1)} %select_n.338), kind=kLoop, calls=%fused_computation.13 | loop fusion | flops 2093056 | bytes 21504 | tf_op jit(solution)/shard_map/reduce_or | solution.py:299
  30.2 2.0 %gather_fusion.1 = bf16[64,2,2]{2,1,0:T(2,128)(2,1)} fusion(bf16[48,2,2]{2,1,0:T(2,128)(2,1)} %copy.31, s32[1024]{0:T(1024)S(1)} %pad_clamp_fusion.4), kind=kCustom, calls=%fused_computation.3 | custom fusion | bytes 1280 | tf_op jit(solution)/shard_map/jit(_take)/gather | solution.py:219
  33.9 1.7 mul.154
  35.6 3.1 %gather_fusion = bf16[64,2,64,256]{3,2,1,0:T(8,128)(2,1)} fusion(bf16[48,2,64,256]{3,2,1,0:T(8,128)(2,1)S(1)} %copy-done, s32[1024]{0:T(1024)} %copy-done.13), kind=kCustom, calls=%fused_computation.2 | custom fusion | bytes 8388864 | tf_op jit(solution)/shard_map/jit(_take)/gather | solution.py:218
  43.7 6.1 %multiply_convert_fusion = bf16[4,16,2,64,256]{4,3,2,1,0:T(8,128)(2,1)} fusion(f32[4,16,2,256]{3,2,1,0:T(2,128)} %mul.154, bf16[4,16,2,64,256]{4,3,2,1,0:T(8,128)(2,1)} %bitcast.161, pred[4,16]{1,0:T(4,128)(4,1)} %compare_and_fusion.6), kind=kLoop, calls=%fused_computation.11 | loop fusion | flops 8388608 | bytes 8519744 | tf_op jit(solution)/shard_map/convert_element_type | solution.py:223
  52.2 2.6 %fusion.9 = f32[2,2,96,2,256]{4,2,3,1,0:T(8,128)S(1)} fusion(bf16[2048,2,256,1,1]{2,1,0,4,3:T(2,128)(2,1)} %bitcast.185, bf16[2,2,96,2048]{3,2,1,0:T(8,128)(2,1)S(1)} %bitcast.163, pred[2,2]{1,0:T(4,128)(4,1)S(1)} %copy-done.22), kind=kOutput, calls=%fused_computation.32 | convolution fusion | flops 806092800 | bytes 4456452 | tf_op jit(solution)/shard_map/tk,kcn->tcn/dot_general | solution.py:254
  56.3 4.7 %fusion = f32[2,2,32,2048]{3,2,1,0:T(8,128)S(1)} fusion(bf16[2,2,32,2048]{3,2,1,0:T(8,128)(2,1)S(1)} %bitcast.164, bf16[2048,2048]{1,0:T(8,128)(2,1)} %param.15), kind=kOutput, calls=%fused_computation.9 | convolution fusion | flops 1073741824 | bytes 9961472 | tf_op jit(solution)/shard_map/dot_general | solution.py:253
  64.7 4.9 %collective-permute-done.8 = f32[96,2,256]{2,0,1:T(8,128)S(1)} collective-permute-done((f32[96,2,256]{2,0,1:T(8,128)S(1)}, f32[96,2,256]{2,0,1:T(8,128)S(1)}, u32[]{:S(2)}, u32[]{:S(2)}) %collective-permute-start.8) | collective-permute-done | bytes 196640 | tf_op jit(solution)/shard_map/ppermute | solution.py:123
  71.7 3.6 %collective-permute-done.9 = bf16[96,2,256]{2,0,1:T(8,128)(2,1)S(1)} collective-permute-done((bf16[96,2,256]{2,0,1:T(8,128)(2,1)S(1)}, bf16[96,2,256]{2,0,1:T(8,128)(2,1)S(1)}, u32[]{:S(2)}, u32[]{:S(2)}) %collective-permute-start.9) | collective-permute-done | bytes 98336 | tf_op jit(solution)/shard_map/ppermute | solution.py:126
  76.3 2.8 %collective-permute-done.4 = f32[32,2048]{1,0:T(8,128)S(1)} collective-permute-done((f32[32,2048]{1,0:T(8,128)S(1)}, f32[32,2048]{1,0:T(8,128)S(1)}, u32[]{:S(2)}, u32[]{:S(2)}) %collective-permute-start.4) | collective-permute-done | bytes 262176 | tf_op jit(solution)/shard_map/ppermute | solution.py:123
  80.7 3.4 %collective-permute-done.5 = bf16[32,2048]{1,0:T(8,128)(2,1)S(1)} collective-permute-done((bf16[32,2048]{1,0:T(8,128)(2,1)S(1)}, bf16[32,2048]{1,0:T(8,128)(2,1)S(1)}, u32[]{:S(2)}, u32[]{:S(2)}) %collective-permute-start.5) | collective-permute-done | bytes 131104 | tf_op jit(solution)/shard_map/ppermute | solution.py:126
  88.8 20.2 %shard_map.113 = (f32[128,2048]{1,0:T(8,128)}, f32[16,128,1]{2,1,0:T(8,128)}, f32[16,128,1]{2,1,0:T(8,128)}) custom-call(f32[1,4096]{1,0:T(1,128)} %and_select_fusion.bias_ref, s32[1,96]{1,0:T(1,128)} %compare_select_fusion.23.rank_ref, bf16[128,2048]{1,0:T(8,128)(2,1)} %bitcast.165, bf16[64,128,256]{2,1,0:T(8,128)(2,1)} %bitcast.159, ...), custom_call_target="tpu_custom_call" | custom-call | tf_op jit(solution)/shard_map/pallas_call | solution.py:66
  109.1 1.7 reduce.1
  110.8 1.6 reduce.2
  114.2 4.1 %constant_dynamic-slice_fusion.2 = (bf16[1,16,2,64,256]{4,3,2,1,0:T(8,128)(2,1)S(1)}, bf16[16,2,64,256]{3,2,1,0:T(8,128)(2,1)}, bf16[16,2,64,256]{3,2,1,0:T(8,128)(2,1)}, bf16[16,2,64,256]{3,2,1,0:T(8,128)(2,1)}) fusion(bf16[4,16,2,64,256]{4,3,2,1,0:T(8,128)(2,1)} %multiply_convert_fusion, s32[]{:T(128)S(6)} %select_n.381, s32[]{:T(128)S(6)} %select_n.384, ...), kind=kLoop, calls=%fused_computation.132 | loop fusion | bytes 8388624 | tf_op jit(solution)/shard_map/jit(dynamic_index_in_dim)/dynamic_slice | solution.py:267
  126.5 40.9 %collective-permute-done.12 = f32[32,32]{1,0:T(8,128)S(1)} collective-permute-done((f32[32,32]{1,0:T(8,128)S(1)}, f32[32,32]{1,0:T(8,128)S(1)}, u32[]{:S(2)}, u32[]{:S(2)}) %collective-permute-start.12) | collective-permute-done | bytes 4128 | tf_op jit(solution)/shard_map/ppermute | solution.py:174
  167.4 2.3 %collective-permute-done.13 = bf16[32,16,128]{2,1,0:T(8,128)(2,1)S(1)} collective-permute-done((bf16[32,16,128]{2,1,0:T(8,128)(2,1)S(1)}, bf16[32,16,128]{2,1,0:T(8,128)(2,1)S(1)}, u32[]{:S(2)}, u32[]{:S(2)}) %collective-permute-start.13) | collective-permute-done | bytes 131104 | tf_op jit(solution)/shard_map/ppermute | solution.py:174
  170.8 2.1 %pad_maximum_fusion = bf16[4,16,2,64,256]{4,3,2,1,0:T(8,128)(2,1)S(1)} fusion(bf16[1,16,2,64,256]{4,3,2,1,0:T(8,128)(2,1)} %bitcast.61, bf16[1,16,2,64,256]{4,3,2,1,0:T(8,128)(2,1)} %bitcast.59, bf16[1,16,2,64,256]{4,3,2,1,0:T(8,128)(2,1)} %bitcast.57, bf16[1,16,2,64,256]{4,3,2,1,0:T(8,128)(2,1)S(1)} %get-tuple-element.28), kind=kLoop, calls=%fused_computation.12 | loop fusion | flops 6291456 | bytes 8388608 | tf_op jit(solution)/shard_map/stack | solution.py:277
  172.9 1.8 %slice_bitcast_fusion.1 = (bf16[64,64,256]{2,1,0:T(8,128)(2,1)}, bf16[64,64,256]{2,1,0:T(8,128)(2,1)S(1)}) fusion(bf16[64,2,64,256]{3,2,1,0:T(8,128)(2,1)S(1)} %bitcast.162), kind=kLoop, calls=%fused_computation.30 | loop fusion | bytes 8388608 | tf_op jit(solution)/shard_map/squeeze | solution.py:295
  174.8 2.2 %gather_fusion.7 = bf16[32,64,256]{2,1,0:T(8,128)(2,1)S(1)} fusion(bf16[64,64,256]{2,1,0:T(8,128)(2,1)} %get-tuple-element.26, s32[1024]{0:T(1024)S(1)} %pad_clamp_fusion), kind=kCustom, calls=%fused_computation.clone | custom fusion | bytes 2097280 | tf_op jit(solution)/shard_map/jit(_take)/gather | solution.py:295
  177.0 1.6 gather_fusion.8
  (180 shorter events, 60.0 us)
Async XLA Ops:
  0.6 35.0 %copy-start = (bf16[48,2,64,256]{3,2,1,0:T(8,128)(2,1)S(1)}, bf16[48,2,64,256]{3,2,1,0:T(8,128)(2,1)}, u32[]{:S(2)}) copy-start(bf16[48,2,64,256]{3,2,1,0:T(8,128)(2,1)} %param.17) | copy-start | bytes 9437188
  5.8 7.2 %copy-start.18 = (s32[128]{0:T(128)S(1)}, s32[128]{0:T(128)}, u32[]{:S(2)}) copy-start(s32[128]{0:T(128)} %param.20) | copy-start | bytes 1540
  5.8 8.4 %copy-start.20 = (s32[128,1]{0,1:T(1,128)S(1)}, s32[128,1]{0,1:T(1,128)}, u32[]{:S(2)}) copy-start(s32[128,1]{0,1:T(1,128)} %param.19) | copy-start | bytes 1540
  9.3 40.5 %collective-permute-start.2 = (bf16[96,2048]{1,0:T(8,128)(2,1)}, bf16[96,2048]{1,0:T(8,128)(2,1)}, u32[]{:S(2)}, u32[]{:S(2)}) collective-permute-start(bf16[96,2048]{1,0:T(8,128)(2,1)} %get-tuple-element.35), channel_id=1, source_target_pairs={{0,12},{4,0},{8,4},{12,8},{1,13},{5,1},{9,5},{13,9},{2,14},{6,2},{... | collective-permute-start | bytes 1179656 | tf_op jit(solution)/shard_map/ppermute | solution.py:241
  11.7 38.1 %collective-permute-start.1 = (bf16[96,2048]{1,0:T(8,128)(2,1)}, bf16[96,2048]{1,0:T(8,128)(2,1)}, u32[]{:S(2)}, u32[]{:S(2)}) collective-permute-start(bf16[96,2048]{1,0:T(8,128)(2,1)} %get-tuple-element.34), channel_id=1, source_target_pairs={{0,8},{4,12},{8,0},{12,4},{1,9},{5,13},{9,1},{13,5},{2,10},{6,14},... | collective-permute-start | bytes 1179656 | tf_op jit(solution)/shard_map/ppermute | solution.py:241
  12.3 37.6 %collective-permute-start = (bf16[96,2048]{1,0:T(8,128)(2,1)}, bf16[96,2048]{1,0:T(8,128)(2,1)}, u32[]{:S(2)}, u32[]{:S(2)}) collective-permute-start(bf16[96,2048]{1,0:T(8,128)(2,1)} %get-tuple-element.33), channel_id=1, source_target_pairs={{0,4},{4,8},{8,12},{12,0},{1,5},{5,9},{9,13},{13,1},{2,6},{6,10},{... | collective-permute-start | bytes 1179656 | tf_op jit(solution)/shard_map/ppermute | solution.py:241
  14.9 8.5 %copy-start.10 = (s32[4,32]{1,0:T(4,128)}, s32[4,32]{1,0:T(4,128)S(1)}, u32[]{:S(2)}) copy-start(s32[4,32]{1,0:T(4,128)S(1)} %reshape_squeeze.3) | copy-start | bytes 1540
  35.6 6.7 %copy-start.9 = (pred[1,4096]{1,0:T(4,128)(4,1)S(1)}, pred[1,4096]{1,0:T(4,128)(4,1)}, u32[]{:S(2)}) copy-start(pred[1,4096]{1,0:T(4,128)(4,1)} %ge.67) | copy-start | bytes 12292
  54.9 7.6 %collective-permute-start.7 = (f32[2,96,2,256]{3,1,2,0:T(8,128)S(1)}, f32[2,96,2,256]{3,1,2,0:T(8,128)S(1)}, u32[]{:S(2)}, u32[]{:S(2)}) collective-permute-start(f32[2,96,2,256]{3,1,2,0:T(8,128)S(1)} %dynamic-slice_bitcast_fusion.6), channel_id=1, source_target_pairs={{0,4},{4,0},{8,12},{12,8},{1,5},{5,1},{9,13},{13,9},{2,6},{6,2},{1... | collective-permute-start | bytes 1179656 | tf_op jit(solution)/shard_map/ppermute | solution.py:116
  61.1 2.5 %collective-permute-start.3 = (f32[2,32,2048]{2,1,0:T(8,128)S(1)}, f32[2,32,2048]{2,1,0:T(8,128)}, u32[]{:S(2)}, u32[]{:S(2)}) collective-permute-start(f32[2,32,2048]{2,1,0:T(8,128)S(1)} %dynamic-slice_bitcast_fusion.5), channel_id=1, source_target_pairs={{0,4},{4,0},{8,12},{12,8},{1,5},{5,1},{9,13},{13,9},{2,6},{6,2},{1... | collective-permute-start | bytes 1572872 | tf_op jit(solution)/shard_map/ppermute | solution.py:116
  62.6 13.4 %copy-start.12 = (pred[2]{0:T(512)(128)(4,1)S(1)}, pred[2]{0:T(512)(128)(4,1)}, u32[]{:S(2)}) copy-start(pred[2]{0:T(512)(128)(4,1)} %compare_and_fusion.3) | copy-start | bytes 10
  62.6 6.9 %collective-permute-start.8 = (f32[96,2,256]{2,0,1:T(8,128)S(1)}, f32[96,2,256]{2,0,1:T(8,128)S(1)}, u32[]{:S(2)}, u32[]{:S(2)}) collective-permute-start(f32[96,2,256]{2,0,1:T(8,128)S(1)} %dynamic-slice_bitcast_fusion.10), channel_id=1, source_target_pairs={{0,8},{4,12},{8,0},{12,4},{1,9},{5,13},{9,1},{13,5},{2,10},{6,14},... | collective-permute-start | bytes 589832 | tf_op jit(solution)/shard_map/ppermute | solution.py:123
  69.5 5.7 %collective-permute-start.9 = (bf16[96,2,256]{2,0,1:T(8,128)(2,1)S(1)}, bf16[96,2,256]{2,0,1:T(8,128)(2,1)S(1)}, u32[]{:S(2)}, u32[]{:S(2)}) collective-permute-start(bf16[96,2,256]{2,0,1:T(8,128)(2,1)S(1)} %fusion.34), channel_id=1, source_target_pairs={{0,8},{4,12},{8,0},{12,4},{1,9},{5,13},{9,1},{13,5},{2,10},{6,14},... | collective-permute-start | bytes 294920 | tf_op jit(solution)/shard_map/ppermute | solution.py:126
  70.2 8.9 %collective-permute-start.4 = (f32[32,2048]{1,0:T(8,128)S(1)}, f32[32,2048]{1,0:T(8,128)S(1)}, u32[]{:S(2)}, u32[]{:S(2)}) collective-permute-start(f32[32,2048]{1,0:T(8,128)S(1)} %dynamic-slice_bitcast_fusion.9), channel_id=1, source_target_pairs={{0,8},{4,12},{8,0},{12,4},{1,9},{5,13},{9,1},{13,5},{2,10},{6,14},... | collective-permute-start | bytes 786440 | tf_op jit(solution)/shard_map/ppermute | solution.py:123
  76.1 3.9 %collective-permute-start.10 = (bf16[2,96,2,256]{3,1,2,0:T(8,128)(2,1)S(1)}, bf16[2,96,2,256]{3,1,2,0:T(8,128)(2,1)S(1)}, u32[]{:S(2)}, u32[]{:S(2)}) collective-permute-start(bf16[2,96,2,256]{3,1,2,0:T(8,128)(2,1)S(1)} %broadcast_select_fusion.3), channel_id=1, source_target_pairs={{0,4},{4,0},{8,12},{12,8},{1,5},{5,1},{9,13},{13,9},{2,6},{6,2},{1... | collective-permute-start | bytes 589832 | tf_op jit(solution)/shard_map/ppermute | solution.py:130
  79.1 5.0 %collective-permute-start.5 = (bf16[32,2048]{1,0:T(8,128)(2,1)S(1)}, bf16[32,2048]{1,0:T(8,128)(2,1)S(1)}, u32[]{:S(2)}, u32[]{:S(2)}) collective-permute-start(bf16[32,2048]{1,0:T(8,128)(2,1)S(1)} %fusion.32), channel_id=1, source_target_pairs={{0,8},{4,12},{8,0},{12,4},{1,9},{5,13},{9,1},{13,5},{2,10},{6,14},... | collective-permute-start | bytes 393224 | tf_op jit(solution)/shard_map/ppermute | solution.py:126
  80.7 33.5 %copy-start.4 = (bf16[4,96,2,256]{3,1,2,0:T(8,128)(2,1)}, bf16[4,96,2,256]{3,1,2,0:T(8,128)(2,1)S(1)}, u32[]{:S(2)}) copy-start(bf16[4,96,2,256]{3,1,2,0:T(8,128)(2,1)S(1)} %bitcast_select_fusion.1) | copy-start | bytes 1179652
  85.0 1.6 collective-permute-start.6
  113.7 6.7 %collective-permute-start.11 = (f32[2,32,2080]{2,1,0:T(8,128)}, f32[2,32,2080]{2,1,0:T(8,128)S(1)}, u32[]{:S(2)}, u32[]{:S(2)}) collective-permute-start(f32[2,32,2080]{2,1,0:T(8,128)} %get-tuple-element.37), channel_id=1, source_target_pairs={{0,4},{4,0},{8,12},{12,8},{1,5},{5,1},{9,13},{13,9},{2,6},{6,2},{1... | collective-permute-start | bytes 1597448 | tf_op jit(solution)/shard_map/ppermute | solution.py:163
  118.3 52.5 %collective-permute-start.16 = (bf16[16,2,64,256]{3,2,1,0:T(8,128)(2,1)}, bf16[16,2,64,256]{3,2,1,0:T(8,128)(2,1)}, u32[]{:S(2)}, u32[]{:S(2)}) collective-permute-start(bf16[16,2,64,256]{3,2,1,0:T(8,128)(2,1)} %get-tuple-element.29), channel_id=1, source_target_pairs={{0,12},{4,0},{8,4},{12,8},{1,13},{5,1},{9,5},{13,9},{2,14},{6,2},{... | collective-permute-start | bytes 3145736 | tf_op jit(solution)/shard_map/ppermute | solution.py:271
  119.1 51.7 %collective-permute-start.15 = (bf16[16,2,64,256]{3,2,1,0:T(8,128)(2,1)}, bf16[16,2,64,256]{3,2,1,0:T(8,128)(2,1)}, u32[]{:S(2)}, u32[]{:S(2)}) collective-permute-start(bf16[16,2,64,256]{3,2,1,0:T(8,128)(2,1)} %get-tuple-element.30), channel_id=1, source_target_pairs={{0,8},{4,12},{8,0},{12,4},{1,9},{5,13},{9,1},{13,5},{2,10},{6,14},... | collective-permute-start | bytes 3145736 | tf_op jit(solution)/shard_map/ppermute | solution.py:271
  120.3 50.5 %collective-permute-start.14 = (bf16[16,2,64,256]{3,2,1,0:T(8,128)(2,1)}, bf16[16,2,64,256]{3,2,1,0:T(8,128)(2,1)}, u32[]{:S(2)}, u32[]{:S(2)}) collective-permute-start(bf16[16,2,64,256]{3,2,1,0:T(8,128)(2,1)} %get-tuple-element.31), channel_id=1, source_target_pairs={{0,4},{4,8},{8,12},{12,0},{1,5},{5,9},{9,13},{13,1},{2,6},{6,10},{... | collective-permute-start | bytes 3145736 | tf_op jit(solution)/shard_map/ppermute | solution.py:271
  124.1 43.2 %collective-permute-start.12 = (f32[32,32]{1,0:T(8,128)S(1)}, f32[32,32]{1,0:T(8,128)S(1)}, u32[]{:S(2)}, u32[]{:S(2)}) collective-permute-start(f32[32,32]{1,0:T(8,128)S(1)} %slice.119), channel_id=1, source_target_pairs={{0,8},{4,12},{8,0},{12,4},{1,9},{5,13},{9,1},{13,5},{2,10},{6,14},... | collective-permute-start | bytes 12296 | tf_op jit(solution)/shard_map/ppermute | solution.py:174
  125.2 44.5 %collective-permute-start.13 = (bf16[32,16,128]{2,1,0:T(8,128)(2,1)S(1)}, bf16[32,16,128]{2,1,0:T(8,128)(2,1)S(1)}, u32[]{:S(2)}, u32[]{:S(2)}) collective-permute-start(bf16[32,16,128]{2,1,0:T(8,128)(2,1)S(1)} %fusion.27), channel_id=1, source_target_pairs={{0,8},{4,12},{8,0},{12,4},{1,9},{5,13},{9,1},{13,5},{2,10},{6,14},... | collective-permute-start | bytes 393224 | tf_op jit(solution)/shard_map/ppermute | solution.py:174
  (17 other events, 55.2 us)
